TPU v7x, 512 devices: a whole 4x4x16 slice. The times are simulated.
512 devices in a mesh: seq: 64 (over y, z_hi, x, core), head: 8 (over z_lo).
Axes of the slice: x: 4, y: 4, z: 16 (z_hi: 2, z_lo: 8; z = z_hi * 8 + z_lo), core: 2. Of those that a mesh axis runs over, the one named last changes fastest.
Arguments:
- cross_q: bfloat16 [512, 2048], P('seq', 'head'), may hold values from -20 to 20
- cross_out: bfloat16 [512, 2048], P('seq', 'head'), may hold values from -0.59765625 to 0.59765625
- cross_grad: bfloat16 [512, 2048], P('seq', 'head'), may hold values from -1800 to 1800
- prefix_k: bfloat16 [8192, 2048], P('seq', 'head'), may hold values from -6 to 6
- prefix_v: bfloat16 [8192, 2048], P('seq', 'head'), may hold values from -6 to 6
- pad_counts: int32 [64], P('seq'), may hold values from 0 to 64, as said below
- self_q: bfloat16 [512, 2048], P(('seq', 'head')), may hold values from -20 to 20
- self_k: bfloat16 [512, 2048], P(('seq', 'head')), may hold values from -6 to 6
- self_v: bfloat16 [512, 2048], P(('seq', 'head')), may hold values from -6 to 6
- self_grad: bfloat16 [512, 2048], P(('seq', 'head')), may hold values from -12 to 12
Outputs:
- cross_dq: bfloat16 [512, 2048], P('seq', 'head')
- prefix_dk: bfloat16 [8192, 2048], P('seq', 'head')
- prefix_dv: bfloat16 [8192, 2048], P('seq', 'head')
- self_dq: bfloat16 [512, 2048], P('seq', 'head')
- self_dk: bfloat16 [512, 2048], P('seq', 'head')
- self_dv: bfloat16 [512, 2048], P('seq', 'head')
Inputs may be any that keep to these rules, and one draw needn't show every extreme that they name: `pad_counts`: every shard keeps at least 64 valid tokens; some shard has exactly 64 padded tokens.
All inputs are finite; a program needn't handle non-finite values.
Results may differ from a plain program's by a relative error of at most 0.0086.
Values may be sent and summed in bfloat16 or wider, within the bound.
No kernel may reach another device: no remote copies, remote signals or barrier semaphores. Data moves between devices by JAX's collectives and lax.ppermute only.
A program may use at most 64 MiB of HBM per device.

v0:
```python
import jax
import jax.numpy as jnp
from jax import lax
from jax.sharding import PartitionSpec as P

HEAD_DIM = 128


def in_one_piece(arrays, axis, dim, along):
    ends, at = ([], 0)
    for a in arrays[:-1]:
        at += a.shape[along]
        ends.append(at)
    both = jnp.concatenate(arrays, axis=along)
    return tuple(jnp.split(lax.all_gather(both, axis, axis=dim, tiled=True), ends, axis=along))


def from_everyone(x, axis):
    copies = jnp.broadcast_to(x, (lax.axis_size(axis), *x.shape))
    return lax.all_to_all(copies, axis, split_axis=0, concat_axis=0, tiled=True)


def all_in_one(x, axis):
    leaves = jax.tree.leaves(x)
    order = sorted(range(len(leaves)), key=lambda k: -leaves[k].size)
    width = (1, *leaves[order[0]].shape)[-1]
    lines = [
        jnp.pad(leaves[k].reshape(-1), (0, -leaves[k].size % width)).reshape(-1, width)
        for k in order
    ]
    both, at, found = (from_everyone(jnp.concatenate(lines), axis), 0, {})
    for k, line in zip(order, lines):
        section = both[:, at : at + len(line)].reshape(len(both), -1)
        found[k] = section[:, : leaves[k].size].reshape(-1, *leaves[k].shape)
        at += len(line)
    numbers = iter(range(len(leaves)))
    return jax.tree.map(lambda _: found[next(numbers)], x)


def joined_by_halves(pieces, combine):
    while len(jax.tree.leaves(pieces)[0]) > 1:
        pieces = jax.vmap(combine)(
            *(jax.tree.map(lambda part: part[side::2], pieces) for side in (0, 1))
        )
    return jax.tree.map(lambda part: part[0], pieces)


def merged(x, axis, combine):
    pieces = all_in_one(x, axis)
    return joined_by_halves(pieces, combine)


def split_up(x, dim, size):
    before, after = (x.shape[:dim], x.shape[dim + 1 :])
    return jnp.moveaxis(x.reshape(*before, size, -1, *after), dim, 0)


def sum_at_owner(x, axis, dim):
    size = lax.axis_size(axis)
    parts = lax.all_to_all(split_up(x, dim, size), axis, 0, 0, tiled=True)
    return jnp.sum(parts, axis=0)


def joined_along(parts, dim):
    lengths = list(parts.shape[1:])
    lengths[dim] *= parts.shape[0]
    return jnp.moveaxis(parts, 0, dim).reshape(lengths)


def gathered_copies(x, axis, dim):
    return joined_along(from_everyone(x, axis), dim)


def merge_stats(left_stats, right_stats):
    row_max = jnp.maximum(left_stats[0], right_stats[0])
    row_sum = left_stats[1] * jnp.exp(left_stats[0] - row_max) + right_stats[1] * jnp.exp(
        right_stats[0] - row_max
    )
    return (row_max, row_sum)


def head_scores(queries, key_rows, score_scale):
    return (
        jnp.einsum("qhd,khd->hqk", queries, key_rows, preferred_element_type=jnp.float32)
        * score_scale
    )


def scores_grad(weights, grad_rows, value_rows, row_dot, score_scale):
    grad_probs = jnp.einsum(
        "qhd,khd->hqk", grad_rows, value_rows, preferred_element_type=jnp.float32
    )
    return (weights * (grad_probs - jnp.transpose(row_dot)[:, :, None]) * score_scale).astype(
        jnp.bfloat16
    )


def contract_rows(left_rows, right_rows):
    return jnp.einsum("hqk,qhd->khd", left_rows, right_rows, preferred_element_type=jnp.float32)


def contract_cols(left_rows, right_rows):
    return jnp.einsum("hqk,khd->qhd", left_rows, right_rows, preferred_element_type=jnp.float32)


def shards(
    cross_q,
    cross_out,
    cross_grad,
    prefix_k,
    prefix_v,
    pad_counts,
    self_q,
    self_k,
    self_v,
    self_grad,
):
    score_scale = HEAD_DIM ** (-0.5)
    own_rows, feature_width = cross_q.shape
    local_heads = feature_width // HEAD_DIM
    tokens = prefix_k.shape[0]
    grad_own = cross_grad.reshape(own_rows, local_heads, HEAD_DIM).astype(jnp.float32)
    out_own = cross_out.reshape(own_rows, local_heads, HEAD_DIM).astype(jnp.float32)
    row_dot = jnp.sum(grad_own * out_own, axis=2).astype(jnp.bfloat16)
    query_all, grad_all, dots_all = in_one_piece((cross_q, cross_grad, row_dot), "seq", 0, 1)
    latents = query_all.shape[0]
    query_heads = query_all.reshape(latents, local_heads, HEAD_DIM)
    grad_heads = grad_all.reshape(latents, local_heads, HEAD_DIM)
    key_heads = prefix_k.reshape(tokens, local_heads, HEAD_DIM)
    value_heads = prefix_v.reshape(tokens, local_heads, HEAD_DIM)
    valid_keys = jnp.arange(tokens) < tokens - pad_counts[0]
    scores = head_scores(query_heads, key_heads, score_scale)
    scores = jnp.where(valid_keys[None, None, :], scores, -jnp.inf)
    row_max = jnp.max(scores, axis=2)
    row_sum = jnp.sum(jnp.exp(scores - row_max[:, :, None]), axis=2)
    row_maxes, row_sums = merged(
        (jnp.transpose(row_max), jnp.transpose(row_sum)), "seq", merge_stats
    )
    log_total = row_maxes + jnp.log(row_sums)
    row_dots = dots_all.astype(jnp.float32)
    weights = jnp.exp(scores - jnp.transpose(log_total)[:, :, None])
    prefix_dv = (
        contract_rows(weights.astype(jnp.bfloat16), grad_heads)
        .reshape(tokens, feature_width)
        .astype(jnp.bfloat16)
    )
    grad_scores = scores_grad(weights, grad_heads, value_heads, row_dots, score_scale)
    prefix_dk = (
        contract_rows(grad_scores, query_heads).reshape(tokens, feature_width).astype(jnp.bfloat16)
    )
    partial_value = contract_cols(grad_scores, key_heads).reshape(latents, feature_width)
    cross_dq = sum_at_owner(partial_value, "seq", 0).astype(jnp.bfloat16)
    stacked = jnp.stack([self_q, self_k, self_v, self_grad])
    regrouped = lax.all_to_all(stacked, "head", split_axis=2, concat_axis=1, tiled=True)
    block_rows = regrouped.shape[1]
    row_start = lax.axis_index("seq") * block_rows
    everything = gathered_copies(regrouped, "seq", 1)
    all_rows = everything.shape[1]
    query_every = everything[0].reshape(all_rows, local_heads, HEAD_DIM)
    key_every = everything[1].reshape(all_rows, local_heads, HEAD_DIM)
    value_every = everything[2].reshape(all_rows, local_heads, HEAD_DIM)
    grad_every = everything[3].reshape(all_rows, local_heads, HEAD_DIM)
    row_ids = jnp.arange(all_rows)
    causal_full = row_ids[:, None] >= row_ids[None, :]
    full_scores = head_scores(query_every, key_every, score_scale)
    full_scores = jnp.where(causal_full[None, :, :], full_scores, -jnp.inf)
    full_lse = jax.nn.logsumexp(full_scores, axis=2)
    full_weights = jnp.exp(full_scores - full_lse[:, :, None])
    full_half = full_weights.astype(jnp.bfloat16)
    full_out = contract_cols(full_half, value_every)
    full_dot = jnp.sum(grad_every.astype(jnp.float32) * full_out, axis=2)
    full_gs = scores_grad(full_weights, grad_every, value_every, full_dot, score_scale)
    query_part = lax.dynamic_slice_in_dim(full_gs, row_start, block_rows, 1)
    self_dq = (
        contract_cols(query_part, key_every).reshape(block_rows, feature_width).astype(jnp.bfloat16)
    )
    key_part = lax.dynamic_slice_in_dim(full_gs, row_start, block_rows, 2)
    half_part = lax.dynamic_slice_in_dim(full_half, row_start, block_rows, 2)
    self_dk = (
        contract_rows(key_part, query_every).reshape(block_rows, feature_width).astype(jnp.bfloat16)
    )
    self_dv = (
        contract_rows(half_part, grad_every).reshape(block_rows, feature_width).astype(jnp.bfloat16)
    )
    return (cross_dq, prefix_dk, prefix_dv, self_dq, self_dk, self_dv)


def solution(mesh):
    in_specs = (
        P("seq", "head"),
        P("seq", "head"),
        P("seq", "head"),
        P("seq", "head"),
        P("seq", "head"),
        P("seq"),
        P(("seq", "head"), None),
        P(("seq", "head"), None),
        P(("seq", "head"), None),
        P(("seq", "head"), None),
    )
    out_specs = (
        P("seq", "head"),
        P("seq", "head"),
        P("seq", "head"),
        P("seq", "head"),
        P("seq", "head"),
        P("seq", "head"),
    )
    return jax.shard_map(shards, mesh=mesh, in_specs=in_specs, out_specs=out_specs, check_vma=False)
```

profile of v0, /device:TPU:64, one launch (start us, length us, event | category | flops | bytes accessed | tf_op | source)
XLA Modules:
  0.0 327.9 jit_solution(5765229599135484474)
XLA Ops:
  1.3 0.8 bitcast_reduce_fusion
  2.2 0.7 pad_maximum_fusion.1
  2.9 164.3 %all_gather.3 = bf16[512,514]{1,0:T(8,128)(2,1)S(1)} all-gather(bf16[8,514]{1,0:T(8,128)(2,1)S(1)} %pad_maximum_fusion.1), channel_id=1, replica_groups=mesh['seq'=64,'head'=8] {'seq'}, dimensions={0}, use_global_device_ids=true | all-gather | bytes 534560 | tf_op jit(solution)/shard_map/all_gather | solution.py:15
  167.8 0.9 broadcast_in_dim.45
  168.7 4.6 %all-to-all-start = ((f32[64,1024,2]{1,2,0:T(2,128)}), f32[64,1024,2]{1,2,0:T(2,128)S(1)}, u32[]{:S(2)}, u32[]{:S(2)}) async-start(f32[64,1024,2]{1,2,0:T(2,128)} %broadcast_in_dim.45), calls=%async_computation | async-start | bytes 1048576 | tf_op jit(solution)/shard_map/all_to_all | solution.py:20
  173.8 0.9 copy.130
  175.2 11.6 %reduce = bf16[2048,4]{1,0:T(8,128)(2,1)S(1)} reduce(bf16[2048,1,4]{2,1,0:T(2,128)(2,1)S(1)} %bitcast.102, bf16[]{:T(256)} %broadcast.32), dimensions={1}, to_apply=%bitcast.76.reduce_sub_computation | reduce | bytes 32770
  186.8 1.4 reshape.96
  188.2 15.8 %all-to-all-done = f32[64,1024,2]{1,2,0:T(2,128)S(1)} async-done(((f32[64,1024,2]{1,2,0:T(2,128)}), f32[64,1024,2]{1,2,0:T(2,128)S(1)}, u32[]{:S(2)}, u32[]{:S(2)}) %all-to-all-start) | async-done | bytes 524320 | tf_op jit(solution)/shard_map/all_to_all | solution.py:20
  204.0 13.3 %all-to-all-start.2 = ((bf16[8,2,512]{2,1,0:T(2,128)(2,1)}), bf16[8,2,512]{2,1,0:T(2,128)(2,1)S(1)}, u32[]{:S(2)}, u32[]{:S(2)}) async-start(bf16[8,2,512]{2,1,0:T(2,128)(2,1)} %reshape.96), calls=%async_computation.2 | async-start | bytes 32768 | tf_op jit(solution)/shard_map/all_to_all | solution.py:154
  218.8 1.2 reshape_reshape.3
  220.0 5.4 %all-to-all-done.2 = bf16[8,2,512]{2,1,0:T(2,128)(2,1)S(1)} async-done(((bf16[8,2,512]{2,1,0:T(2,128)(2,1)}), bf16[8,2,512]{2,1,0:T(2,128)(2,1)S(1)}, u32[]{:S(2)}, u32[]{:S(2)}) %all-to-all-start.2) | async-done | bytes 16416 | tf_op jit(solution)/shard_map/all_to_all | solution.py:154
  225.4 4.8 %all-to-all-start.1 = ((f32[64,8,256]{2,1,0:T(8,128)}), f32[64,8,256]{2,1,0:T(8,128)S(1)}, u32[]{:S(2)}, u32[]{:S(2)}) async-start(f32[64,8,256]{2,1,0:T(8,128)} %reshape_reshape.3), calls=%async_computation.1 | async-start | bytes 1048576 | tf_op jit(solution)/shard_map/all_to_all | solution.py:60
  230.3 1.4 reshape.97
  232.3 31.1 %all-to-all-done.1 = f32[64,8,256]{2,1,0:T(8,128)S(1)} async-done(((f32[64,8,256]{2,1,0:T(8,128)}), f32[64,8,256]{2,1,0:T(8,128)S(1)}, u32[]{:S(2)}, u32[]{:S(2)}) %all-to-all-start.1) | async-done | bytes 524320 | tf_op jit(solution)/shard_map/all_to_all | solution.py:60
  263.4 1.1 broadcast_in_dim.46
  264.5 7.9 %all-to-all-start.3 = ((bf16[64,4,8,256]{3,2,1,0:T(8,128)(2,1)}), bf16[64,4,8,256]{3,2,1,0:T(8,128)(2,1)S(1)}, u32[]{:S(2)}, u32[]{:S(2)}) async-start(bf16[64,4,8,256]{3,2,1,0:T(8,128)(2,1)} %broadcast_in_dim.46), calls=%async_computation.3 | async-start | bytes 2097152 | tf_op jit(solution)/shard_map/all_to_all | solution.py:20
  272.7 0.7 copy.144
  273.7 0.7 copy.145
  274.5 0.7 reduce_sum.47
  275.1 47.4 %all-to-all-done.3 = bf16[64,4,8,256]{3,2,1,0:T(8,128)(2,1)S(1)} async-done(((bf16[64,4,8,256]{3,2,1,0:T(8,128)(2,1)}), bf16[64,4,8,256]{3,2,1,0:T(8,128)(2,1)S(1)}, u32[]{:S(2)}, u32[]{:S(2)}) %all-to-all-start.3) | async-done | bytes 1048608 | tf_op jit(solution)/shard_map/all_to_all | solution.py:20
  324.4 0.8 fusion.8
  326.2 0.8 fusion.7
  326.9 0.9 fusion.9
  (53 shorter events, 6.8 us)
Async XLA Ops:
  0.6 166.8 %copy-start = (bf16[128,256]{1,0:T(8,128)(2,1)S(1)}, bf16[128,256]{1,0:T(8,128)(2,1)}, u32[]{:S(2)}) copy-start(bf16[128,256]{1,0:T(8,128)(2,1)} %param.13) | copy-start | bytes 196612
  167.4 6.3 %copy-start.2 = (bf16[1,2048]{1,0:T(2,128)(2,1)S(1)}, bf16[1,2048]{1,0:T(2,128)(2,1)}, u32[]{:S(2)}) copy-start(bf16[1,2048]{1,0:T(2,128)(2,1)} %param.19) | copy-start | bytes 12292
  167.4 6.3 %copy-start.3 = (bf16[1,2048]{1,0:T(2,128)(2,1)S(1)}, bf16[1,2048]{1,0:T(2,128)(2,1)}, u32[]{:S(2)}) copy-start(bf16[1,2048]{1,0:T(2,128)(2,1)} %param.18) | copy-start | bytes 12292
  167.4 6.3 %copy-start.4 = (bf16[1,2048]{1,0:T(2,128)(2,1)S(1)}, bf16[1,2048]{1,0:T(2,128)(2,1)}, u32[]{:S(2)}) copy-start(bf16[1,2048]{1,0:T(2,128)(2,1)} %param.17) | copy-start | bytes 12292
  167.4 6.3 %copy-start.5 = (bf16[1,2048]{1,0:T(2,128)(2,1)S(1)}, bf16[1,2048]{1,0:T(2,128)(2,1)}, u32[]{:S(2)}) copy-start(bf16[1,2048]{1,0:T(2,128)(2,1)} %param.16) | copy-start | bytes 12292
  168.7 35.3 %all-to-all-start = ((f32[64,1024,2]{1,2,0:T(2,128)}), f32[64,1024,2]{1,2,0:T(2,128)S(1)}, u32[]{:S(2)}, u32[]{:S(2)}) async-start(f32[64,1024,2]{1,2,0:T(2,128)} %broadcast_in_dim.45), calls=%async_computation | async-start | bytes 1048576 | tf_op jit(solution)/shard_map/all_to_all | solution.py:20
  175.2 42.6 %copy-start.1 = (bf16[128,256]{1,0:T(8,128)(2,1)S(1)}, bf16[128,256]{1,0:T(8,128)(2,1)}, u32[]{:S(2)}) copy-start(bf16[128,256]{1,0:T(8,128)(2,1)} %param.14) | copy-start | bytes 196612
  204.0 21.4 %all-to-all-start.2 = ((bf16[8,2,512]{2,1,0:T(2,128)(2,1)}), bf16[8,2,512]{2,1,0:T(2,128)(2,1)S(1)}, u32[]{:S(2)}, u32[]{:S(2)}) async-start(bf16[8,2,512]{2,1,0:T(2,128)(2,1)} %reshape.96), calls=%async_computation.2 | async-start | bytes 32768 | tf_op jit(solution)/shard_map/all_to_all | solution.py:154
  225.4 38.0 %all-to-all-start.1 = ((f32[64,8,256]{2,1,0:T(8,128)}), f32[64,8,256]{2,1,0:T(8,128)S(1)}, u32[]{:S(2)}, u32[]{:S(2)}) async-start(f32[64,8,256]{2,1,0:T(8,128)} %reshape_reshape.3), calls=%async_computation.1 | async-start | bytes 1048576 | tf_op jit(solution)/shard_map/all_to_all | solution.py:60
  264.5 58.0 %all-to-all-start.3 = ((bf16[64,4,8,256]{3,2,1,0:T(8,128)(2,1)}), bf16[64,4,8,256]{3,2,1,0:T(8,128)(2,1)S(1)}, u32[]{:S(2)}, u32[]{:S(2)}) async-start(bf16[64,4,8,256]{3,2,1,0:T(8,128)(2,1)} %broadcast_in_dim.46), calls=%async_computation.3 | async-start | bytes 2097152 | tf_op jit(solution)/shard_map/all_to_all | solution.py:20
where the time goes:
time: 328 us
  blocking collectives  164 us (50%)
  waiting for transfers between devices  99.7 us (30%)
  starting transfers between devices  30.7 us (9%)
  other arithmetic  15.1 us (5%)
  local copies, waits for them, and re-layouts  11.2 us (3%)
  matrix products  5.17 us (2%)
    all_gather x1, blocking collectives, in_one_piece(): lax.all_gather(both, axis, axis=dim, tiled=True)  164 us
    all_to_all x2, waiting for transfers between devices, from_everyone(): return lax.all_to_all(copies, axis, split_axis=0, concat_axis=0, tiled=True)  63.2 us
    all_to_all x1, waiting for transfers between devices, sum_at_owner(): parts = lax.all_to_all(split_up(x, dim, size), axis, 0, 0, tiled=True)  31.1 us
    all_to_all x1, starting transfers between devices, shards(): lax.all_to_all(stacked, 'head', split_axis=2, concat_axis=1, tiled=True)  13.3 us
    all_to_all x2, starting transfers between devices, from_everyone(): return lax.all_to_all(copies, axis, split_axis=0, concat_axis=0, tiled=True)  12.5 us
    unnamed x1, other arithmetic  11.6 us
  transfers between devices with their start and end apart: 4, of which 4 were waited for; matrix products, arithmetic and copies ran while one was open for 7% of the time, Pallas kernels for 0%

commit v1 on v0

--- a/solution.py
+++ b/solution.py
@@ -101,6 +101,24 @@
 
 def contract_cols(left_rows, right_rows):
     return jnp.einsum("hqk,khd->qhd", left_rows, right_rows, preferred_element_type=jnp.float32)
+
+
+SEQ_PARTS = ("c", "x", "zh", "y")
+
+
+def gather_seq(x, dim):
+    for axis in SEQ_PARTS:
+        x = lax.all_gather(x, axis, axis=dim, tiled=True)
+    return x
+
+
+def merged_seq(row_max, row_sum):
+    for axis in SEQ_PARTS:
+        both = lax.all_gather(jnp.stack([row_max, row_sum]), axis)
+        top = jnp.max(both[:, 0], axis=0)
+        row_sum = jnp.sum(both[:, 1] * jnp.exp(both[:, 0] - top), axis=0)
+        row_max = top
+    return row_max, row_sum
 
 
 def shards(
@@ -122,7 +140,17 @@
     grad_own = cross_grad.reshape(own_rows, local_heads, HEAD_DIM).astype(jnp.float32)
     out_own = cross_out.reshape(own_rows, local_heads, HEAD_DIM).astype(jnp.float32)
     row_dot = jnp.sum(grad_own * out_own, axis=2).astype(jnp.bfloat16)
-    query_all, grad_all, dots_all = in_one_piece((cross_q, cross_grad, row_dot), "seq", 0, 1)
+    stacked = jnp.stack([self_q, self_k, self_v, self_grad])
+    regrouped = lax.all_to_all(stacked, "zl", split_axis=2, concat_axis=1, tiled=True)
+    block_rows = regrouped.shape[1]
+    self_cols = jnp.transpose(regrouped, (1, 0, 2)).reshape(block_rows, -1)
+    pieces = (cross_q, cross_grad, row_dot, self_cols)
+    ends, at = [], 0
+    for piece in pieces[:-1]:
+        at += piece.shape[1]
+        ends.append(at)
+    gathered = gather_seq(jnp.concatenate(pieces, axis=1), 0)
+    query_all, grad_all, dots_all, self_all = jnp.split(gathered, ends, axis=1)
     latents = query_all.shape[0]
     query_heads = query_all.reshape(latents, local_heads, HEAD_DIM)
     grad_heads = grad_all.reshape(latents, local_heads, HEAD_DIM)
@@ -133,12 +161,10 @@
     scores = jnp.where(valid_keys[None, None, :], scores, -jnp.inf)
     row_max = jnp.max(scores, axis=2)
     row_sum = jnp.sum(jnp.exp(scores - row_max[:, :, None]), axis=2)
-    row_maxes, row_sums = merged(
-        (jnp.transpose(row_max), jnp.transpose(row_sum)), "seq", merge_stats
-    )
+    row_maxes, row_sums = merged_seq(row_max, row_sum)
     log_total = row_maxes + jnp.log(row_sums)
     row_dots = dots_all.astype(jnp.float32)
-    weights = jnp.exp(scores - jnp.transpose(log_total)[:, :, None])
+    weights = jnp.exp(scores - log_total[:, :, None])
     prefix_dv = (
         contract_rows(weights.astype(jnp.bfloat16), grad_heads)
         .reshape(tokens, feature_width)
@@ -149,12 +175,9 @@
         contract_rows(grad_scores, query_heads).reshape(tokens, feature_width).astype(jnp.bfloat16)
     )
     partial_value = contract_cols(grad_scores, key_heads).reshape(latents, feature_width)
-    cross_dq = sum_at_owner(partial_value, "seq", 0).astype(jnp.bfloat16)
-    stacked = jnp.stack([self_q, self_k, self_v, self_grad])
-    regrouped = lax.all_to_all(stacked, "head", split_axis=2, concat_axis=1, tiled=True)
-    block_rows = regrouped.shape[1]
-    row_start = lax.axis_index("seq") * block_rows
-    everything = gathered_copies(regrouped, "seq", 1)
+    cross_dq = sum_at_owner(partial_value, SEQ_AXES, 0).astype(jnp.bfloat16)
+    everything = jnp.transpose(self_all.reshape(latents, 4, feature_width), (1, 0, 2))
+    row_start = lax.axis_index(SEQ_AXES) * block_rows
     all_rows = everything.shape[1]
     query_every = everything[0].reshape(all_rows, local_heads, HEAD_DIM)
     key_every = everything[1].reshape(all_rows, local_heads, HEAD_DIM)
@@ -185,25 +208,31 @@
     return (cross_dq, prefix_dk, prefix_dv, self_dq, self_dk, self_dv)
 
 
+SEQ_AXES = ("y", "zh", "x", "c")
+
+
 def solution(mesh):
+    sizes = dict(mesh.shape)
+    split = mesh.devices.reshape(4, 2, 4, 2, sizes["head"])
+    mesh = jax.sharding.Mesh(split, (*SEQ_AXES, "zl"))
     in_specs = (
-        P("seq", "head"),
-        P("seq", "head"),
-        P("seq", "head"),
-        P("seq", "head"),
-        P("seq", "head"),
-        P("seq"),
-        P(("seq", "head"), None),
-        P(("seq", "head"), None),
-        P(("seq", "head"), None),
-        P(("seq", "head"), None),
+        P(SEQ_AXES, "zl"),
+        P(SEQ_AXES, "zl"),
+        P(SEQ_AXES, "zl"),
+        P(SEQ_AXES, "zl"),
+        P(SEQ_AXES, "zl"),
+        P(SEQ_AXES),
+        P((*SEQ_AXES, "zl"), None),
+        P((*SEQ_AXES, "zl"), None),
+        P((*SEQ_AXES, "zl"), None),
+        P((*SEQ_AXES, "zl"), None),
     )
     out_specs = (
-        P("seq", "head"),
-        P("seq", "head"),
-        P("seq", "head"),
-        P("seq", "head"),
-        P("seq", "head"),
-        P("seq", "head"),
+        P(SEQ_AXES, "zl"),
+        P(SEQ_AXES, "zl"),
+        P(SEQ_AXES, "zl"),
+        P(SEQ_AXES, "zl"),
+        P(SEQ_AXES, "zl"),
+        P(SEQ_AXES, "zl"),
     )
     return jax.shard_map(shards, mesh=mesh, in_specs=in_specs, out_specs=out_specs, check_vma=False)

time: 328 us -> 229 us (0.70)
  the two profiles are of different devices: /device:TPU:64 before, /device:TPU:32 now
where the time goes in v1:
time: 229 us; the launch traced here: 228 us
  blocking collectives  81.5 us (36%)
  waiting for transfers between devices  72.8 us (32%)
  starting transfers between devices  27.6 us (12%)
  other arithmetic  15.1 us (7%)
  between operations  15 us (7%)
  local copies, waits for them, and re-layouts  10.9 us (5%)
  matrix products  5.29 us (2%)
    all_gather x3, blocking collectives, gather_seq(): x = lax.all_gather(x, axis, axis=dim, tiled=True)  42.4 us
    all_gather x4, blocking collectives, merged_seq(): both = lax.all_gather(jnp.stack([row_max, row_sum]), axis)  39.1 us
    all_to_all x1, waiting for transfers between devices, sum_at_owner(): parts = lax.all_to_all(split_up(x, dim, size), axis, 0, 0, tiled=True)  33.3 us
    all_gather x1, waiting for transfers between devices, gather_seq(): x = lax.all_gather(x, axis, axis=dim, tiled=True)  30.7 us
    all_to_all x1, starting transfers between devices, sum_at_owner(): parts = lax.all_to_all(split_up(x, dim, size), axis, 0, 0, tiled=True)  15 us
    all_to_all x1, starting transfers between devices, shards(): lax.all_to_all(stacked, 'zl', split_axis=2, concat_axis=1, tiled=True)  12.6 us
    unnamed x1, other arithmetic  11.6 us
    all_to_all x1, waiting for transfers between devices, shards(): lax.all_to_all(stacked, 'zl', split_axis=2, concat_axis=1, tiled=True)  8.8 us
  transfers between devices with their start and end apart: 3, of which 3 were waited for; matrix products, arithmetic and copies ran while one was open for 2% of the time, Pallas kernels for 0%

profile of v1, /device:TPU:32, one launch (start us, length us, event | category | flops | bytes accessed | tf_op | source)
XLA Modules:
  0.0 228.2 jit_solution(2826771414848816739)
XLA Ops:
  7.2 0.8 pad_maximum_fusion
  8.0 0.9 copy.128
  9.5 11.6 %reduce.4 = bf16[2048,4]{1,0:T(8,128)(2,1)S(1)} reduce(bf16[2048,1,4]{2,1,0:T(2,128)(2,1)S(1)} %bitcast.168, bf16[]{:T(256)} %broadcast.35), dimensions={1}, to_apply=%bitcast.135.reduce_sub_computation | reduce | bytes 32770
  21.1 1.4 reshape.100
  22.5 12.6 %all-to-all-start = ((bf16[8,2,512]{2,1,0:T(2,128)(2,1)}), bf16[8,2,512]{2,1,0:T(2,128)(2,1)S(1)}, u32[]{:S(2)}, u32[]{:S(2)}) async-start(bf16[8,2,512]{2,1,0:T(2,128)(2,1)} %reshape.100), calls=%async_computation | async-start | bytes 32768 | tf_op jit(solution)/shard_map/all_to_all | solution.py:144
  35.3 8.8 %all-to-all-done = bf16[8,2,512]{2,1,0:T(2,128)(2,1)S(1)} async-done(((bf16[8,2,512]{2,1,0:T(2,128)(2,1)}), bf16[8,2,512]{2,1,0:T(2,128)(2,1)S(1)}, u32[]{:S(2)}, u32[]{:S(2)}) %all-to-all-start) | async-done | bytes 16416 | tf_op jit(solution)/shard_map/all_to_all | solution.py:144
  44.1 1.4 reshape.101
  46.2 1.8 all_gather.36
  48.0 12.5 %all_gather.37 = bf16[64,1538]{1,0:T(8,128)(2,1)S(1)} all-gather(bf16[16,1538]{1,0:T(8,128)(2,1)S(1)} %all_gather.36), channel_id=1, replica_groups=mesh['y'=4,'zh'=2,'x'=4,'c'=2,'zl'=8] {'x'}, dimensions={0}, use_global_device_ids=true | all-gather | bytes 246080 | tf_op jit(solution)/shard_map/all_gather | solution.py:111
  60.5 28.1 %all_gather.38 = bf16[128,1538]{1,0:T(8,128)(2,1)} all-gather(bf16[64,1538]{1,0:T(8,128)(2,1)S(1)} %all_gather.37), channel_id=1, replica_groups=mesh['y'=4,'zh'=2,'x'=4,'c'=2,'zl'=8] {'zh'}, dimensions={0}, use_global_device_ids=true | all-gather | bytes 590592 | tf_op jit(solution)/shard_map/all_gather | solution.py:111
  89.4 30.7 %all-gather.6.cloned.1.call-done = bf16[512,1538]{1,0:T(8,128)(2,1)} async-done(((bf16[128,1538]{1,0:T(8,128)(2,1)}), bf16[512,1538]{1,0:T(8,128)(2,1)}) %all-gather.6.cloned.1.call-update) | async-done | bytes 1574928 | tf_op jit(solution)/shard_map/all_gather | solution.py:111
  120.0 0.9 convert_bitcast_fusion
  121.1 1.1 fusion.37
  122.8 1.9 all-gather
  124.8 12.2 %all-gather.1 = f32[8,2,512]{2,1,0:T(2,128)S(1)} all-gather(f32[2,2,512]{2,1,0:T(2,128)S(1)} %pad_maximum_fusion.2), channel_id=3, replica_groups=mesh['y'=4,'zh'=2,'x'=4,'c'=2,'zl'=8] {'x'}, dimensions={0}, use_global_device_ids=true | all-gather | bytes 40960 | tf_op jit(solution)/shard_map/all_gather | solution.py:117
  137.1 13.1 %all-gather.2 = f32[4,2,512]{2,1,0:T(2,128)S(1)} all-gather(f32[2,2,512]{2,1,0:T(2,128)S(1)} %pad_maximum_fusion.3), channel_id=4, replica_groups=mesh['y'=4,'zh'=2,'x'=4,'c'=2,'zl'=8] {'zh'}, dimensions={0}, use_global_device_ids=true | all-gather | bytes 24576 | tf_op jit(solution)/shard_map/all_gather | solution.py:117
  150.3 11.9 %all-gather.3 = f32[8,2,512]{2,1,0:T(2,128)S(1)} all-gather(f32[2,2,512]{2,1,0:T(2,128)S(1)} %pad_maximum_fusion.4), channel_id=5, replica_groups=mesh['y'=4,'zh'=2,'x'=4,'c'=2,'zl'=8] {'y'}, dimensions={0}, use_global_device_ids=true | all-gather | bytes 40960 | tf_op jit(solution)/shard_map/all_gather | solution.py:117
  164.5 0.7 copy.159
  166.4 1.2 reshape_reshape.3
  167.6 15.0 %all-to-all-start.1 = ((f32[64,8,256]{2,1,0:T(8,128)}), f32[64,8,256]{2,1,0:T(8,128)S(1)}, u32[]{:S(2)}, u32[]{:S(2)}) async-start(f32[64,8,256]{2,1,0:T(8,128)} %reshape_reshape.3), calls=%async_computation.1 | async-start | bytes 1048576 | tf_op jit(solution)/shard_map/all_to_all | solution.py:60
  183.9 0.8 fusion.8
  185.6 0.8 fusion.7
  186.4 1.0 fusion.9
  187.4 33.3 %all-to-all-done.1 = f32[64,8,256]{2,1,0:T(8,128)S(1)} async-done(((f32[64,8,256]{2,1,0:T(8,128)}), f32[64,8,256]{2,1,0:T(8,128)S(1)}, u32[]{:S(2)}, u32[]{:S(2)}) %all-to-all-start.1) | async-done | bytes 524320 | tf_op jit(solution)/shard_map/all_to_all | solution.py:60
  (57 shorter events, 8.7 us)
Async XLA Ops:
  7.2 115.3 %copy-start = (bf16[128,256]{1,0:T(8,128)(2,1)S(1)}, bf16[128,256]{1,0:T(8,128)(2,1)}, u32[]{:S(2)}) copy-start(bf16[128,256]{1,0:T(8,128)(2,1)} %param.13) | copy-start | bytes 196612
  7.2 27.9 %copy-start.3 = (bf16[8,256]{1,0:T(8,128)(2,1)S(1)}, bf16[8,256]{1,0:T(8,128)(2,1)}, u32[]{:S(2)}) copy-start(bf16[8,256]{1,0:T(8,128)(2,1)} %param.12) | copy-start | bytes 12292
  7.2 27.9 %copy-start.4 = (bf16[8,256]{1,0:T(8,128)(2,1)S(1)}, bf16[8,256]{1,0:T(8,128)(2,1)}, u32[]{:S(2)}) copy-start(bf16[8,256]{1,0:T(8,128)(2,1)} %param.11) | copy-start | bytes 12292
  9.5 36.6 %copy-start.5 = (bf16[8,256]{1,0:T(8,128)(2,1)S(1)}, bf16[8,256]{1,0:T(8,128)(2,1)}, u32[]{:S(2)}) copy-start(bf16[8,256]{1,0:T(8,128)(2,1)} %param.10) | copy-start | bytes 12292
  22.5 21.6 %all-to-all-start = ((bf16[8,2,512]{2,1,0:T(2,128)(2,1)}), bf16[8,2,512]{2,1,0:T(2,128)(2,1)S(1)}, u32[]{:S(2)}, u32[]{:S(2)}) async-start(bf16[8,2,512]{2,1,0:T(2,128)(2,1)} %reshape.100), calls=%async_computation | async-start | bytes 32768 | tf_op jit(solution)/shard_map/all_to_all | solution.py:144
  35.1 84.9 %all-gather.6.cloned.1.call-start = ((), (), s32[]{:S(2)}) async-start(), calls=%async_computation.2 | async-start | bytes 2129920 | tf_op jit(solution)/shard_map/all_gather | solution.py:111
  122.2 40.3 %copy-start.2 = (bf16[128,256]{1,0:T(8,128)(2,1)S(1)}, bf16[128,256]{1,0:T(8,128)(2,1)}, u32[]{:S(2)}) copy-start(bf16[128,256]{1,0:T(8,128)(2,1)} %param.14) | copy-start | bytes 196612
  122.7 40.5 %copy-start.1 = (bf16[512,1538]{1,0:T(8,128)(2,1)S(1)}, bf16[512,1538]{1,0:T(8,128)(2,1)}, u32[]{:S(2)}) copy-start(bf16[512,1538]{1,0:T(8,128)(2,1)} %all-gather.6.cloned.1.call-done) | copy-start | bytes 4724740
  167.6 53.1 %all-to-all-start.1 = ((f32[64,8,256]{2,1,0:T(8,128)}), f32[64,8,256]{2,1,0:T(8,128)S(1)}, u32[]{:S(2)}, u32[]{:S(2)}) async-start(f32[64,8,256]{2,1,0:T(8,128)} %reshape_reshape.3), calls=%async_computation.1 | async-start | bytes 1048576 | tf_op jit(solution)/shard_map/all_to_all | solution.py:60
Sparse Core Ops, SparseCore 0:
  88.7 31.2 all-gather.5

commit v2 on v1

--- a/solution.py
+++ b/solution.py
@@ -140,10 +140,13 @@
     grad_own = cross_grad.reshape(own_rows, local_heads, HEAD_DIM).astype(jnp.float32)
     out_own = cross_out.reshape(own_rows, local_heads, HEAD_DIM).astype(jnp.float32)
     row_dot = jnp.sum(grad_own * out_own, axis=2).astype(jnp.bfloat16)
-    stacked = jnp.stack([self_q, self_k, self_v, self_grad])
-    regrouped = lax.all_to_all(stacked, "zl", split_axis=2, concat_axis=1, tiled=True)
-    block_rows = regrouped.shape[1]
-    self_cols = jnp.transpose(regrouped, (1, 0, 2)).reshape(block_rows, -1)
+    head_groups = lax.axis_size("zl")
+    stacked = jnp.stack([self_q, self_k, self_v, self_grad]).reshape(4, head_groups, feature_width)
+    regrouped = lax.all_to_all(
+        jnp.transpose(stacked, (1, 0, 2)), "zl", split_axis=0, concat_axis=0, tiled=True
+    )
+    block_rows = regrouped.shape[0]
+    self_cols = regrouped.reshape(block_rows, -1)
     pieces = (cross_q, cross_grad, row_dot, self_cols)
     ends, at = [], 0
     for piece in pieces[:-1]:

time: 229 us -> 218 us (0.952)
  other arithmetic: 15.1 us -> 5.43 us
  local copies, waits for them, and re-layouts: 10.9 us -> 7.11 us
    unnamed x1 -> x4, other arithmetic: 11.6 us -> 2.95 us
    unnamed x18 -> x9, local copies, waits for them, and re-layouts: 4.82 us -> 1.51 us
    all_gather x1, waiting for transfers between devices: 30.7 us -> 33.3 us  [gather_seq(): x = lax.all_gather(x, axis, axis=dim, tiled=True)]
  transfers between devices with their start and end apart: 3 -> 3, of which waited for: 3 -> 3; matrix products, arithmetic and copies ran while one was open for 2% -> 3% of each run, Pallas kernels for 0% -> 0%
where the time goes in v2:
time: 218 us; the launch traced here: 217 us
  blocking collectives  81.3 us (37%)
  waiting for transfers between devices  74.7 us (34%)
  starting transfers between devices  28.2 us (13%)
  between operations  15 us (7%)
  local copies, waits for them, and re-layouts  7.11 us (3%)
  other arithmetic  5.43 us (2%)
  matrix products  5.29 us (2%)
    all_gather x3, blocking collectives, gather_seq(): x = lax.all_gather(x, axis, axis=dim, tiled=True)  42.3 us
    all_gather x4, blocking collectives, merged_seq(): both = lax.all_gather(jnp.stack([row_max, row_sum]), axis)  39 us
    all_to_all x1, waiting for transfers between devices, sum_at_owner(): parts = lax.all_to_all(split_up(x, dim, size), axis, 0, 0, tiled=True)  33.3 us
    all_gather x1, waiting for transfers between devices, gather_seq(): x = lax.all_gather(x, axis, axis=dim, tiled=True)  33.3 us
    all_to_all x1, starting transfers between devices, sum_at_owner(): parts = lax.all_to_all(split_up(x, dim, size), axis, 0, 0, tiled=True)  15.5 us
    all_to_all x1, starting transfers between devices, shards(): lax.all_to_all(jnp.transpose(stacked, (1, 0, 2)), 'zl', split_axis=0, con...  12.6 us
    all_to_all x1, waiting for transfers between devices, shards(): lax.all_to_all(jnp.transpose(stacked, (1, 0, 2)), 'zl', split_axis=0, con...  8.11 us
  transfers between devices with their start and end apart: 3, of which 3 were waited for; matrix products, arithmetic and copies ran while one was open for 3% of the time, Pallas kernels for 0%

profile of v2, /device:TPU:32, one launch (start us, length us, event | category | flops | bytes accessed | tf_op | source)
XLA Modules:
  0.0 217.0 jit_solution(14411078037183456727)
XLA Ops:
  7.2 0.8 reduce.4
  8.7 0.7 reduce.6
  10.8 12.6 %all-to-all-start = ((bf16[8,4,256]{2,1,0:T(4,128)(2,1)}), bf16[8,4,256]{2,1,0:T(4,128)(2,1)S(1)}, u32[]{:S(2)}, u32[]{:S(2)}) async-start(bf16[8,4,256]{2,1,0:T(4,128)(2,1)} %bitcast.153), calls=%async_computation | async-start | bytes 32768 | tf_op jit(solution)/shard_map/all_to_all | solution.py:145
  23.4 0.8 bitcast_reduce_fusion.4
  24.3 8.1 %all-to-all-done = bf16[8,4,256]{2,1,0:T(4,128)(2,1)S(1)} async-done(((bf16[8,4,256]{2,1,0:T(4,128)(2,1)}), bf16[8,4,256]{2,1,0:T(4,128)(2,1)S(1)}, u32[]{:S(2)}, u32[]{:S(2)}) %all-to-all-start) | async-done | bytes 16416 | tf_op jit(solution)/shard_map/all_to_all | solution.py:145
  32.5 0.8 concatenate.4
  33.2 1.8 all_gather.36
  35.1 12.5 %all_gather.37 = bf16[64,1538]{1,0:T(8,128)(2,1)S(1)} all-gather(bf16[16,1538]{1,0:T(8,128)(2,1)S(1)} %all_gather.36), channel_id=1, replica_groups=mesh['y'=4,'zh'=2,'x'=4,'c'=2,'zl'=8] {'x'}, dimensions={0}, use_global_device_ids=true | all-gather | bytes 246080 | tf_op jit(solution)/shard_map/all_gather | solution.py:111
  47.6 28.0 %all_gather.38 = bf16[128,1538]{1,0:T(8,128)(2,1)S(1)} all-gather(bf16[64,1538]{1,0:T(8,128)(2,1)S(1)} %all_gather.37), channel_id=1, replica_groups=mesh['y'=4,'zh'=2,'x'=4,'c'=2,'zl'=8] {'zh'}, dimensions={0}, use_global_device_ids=true | all-gather | bytes 590592 | tf_op jit(solution)/shard_map/all_gather | solution.py:111
  75.5 0.9 copy.101
  77.3 33.3 %all-gather.6.cloned.1.call-done = bf16[512,1538]{0,1:T(8,128)(2,1)} async-done(((bf16[128,1538]{0,1:T(8,128)(2,1)}), bf16[512,1538]{0,1:T(8,128)(2,1)}) %all-gather.6.cloned.1.call-update) | async-done | bytes 1574928 | tf_op jit(solution)/shard_map/all_gather | solution.py:111
  110.6 1.2 fusion.37
  112.1 1.8 all-gather
  114.0 12.2 %all-gather.1 = f32[8,2,512]{2,1,0:T(2,128)S(1)} all-gather(f32[2,2,512]{2,1,0:T(2,128)S(1)} %pad_maximum_fusion.2), channel_id=3, replica_groups=mesh['y'=4,'zh'=2,'x'=4,'c'=2,'zl'=8] {'x'}, dimensions={0}, use_global_device_ids=true | all-gather | bytes 40960 | tf_op jit(solution)/shard_map/all_gather | solution.py:117
  126.3 13.1 %all-gather.2 = f32[4,2,512]{2,1,0:T(2,128)S(1)} all-gather(f32[2,2,512]{2,1,0:T(2,128)S(1)} %pad_maximum_fusion.3), channel_id=4, replica_groups=mesh['y'=4,'zh'=2,'x'=4,'c'=2,'zl'=8] {'zh'}, dimensions={0}, use_global_device_ids=true | all-gather | bytes 24576 | tf_op jit(solution)/shard_map/all_gather | solution.py:117
  139.4 11.9 %all-gather.3 = f32[8,2,512]{2,1,0:T(2,128)S(1)} all-gather(f32[2,2,512]{2,1,0:T(2,128)S(1)} %pad_maximum_fusion.4), channel_id=5, replica_groups=mesh['y'=4,'zh'=2,'x'=4,'c'=2,'zl'=8] {'y'}, dimensions={0}, use_global_device_ids=true | all-gather | bytes 40960 | tf_op jit(solution)/shard_map/all_gather | solution.py:117
  152.8 0.7 copy.126
  153.5 0.7 copy.127
  154.7 1.2 reshape_reshape.3
  155.9 15.5 %all-to-all-start.1 = ((f32[64,8,256]{2,1,0:T(8,128)}), f32[64,8,256]{2,1,0:T(8,128)S(1)}, u32[]{:S(2)}, u32[]{:S(2)}) async-start(f32[64,8,256]{2,1,0:T(8,128)} %reshape_reshape.3), calls=%async_computation.1 | async-start | bytes 1048576 | tf_op jit(solution)/shard_map/all_to_all | solution.py:60
  172.7 0.8 fusion.8
  174.5 0.8 fusion.7
  175.2 1.0 fusion.9
  176.2 33.3 %all-to-all-done.1 = f32[64,8,256]{2,1,0:T(8,128)S(1)} async-done(((f32[64,8,256]{2,1,0:T(8,128)}), f32[64,8,256]{2,1,0:T(8,128)S(1)}, u32[]{:S(2)}, u32[]{:S(2)}) %all-to-all-start.1) | async-done | bytes 524320 | tf_op jit(solution)/shard_map/all_to_all | solution.py:60
  (51 shorter events, 7.5 us)
Async XLA Ops:
  7.2 104.6 %copy-start = (bf16[128,256]{1,0:T(8,128)(2,1)S(1)}, bf16[128,256]{1,0:T(8,128)(2,1)}, u32[]{:S(2)}) copy-start(bf16[128,256]{1,0:T(8,128)(2,1)} %param.13) | copy-start | bytes 196612
  10.8 21.6 %all-to-all-start = ((bf16[8,4,256]{2,1,0:T(4,128)(2,1)}), bf16[8,4,256]{2,1,0:T(4,128)(2,1)S(1)}, u32[]{:S(2)}, u32[]{:S(2)}) async-start(bf16[8,4,256]{2,1,0:T(4,128)(2,1)} %bitcast.153), calls=%async_computation | async-start | bytes 32768 | tf_op jit(solution)/shard_map/all_to_all | solution.py:145
  23.4 87.1 %all-gather.6.cloned.1.call-start = ((), (), s32[]{:S(2)}) async-start(), calls=%async_computation.2 | async-start | bytes 1976320 | tf_op jit(solution)/shard_map/all_gather | solution.py:111
  76.5 75.2 %copy-start.2 = (bf16[128,256]{1,0:T(8,128)(2,1)S(1)}, bf16[128,256]{1,0:T(8,128)(2,1)}, u32[]{:S(2)}) copy-start(bf16[128,256]{1,0:T(8,128)(2,1)} %param.14) | copy-start | bytes 196612
  110.6 41.1 %copy-start.1 = (bf16[512,1538]{0,1:T(8,128)(2,1)S(1)}, bf16[512,1538]{0,1:T(8,128)(2,1)}, u32[]{:S(2)}) copy-start(bf16[512,1538]{0,1:T(8,128)(2,1)} %all-gather.6.cloned.1.call-done) | copy-start | bytes 4724740
  155.9 53.6 %all-to-all-start.1 = ((f32[64,8,256]{2,1,0:T(8,128)}), f32[64,8,256]{2,1,0:T(8,128)S(1)}, u32[]{:S(2)}, u32[]{:S(2)}) async-start(f32[64,8,256]{2,1,0:T(8,128)} %reshape_reshape.3), calls=%async_computation.1 | async-start | bytes 1048576 | tf_op jit(solution)/shard_map/all_to_all | solution.py:60
Sparse Core Ops, SparseCore 0:
  76.6 33.9 all-gather.5

commit v3 on v2

--- a/solution.py
+++ b/solution.py
@@ -106,10 +106,15 @@
 SEQ_PARTS = ("c", "x", "zh", "y")
 
 
-def gather_seq(x, dim):
-    for axis in SEQ_PARTS:
-        x = lax.all_gather(x, axis, axis=dim, tiled=True)
-    return x
+GATHER_ORDER = ("zh", "c", "x", "y")
+
+
+def gather_seq(x):
+    for axis in GATHER_ORDER:
+        x = lax.all_gather(x, axis, axis=0, tiled=False)
+    order = [GATHER_ORDER[::-1].index(axis) for axis in SEQ_AXES]
+    x = jnp.transpose(x, (*order, *range(4, x.ndim)))
+    return x.reshape(-1, *x.shape[5:])
 
 
 def merged_seq(row_max, row_sum):
@@ -152,7 +157,7 @@
     for piece in pieces[:-1]:
         at += piece.shape[1]
         ends.append(at)
-    gathered = gather_seq(jnp.concatenate(pieces, axis=1), 0)
+    gathered = gather_seq(jnp.concatenate(pieces, axis=1))
     query_all, grad_all, dots_all, self_all = jnp.split(gathered, ends, axis=1)
     latents = query_all.shape[0]
     query_heads = query_all.reshape(latents, local_heads, HEAD_DIM)

time: 218 us -> 201 us (0.922)
  blocking collectives: 81.3 us -> 68.6 us
    all_gather x3, blocking collectives: 42.3 us -> 29.6 us  [gather_seq(): x = lax.all_gather(x, axis, axis=0, tiled=False)]
    unnamed x4 -> x0, other arithmetic: 2.95 us -> none
where the time goes in v3:
time: 201 us
  waiting for transfers between devices  73 us (36%)
  blocking collectives  68.6 us (34%)
  starting transfers between devices  27.6 us (14%)
  between operations  14.9 us (7%)
  local copies, waits for them, and re-layouts  7.31 us (4%)
  matrix products  5.29 us (3%)
  other arithmetic  3.92 us (2%)
    all_gather x4, blocking collectives, merged_seq(): both = lax.all_gather(jnp.stack([row_max, row_sum]), axis)  39 us
    all_to_all x1, waiting for transfers between devices, sum_at_owner(): parts = lax.all_to_all(split_up(x, dim, size), axis, 0, 0, tiled=True)  33.3 us
    all_gather x1, waiting for transfers between devices, gather_seq(): x = lax.all_gather(x, axis, axis=0, tiled=False)  31.5 us
    all_gather x3, blocking collectives, gather_seq(): x = lax.all_gather(x, axis, axis=0, tiled=False)  29.6 us
    all_to_all x1, starting transfers between devices, sum_at_owner(): parts = lax.all_to_all(split_up(x, dim, size), axis, 0, 0, tiled=True)  15 us
    all_to_all x1, starting transfers between devices, shards(): lax.all_to_all(jnp.transpose(stacked, (1, 0, 2)), 'zl', split_axis=0, con...  12.6 us
    all_to_all x1, waiting for transfers between devices, shards(): lax.all_to_all(jnp.transpose(stacked, (1, 0, 2)), 'zl', split_axis=0, con...  8.11 us
  transfers between devices with their start and end apart: 3, of which 3 were waited for; matrix products, arithmetic and copies ran while one was open for 3% of the time, Pallas kernels for 0%

profile of v3, /device:TPU:32, one launch (start us, length us, event | category | flops | bytes accessed | tf_op | source)
XLA Modules:
  0.0 200.7 jit_solution(11424457720307250681)
XLA Ops:
  7.2 1.4 maximum_bitcast_fusion
  8.6 12.6 %all-to-all-start = ((bf16[8,4,256]{2,1,0:T(4,128)(2,1)}), bf16[8,4,256]{2,1,0:T(4,128)(2,1)S(1)}, u32[]{:S(2)}, u32[]{:S(2)}) async-start(bf16[8,4,256]{2,1,0:T(4,128)(2,1)} %maximum_bitcast_fusion), calls=%async_computation | async-start | bytes 32768 | tf_op jit(solution)/shard_map/all_to_all | solution.py:150
  21.2 0.8 bitcast_reduce_fusion.4
  22.1 8.1 %all-to-all-done = bf16[8,4,256]{2,1,0:T(4,128)(2,1)S(1)} async-done(((bf16[8,4,256]{2,1,0:T(4,128)(2,1)}), bf16[8,4,256]{2,1,0:T(4,128)(2,1)S(1)}, u32[]{:S(2)}, u32[]{:S(2)}) %all-to-all-start) | async-done | bytes 16416 | tf_op jit(solution)/shard_map/all_to_all | solution.py:150
  30.3 0.8 concatenate.4
  31.0 14.1 %all-gather = bf16[16,1538]{1,0:T(8,128)(2,1)S(1)} all-gather(bf16[8,1538]{1,0:T(8,128)(2,1)S(1)} %concatenate.4), channel_id=2, replica_groups=mesh['y'=4,'zh'=2,'x'=4,'c'=2,'zl'=8] {'zh'}, dimensions={0}, use_global_device_ids=true | all-gather | bytes 73824 | tf_op jit(solution)/shard_map/all_gather | solution.py:114
  45.1 1.9 all-gather.1
  47.0 13.7 %all-gather.2 = bf16[8,2,8,1538]{3,2,1,0:T(8,128)(2,1)} all-gather(bf16[2,2,8,1538]{3,2,1,0:T(8,128)(2,1)S(1)} %bitcast.183), channel_id=4, replica_groups=mesh['y'=4,'zh'=2,'x'=4,'c'=2,'zl'=8] {'x'}, dimensions={0}, use_global_device_ids=true | all-gather | bytes 492160 | tf_op jit(solution)/shard_map/all_gather | solution.py:114
  61.4 31.5 %all-gather.10.cloned.1.call-done = bf16[16,2,2,8,1538]{4,3,2,1,0:T(8,128)(2,1)} async-done(((bf16[4,2,2,8,1538]{4,3,2,1,0:T(8,128)(2,1)}), bf16[16,2,2,8,1538]{4,3,2,1,0:T(8,128)(2,1)}) %all-gather.10.cloned.1.call-update) | async-done | bytes 1574928 | tf_op jit(solution)/shard_map/all_gather | solution.py:114
  93.0 1.6 copy.68
  94.7 0.6 split.19
  96.1 1.8 all-gather.4
  98.0 12.2 %all-gather.5 = f32[8,2,512]{2,1,0:T(2,128)S(1)} all-gather(f32[2,2,512]{2,1,0:T(2,128)S(1)} %pad_maximum_fusion.1), channel_id=7, replica_groups=mesh['y'=4,'zh'=2,'x'=4,'c'=2,'zl'=8] {'x'}, dimensions={0}, use_global_device_ids=true | all-gather | bytes 40960 | tf_op jit(solution)/shard_map/all_gather | solution.py:122
  110.2 13.1 %all-gather.6 = f32[4,2,512]{2,1,0:T(2,128)S(1)} all-gather(f32[2,2,512]{2,1,0:T(2,128)S(1)} %pad_maximum_fusion.2), channel_id=8, replica_groups=mesh['y'=4,'zh'=2,'x'=4,'c'=2,'zl'=8] {'zh'}, dimensions={0}, use_global_device_ids=true | all-gather | bytes 24576 | tf_op jit(solution)/shard_map/all_gather | solution.py:122
  123.4 11.9 %all-gather.7 = f32[8,2,512]{2,1,0:T(2,128)S(1)} all-gather(f32[2,2,512]{2,1,0:T(2,128)S(1)} %pad_maximum_fusion.3), channel_id=9, replica_groups=mesh['y'=4,'zh'=2,'x'=4,'c'=2,'zl'=8] {'y'}, dimensions={0}, use_global_device_ids=true | all-gather | bytes 40960 | tf_op jit(solution)/shard_map/all_gather | solution.py:122
  137.0 0.7 copy.97
  137.7 0.7 copy.98
  138.9 1.2 reshape_reshape.3
  140.1 15.0 %all-to-all-start.1 = ((f32[64,8,256]{2,1,0:T(8,128)}), f32[64,8,256]{2,1,0:T(8,128)S(1)}, u32[]{:S(2)}, u32[]{:S(2)}) async-start(f32[64,8,256]{2,1,0:T(8,128)} %reshape_reshape.3), calls=%async_computation.1 | async-start | bytes 1048576 | tf_op jit(solution)/shard_map/all_to_all | solution.py:60
  156.4 0.8 fusion.8
  158.1 0.8 fusion.7
  158.9 1.0 fusion.9
  159.9 33.3 %all-to-all-done.1 = f32[64,8,256]{2,1,0:T(8,128)S(1)} async-done(((f32[64,8,256]{2,1,0:T(8,128)}), f32[64,8,256]{2,1,0:T(8,128)S(1)}, u32[]{:S(2)}, u32[]{:S(2)}) %all-to-all-start.1) | async-done | bytes 524320 | tf_op jit(solution)/shard_map/all_to_all | solution.py:60
  193.2 0.7 reduce_sum.87
  (44 shorter events, 5.4 us)
Async XLA Ops:
  7.2 88.6 %copy-start = (bf16[128,256]{1,0:T(8,128)(2,1)S(1)}, bf16[128,256]{1,0:T(8,128)(2,1)}, u32[]{:S(2)}) copy-start(bf16[128,256]{1,0:T(8,128)(2,1)} %param.13) | copy-start | bytes 196612
  8.6 21.6 %all-to-all-start = ((bf16[8,4,256]{2,1,0:T(4,128)(2,1)}), bf16[8,4,256]{2,1,0:T(4,128)(2,1)S(1)}, u32[]{:S(2)}, u32[]{:S(2)}) async-start(bf16[8,4,256]{2,1,0:T(4,128)(2,1)} %maximum_bitcast_fusion), calls=%async_computation | async-start | bytes 32768 | tf_op jit(solution)/shard_map/all_to_all | solution.py:150
  21.2 71.7 %all-gather.10.cloned.1.call-start = ((), (), s32[]{:S(2)}) async-start(), calls=%async_computation.2 | async-start | bytes 2129920 | tf_op jit(solution)/shard_map/all_gather | solution.py:114
  95.3 40.3 %copy-start.1 = (bf16[128,256]{1,0:T(8,128)(2,1)S(1)}, bf16[128,256]{1,0:T(8,128)(2,1)}, u32[]{:S(2)}) copy-start(bf16[128,256]{1,0:T(8,128)(2,1)} %param.14) | copy-start | bytes 196612
  140.1 53.1 %all-to-all-start.1 = ((f32[64,8,256]{2,1,0:T(8,128)}), f32[64,8,256]{2,1,0:T(8,128)S(1)}, u32[]{:S(2)}, u32[]{:S(2)}) async-start(f32[64,8,256]{2,1,0:T(8,128)} %reshape_reshape.3), calls=%async_computation.1 | async-start | bytes 1048576 | tf_op jit(solution)/shard_map/all_to_all | solution.py:60
Sparse Core Ops, SparseCore 0:
  60.8 32.1 all-gather.9

commit v4 on v3

--- a/solution.py
+++ b/solution.py
@@ -109,8 +109,8 @@
 GATHER_ORDER = ("zh", "c", "x", "y")
 
 
-def gather_seq(x):
-    for axis in GATHER_ORDER:
+def gather_seq(x, axes):
+    for axis in axes:
         x = lax.all_gather(x, axis, axis=0, tiled=False)
     order = [GATHER_ORDER[::-1].index(axis) for axis in SEQ_AXES]
     x = jnp.transpose(x, (*order, *range(4, x.ndim)))
@@ -152,13 +152,22 @@
     )
     block_rows = regrouped.shape[0]
     self_cols = regrouped.reshape(block_rows, -1)
-    pieces = (cross_q, cross_grad, row_dot, self_cols)
-    ends, at = [], 0
-    for piece in pieces[:-1]:
-        at += piece.shape[1]
-        ends.append(at)
-    gathered = gather_seq(jnp.concatenate(pieces, axis=1))
-    query_all, grad_all, dots_all, self_all = jnp.split(gathered, ends, axis=1)
+    cross_cols = jnp.concatenate((cross_q, cross_grad, row_dot), axis=1)
+    cross_width = cross_cols.shape[1]
+    first = jnp.concatenate((cross_cols, self_cols), axis=1)
+    for axis in GATHER_ORDER[:2]:
+        first = lax.all_gather(first, axis, axis=0)
+    core = lax.axis_index("c")
+    self_heads = first[..., cross_width:].reshape(*first.shape[:-1], 4, local_heads, HEAD_DIM)
+    self_mine = lax.dynamic_index_in_dim(self_heads, core, axis=4, keepdims=False)
+    rest = jnp.concatenate(
+        (first[..., :cross_width], self_mine.reshape(*first.shape[:-1], -1)), axis=-1
+    )
+    gathered = gather_seq(rest, GATHER_ORDER[2:])
+    query_all = gathered[:, : cross_q.shape[1]]
+    grad_all = gathered[:, cross_q.shape[1] : 2 * cross_q.shape[1]]
+    dots_all = gathered[:, 2 * cross_q.shape[1] : cross_width]
+    self_all = gathered[:, cross_width:]
     latents = query_all.shape[0]
     query_heads = query_all.reshape(latents, local_heads, HEAD_DIM)
     grad_heads = grad_all.reshape(latents, local_heads, HEAD_DIM)
@@ -184,13 +193,12 @@
     )
     partial_value = contract_cols(grad_scores, key_heads).reshape(latents, feature_width)
     cross_dq = sum_at_owner(partial_value, SEQ_AXES, 0).astype(jnp.bfloat16)
-    everything = jnp.transpose(self_all.reshape(latents, 4, feature_width), (1, 0, 2))
-    row_start = lax.axis_index(SEQ_AXES) * block_rows
+    everything = jnp.transpose(self_all.reshape(latents, 4, HEAD_DIM), (1, 0, 2))
     all_rows = everything.shape[1]
-    query_every = everything[0].reshape(all_rows, local_heads, HEAD_DIM)
-    key_every = everything[1].reshape(all_rows, local_heads, HEAD_DIM)
-    value_every = everything[2].reshape(all_rows, local_heads, HEAD_DIM)
-    grad_every = everything[3].reshape(all_rows, local_heads, HEAD_DIM)
+    query_every = everything[0].reshape(all_rows, 1, HEAD_DIM)
+    key_every = everything[1].reshape(all_rows, 1, HEAD_DIM)
+    value_every = everything[2].reshape(all_rows, 1, HEAD_DIM)
+    grad_every = everything[3].reshape(all_rows, 1, HEAD_DIM)
     row_ids = jnp.arange(all_rows)
     causal_full = row_ids[:, None] >= row_ids[None, :]
     full_scores = head_scores(query_every, key_every, score_scale)
@@ -201,18 +209,23 @@
     full_out = contract_cols(full_half, value_every)
     full_dot = jnp.sum(grad_every.astype(jnp.float32) * full_out, axis=2)
     full_gs = scores_grad(full_weights, grad_every, value_every, full_dot, score_scale)
-    query_part = lax.dynamic_slice_in_dim(full_gs, row_start, block_rows, 1)
-    self_dq = (
-        contract_cols(query_part, key_every).reshape(block_rows, feature_width).astype(jnp.bfloat16)
-    )
-    key_part = lax.dynamic_slice_in_dim(full_gs, row_start, block_rows, 2)
-    half_part = lax.dynamic_slice_in_dim(full_half, row_start, block_rows, 2)
-    self_dk = (
-        contract_rows(key_part, query_every).reshape(block_rows, feature_width).astype(jnp.bfloat16)
-    )
-    self_dv = (
-        contract_rows(half_part, grad_every).reshape(block_rows, feature_width).astype(jnp.bfloat16)
-    )
+    cores = lax.axis_size("c")
+    chip_rows = block_rows * cores
+    chip_start = (lax.axis_index(SEQ_AXES) - core) * block_rows
+    query_part = lax.dynamic_slice_in_dim(full_gs, chip_start, chip_rows, 1)
+    key_part = lax.dynamic_slice_in_dim(full_gs, chip_start, chip_rows, 2)
+    half_part = lax.dynamic_slice_in_dim(full_half, chip_start, chip_rows, 2)
+    head_results = jnp.stack(
+        [
+            contract_cols(query_part, key_every),
+            contract_rows(key_part, query_every),
+            contract_rows(half_part, grad_every),
+        ]
+    ).astype(jnp.bfloat16)
+    both = lax.all_gather(head_results.reshape(3, chip_rows, HEAD_DIM), "c", axis=0)
+    mine = lax.dynamic_slice_in_dim(both, core * block_rows, block_rows, 2)
+    mine = jnp.transpose(mine, (1, 2, 0, 3)).reshape(3, block_rows, feature_width)
+    self_dq, self_dk, self_dv = mine[0], mine[1], mine[2]
     return (cross_dq, prefix_dk, prefix_dv, self_dq, self_dk, self_dv)
 
 

time: 201 us -> 197 us (0.980)
  waiting for transfers between devices: 73 us -> 70.1 us
  matrix products: 5.29 us -> 2.75 us
    all_gather x0 -> x3, blocking collectives: none -> 17.8 us  [the longest x2 15.9 us: shards(): first = lax.all_gather(first, axis, axis=0)]
    all_gather x3 -> x1, blocking collectives: 29.6 us -> 13.4 us  [gather_seq(): x = lax.all_gather(x, axis, axis=0, tiled=False)]
    all_gather x1, waiting for transfers between devices: 31.5 us -> 28.3 us  [gather_seq(): x = lax.all_gather(x, axis, axis=0, tiled=False)]
  transfers between devices with their start and end apart: 3 -> 3, of which waited for: 3 -> 3; matrix products, arithmetic and copies ran while one was open for 3% -> 2% of each run, Pallas kernels for 0% -> 0%
where the time goes in v4:
time: 197 us
  blocking collectives  70.2 us (36%)
  waiting for transfers between devices  70.1 us (36%)
  starting transfers between devices  27.8 us (14%)
  between operations  14.9 us (8%)
  local copies, waits for them, and re-layouts  7.01 us (4%)
  other arithmetic  3.69 us (2%)
  matrix products  2.75 us (1%)
    all_gather x4, blocking collectives, merged_seq(): both = lax.all_gather(jnp.stack([row_max, row_sum]), axis)  39 us
    all_to_all x1, waiting for transfers between devices, sum_at_owner(): parts = lax.all_to_all(split_up(x, dim, size), axis, 0, 0, tiled=True)  33.7 us
    all_gather x1, waiting for transfers between devices, gather_seq(): x = lax.all_gather(x, axis, axis=0, tiled=False)  28.3 us
    all_gather x2, blocking collectives, shards(): first = lax.all_gather(first, axis, axis=0)  15.9 us
    all_to_all x1, starting transfers between devices, sum_at_owner(): parts = lax.all_to_all(split_up(x, dim, size), axis, 0, 0, tiled=True)  15.2 us
    all_gather x1, blocking collectives, gather_seq(): x = lax.all_gather(x, axis, axis=0, tiled=False)  13.4 us
    all_to_all x1, starting transfers between devices, shards(): lax.all_to_all(jnp.transpose(stacked, (1, 0, 2)), 'zl', split_axis=0, con...  12.6 us
    all_to_all x1, waiting for transfers between devices, shards(): lax.all_to_all(jnp.transpose(stacked, (1, 0, 2)), 'zl', split_axis=0, con...  8.11 us
  transfers between devices with their start and end apart: 3, of which 3 were waited for; matrix products, arithmetic and copies ran while one was open for 2% of the time, Pallas kernels for 0%

profile of v4, /device:TPU:32, one launch (start us, length us, event | category | flops | bytes accessed | tf_op | source)
XLA Modules:
  0.0 196.5 jit_solution(2809000943631721643)
XLA Ops:
  7.2 1.4 maximum_bitcast_fusion
  8.6 12.6 %all-to-all-start = ((bf16[8,4,256]{2,1,0:T(4,128)(2,1)}), bf16[8,4,256]{2,1,0:T(4,128)(2,1)S(1)}, u32[]{:S(2)}, u32[]{:S(2)}) async-start(bf16[8,4,256]{2,1,0:T(4,128)(2,1)} %maximum_bitcast_fusion), calls=%async_computation | async-start | bytes 32768 | tf_op jit(solution)/shard_map/all_to_all | solution.py:150
  21.2 0.8 bitcast_reduce_fusion.4
  22.1 8.1 %all-to-all-done = bf16[8,4,256]{2,1,0:T(4,128)(2,1)S(1)} async-done(((bf16[8,4,256]{2,1,0:T(4,128)(2,1)}), bf16[8,4,256]{2,1,0:T(4,128)(2,1)S(1)}, u32[]{:S(2)}, u32[]{:S(2)}) %all-to-all-start) | async-done | bytes 16416 | tf_op jit(solution)/shard_map/all_to_all | solution.py:150
  30.3 0.8 concatenate.17
  31.0 14.1 %all-gather = bf16[16,1538]{1,0:T(8,128)(2,1)S(1)} all-gather(bf16[8,1538]{1,0:T(8,128)(2,1)S(1)} %concatenate.17), channel_id=2, replica_groups=mesh['y'=4,'zh'=2,'x'=4,'c'=2,'zl'=8] {'zh'}, dimensions={0}, use_global_device_ids=true | all-gather | bytes 73824 | tf_op jit(solution)/shard_map/all_gather | solution.py:159
  45.1 1.9 all-gather.1
  47.2 13.4 %all-gather.2 = bf16[8,2,8,1026]{3,2,1,0:T(8,128)(2,1)} all-gather(bf16[2,2,8,1026]{3,2,1,0:T(8,128)(2,1)S(1)} %pad_maximum_fusion), channel_id=4, replica_groups=mesh['y'=4,'zh'=2,'x'=4,'c'=2,'zl'=8] {'x'}, dimensions={0}, use_global_device_ids=true | all-gather | bytes 328320 | tf_op jit(solution)/shard_map/all_gather | solution.py:114
  61.3 28.3 %all-gather.10.cloned.1.call-done = bf16[16,2,2,8,1026]{4,3,2,1,0:T(8,128)(2,1)} async-done(((bf16[4,2,2,8,1026]{4,3,2,1,0:T(8,128)(2,1)}), bf16[16,2,2,8,1026]{4,3,2,1,0:T(8,128)(2,1)}) %all-gather.10.cloned.1.call-update) | async-done | bytes 1050640 | tf_op jit(solution)/shard_map/all_gather | solution.py:114
  89.6 1.4 copy.57
  92.1 1.8 all-gather.4
  94.0 12.2 %all-gather.5 = f32[8,2,512]{2,1,0:T(2,128)S(1)} all-gather(f32[2,2,512]{2,1,0:T(2,128)S(1)} %pad_maximum_fusion.3), channel_id=7, replica_groups=mesh['y'=4,'zh'=2,'x'=4,'c'=2,'zl'=8] {'x'}, dimensions={0}, use_global_device_ids=true | all-gather | bytes 40960 | tf_op jit(solution)/shard_map/all_gather | solution.py:122
  106.3 13.1 %all-gather.6 = f32[4,2,512]{2,1,0:T(2,128)S(1)} all-gather(f32[2,2,512]{2,1,0:T(2,128)S(1)} %pad_maximum_fusion.4), channel_id=8, replica_groups=mesh['y'=4,'zh'=2,'x'=4,'c'=2,'zl'=8] {'zh'}, dimensions={0}, use_global_device_ids=true | all-gather | bytes 24576 | tf_op jit(solution)/shard_map/all_gather | solution.py:122
  119.4 11.9 %all-gather.7 = f32[8,2,512]{2,1,0:T(2,128)S(1)} all-gather(f32[2,2,512]{2,1,0:T(2,128)S(1)} %pad_maximum_fusion.5), channel_id=9, replica_groups=mesh['y'=4,'zh'=2,'x'=4,'c'=2,'zl'=8] {'y'}, dimensions={0}, use_global_device_ids=true | all-gather | bytes 40960 | tf_op jit(solution)/shard_map/all_gather | solution.py:122
  132.6 0.7 copy.77
  133.4 0.7 copy.78
  134.1 0.4 copy.72
  134.5 1.2 reshape_reshape.3
  135.7 15.2 %all-to-all-start.1 = ((f32[64,8,256]{2,1,0:T(8,128)}), f32[64,8,256]{2,1,0:T(8,128)S(1)}, u32[]{:S(2)}, u32[]{:S(2)}) async-start(f32[64,8,256]{2,1,0:T(8,128)} %reshape_reshape.3), calls=%async_computation.1 | async-start | bytes 1048576 | tf_op jit(solution)/shard_map/all_to_all | solution.py:60
  152.1 0.4 fusion.3
  152.9 1.8 all_gather.67
  154.7 0.6 slice_bitcast_fusion.13
  155.3 33.7 %all-to-all-done.1 = f32[64,8,256]{2,1,0:T(8,128)S(1)} async-done(((f32[64,8,256]{2,1,0:T(8,128)}), f32[64,8,256]{2,1,0:T(8,128)S(1)}, u32[]{:S(2)}, u32[]{:S(2)}) %all-to-all-start.1) | async-done | bytes 524320 | tf_op jit(solution)/shard_map/all_to_all | solution.py:60
  189.0 0.7 reduce_sum.87
  (50 shorter events, 4.3 us)
Async XLA Ops:
  7.2 84.6 %copy-start = (bf16[128,256]{1,0:T(8,128)(2,1)S(1)}, bf16[128,256]{1,0:T(8,128)(2,1)}, u32[]{:S(2)}) copy-start(bf16[128,256]{1,0:T(8,128)(2,1)} %param.13) | copy-start | bytes 196612
  8.6 21.6 %all-to-all-start = ((bf16[8,4,256]{2,1,0:T(4,128)(2,1)}), bf16[8,4,256]{2,1,0:T(4,128)(2,1)S(1)}, u32[]{:S(2)}, u32[]{:S(2)}) async-start(bf16[8,4,256]{2,1,0:T(4,128)(2,1)} %maximum_bitcast_fusion), calls=%async_computation | async-start | bytes 32768 | tf_op jit(solution)/shard_map/all_to_all | solution.py:150
  21.2 68.4 %all-gather.10.cloned.1.call-start = ((), (), s32[]{:S(2)}) async-start(), calls=%async_computation.2 | async-start | bytes 1474560 | tf_op jit(solution)/shard_map/all_gather | solution.py:114
  91.7 39.9 %copy-start.1 = (bf16[128,256]{1,0:T(8,128)(2,1)S(1)}, bf16[128,256]{1,0:T(8,128)(2,1)}, u32[]{:S(2)}) copy-start(bf16[128,256]{1,0:T(8,128)(2,1)} %param.14) | copy-start | bytes 196612
  135.7 53.3 %all-to-all-start.1 = ((f32[64,8,256]{2,1,0:T(8,128)}), f32[64,8,256]{2,1,0:T(8,128)S(1)}, u32[]{:S(2)}, u32[]{:S(2)}) async-start(f32[64,8,256]{2,1,0:T(8,128)} %reshape_reshape.3), calls=%async_computation.1 | async-start | bytes 1048576 | tf_op jit(solution)/shard_map/all_to_all | solution.py:60
Sparse Core Ops, SparseCore 0:
  60.7 28.8 all-gather.9

commit v5 on v4

--- a/solution.py
+++ b/solution.py
@@ -117,13 +117,29 @@
     return x.reshape(-1, *x.shape[5:])
 
 
-def merged_seq(row_max, row_sum):
-    for axis in SEQ_PARTS:
-        both = lax.all_gather(jnp.stack([row_max, row_sum]), axis)
-        top = jnp.max(both[:, 0], axis=0)
-        row_sum = jnp.sum(both[:, 1] * jnp.exp(both[:, 0] - top), axis=0)
+def merged_with_dq(row_max, row_sum, partial_dq):
+    rows = partial_dq.shape[0]
+    width = partial_dq[0].size
+    start = 0
+    for axis in SEQ_AXES:
+        size = lax.axis_size(axis)
+        rows //= size
+        stats = jnp.stack([row_max, row_sum]).reshape(1, -1)
+        send = jnp.concatenate(
+            [partial_dq.reshape(size, -1), jnp.broadcast_to(stats, (size, stats.shape[1]))], axis=1
+        )
+        got = lax.all_to_all(send, axis, 0, 0, tiled=True)
+        got_dq = got[:, : rows * width].reshape(size, rows, *partial_dq.shape[1:])
+        got_stats = got[:, rows * width :].reshape(size, 2, *row_max.shape)
+        top = jnp.max(got_stats[:, 0], axis=0)
+        rescale = jnp.exp(got_stats[:, 0] - top)
+        row_sum = jnp.sum(got_stats[:, 1] * rescale, axis=0)
         row_max = top
-    return row_max, row_sum
+        start = start + lax.axis_index(axis) * rows
+        dq_rescale = jnp.transpose(lax.dynamic_slice_in_dim(rescale, start, rows, 2), (0, 2, 1))
+        partial_dq = jnp.sum(dq_rescale[..., None] * got_dq, axis=0)
+    own_sum = jnp.transpose(lax.dynamic_slice_in_dim(row_sum, start, rows, 1))
+    return row_max, row_sum, partial_dq / own_sum[..., None]
 
 
 def shards(
@@ -177,10 +193,22 @@
     scores = head_scores(query_heads, key_heads, score_scale)
     scores = jnp.where(valid_keys[None, None, :], scores, -jnp.inf)
     row_max = jnp.max(scores, axis=2)
-    row_sum = jnp.sum(jnp.exp(scores - row_max[:, :, None]), axis=2)
-    row_maxes, row_sums = merged_seq(row_max, row_sum)
+    shifted = jnp.exp(scores - row_max[:, :, None])
+    row_sum = jnp.sum(shifted, axis=2)
+    row_dots = dots_all.astype(jnp.float32)
+    grad_probs = jnp.einsum(
+        "qhd,khd->hqk", grad_heads, value_heads, preferred_element_type=jnp.float32
+    )
+    local_gs = shifted * (grad_probs - jnp.transpose(row_dots)[:, :, None]) * score_scale
+    local_dq = jnp.einsum(
+        "hqk,khd->qhd",
+        local_gs,
+        key_heads.astype(jnp.float32),
+        precision=lax.Precision.HIGHEST,
+        preferred_element_type=jnp.float32,
+    )
+    row_maxes, row_sums, own_dq = merged_with_dq(row_max, row_sum, local_dq)
     log_total = row_maxes + jnp.log(row_sums)
-    row_dots = dots_all.astype(jnp.float32)
     weights = jnp.exp(scores - log_total[:, :, None])
     prefix_dv = (
         contract_rows(weights.astype(jnp.bfloat16), grad_heads)
@@ -191,8 +219,7 @@
     prefix_dk = (
         contract_rows(grad_scores, query_heads).reshape(tokens, feature_width).astype(jnp.bfloat16)
     )
-    partial_value = contract_cols(grad_scores, key_heads).reshape(latents, feature_width)
-    cross_dq = sum_at_owner(partial_value, SEQ_AXES, 0).astype(jnp.bfloat16)
+    cross_dq = own_dq.reshape(own_rows, feature_width).astype(jnp.bfloat16)
     everything = jnp.transpose(self_all.reshape(latents, 4, HEAD_DIM), (1, 0, 2))
     all_rows = everything.shape[1]
     query_every = everything[0].reshape(all_rows, 1, HEAD_DIM)

time: 197 us -> 166 us (0.84)
  blocking collectives: 70.2 us -> 34.9 us
  waiting for transfers between devices: 70.1 us -> 60.4 us
  local copies, waits for them, and re-layouts: 7.01 us -> 13.5 us
  starting transfers between devices: 27.8 us -> 31.7 us
    all_gather x4 -> x0, blocking collectives: 39 us -> none  [merged_seq(): both = lax.all_gather(jnp.stack([row_max, row_sum]), axis)]
    all_to_all x1 -> x3, waiting for transfers between devices: 33.7 us -> 24 us  [merged_with_dq(): got = lax.all_to_all(send, axis, 0, 0, tiled=True)]
    all_to_all x1 -> x3, starting transfers between devices: 15.2 us -> 19.1 us  [merged_with_dq(): got = lax.all_to_all(send, axis, 0, 0, tiled=True)]
    all_to_all x0 -> x1, blocking collectives: none -> 3.75 us  [merged_with_dq(): got = lax.all_to_all(send, axis, 0, 0, tiled=True)]
    all_to_all x0 -> x4, local copies, waits for them, and re-layouts: none -> 2.83 us  [merged_with_dq(): got = lax.all_to_all(send, axis, 0, 0, tiled=True)]
  transfers between devices with their start and end apart: 3 -> 5, of which waited for: 3 -> 5; matrix products, arithmetic and copies ran while one was open for 2% -> 3% of each run, Pallas kernels for 0% -> 0%
where the time goes in v5:
time: 166 us; the launch traced here: 165 us
  waiting for transfers between devices  60.4 us (36%)
  blocking collectives  34.9 us (21%)
  starting transfers between devices  31.7 us (19%)
  between operations  15.3 us (9%)
  local copies, waits for them, and re-layouts  13.5 us (8%)
  other arithmetic  4.68 us (3%)
  matrix products  4 us (2%)
    all_gather x1, waiting for transfers between devices, gather_seq(): x = lax.all_gather(x, axis, axis=0, tiled=False)  28.3 us
    all_to_all x3, waiting for transfers between devices, merged_with_dq(): got = lax.all_to_all(send, axis, 0, 0, tiled=True)  24 us
    all_to_all x3, starting transfers between devices, merged_with_dq(): got = lax.all_to_all(send, axis, 0, 0, tiled=True)  19.1 us
    all_gather x2, blocking collectives, shards(): first = lax.all_gather(first, axis, axis=0)  15.9 us
    all_gather x1, blocking collectives, gather_seq(): x = lax.all_gather(x, axis, axis=0, tiled=False)  13.4 us
    all_to_all x1, starting transfers between devices, shards(): lax.all_to_all(jnp.transpose(stacked, (1, 0, 2)), 'zl', split_axis=0, con...  12.6 us
    all_to_all x1, waiting for transfers between devices, shards(): lax.all_to_all(jnp.transpose(stacked, (1, 0, 2)), 'zl', split_axis=0, con...  8.11 us
    all_to_all x1, blocking collectives, merged_with_dq(): got = lax.all_to_all(send, axis, 0, 0, tiled=True)  3.75 us
  transfers between devices with their start and end apart: 5, of which 5 were waited for; matrix products, arithmetic and copies ran while one was open for 3% of the time, Pallas kernels for 0%

profile of v5, /device:TPU:32, one launch (start us, length us, event | category | flops | bytes accessed | tf_op | source)
XLA Modules:
  0.0 164.5 jit_solution(14197491208551475739)
XLA Ops:
  7.2 1.4 maximum_bitcast_fusion.1
  8.6 12.6 %all-to-all-start = ((bf16[8,4,256]{2,1,0:T(4,128)(2,1)}), bf16[8,4,256]{2,1,0:T(4,128)(2,1)S(1)}, u32[]{:S(2)}, u32[]{:S(2)}) async-start(bf16[8,4,256]{2,1,0:T(4,128)(2,1)} %maximum_bitcast_fusion.1), calls=%async_computation | async-start | bytes 32768 | tf_op jit(solution)/shard_map/all_to_all | solution.py:166
  21.2 0.8 bitcast_reduce_fusion.4
  22.1 8.1 %all-to-all-done = bf16[8,4,256]{2,1,0:T(4,128)(2,1)S(1)} async-done(((bf16[8,4,256]{2,1,0:T(4,128)(2,1)}), bf16[8,4,256]{2,1,0:T(4,128)(2,1)S(1)}, u32[]{:S(2)}, u32[]{:S(2)}) %all-to-all-start) | async-done | bytes 16416 | tf_op jit(solution)/shard_map/all_to_all | solution.py:166
  30.3 0.8 concatenate.29
  31.0 14.1 %all-gather = bf16[16,1538]{1,0:T(8,128)(2,1)S(1)} all-gather(bf16[8,1538]{1,0:T(8,128)(2,1)S(1)} %concatenate.29), channel_id=2, replica_groups=mesh['y'=4,'zh'=2,'x'=4,'c'=2,'zl'=8] {'zh'}, dimensions={0}, use_global_device_ids=true | all-gather | bytes 73824 | tf_op jit(solution)/shard_map/all_gather | solution.py:175
  45.1 1.9 %all-gather.1 = bf16[4,8,1538]{2,1,0:T(8,128)(2,1)S(1)} all-gather(bf16[2,8,1538]{2,1,0:T(8,128)(2,1)S(1)} %bitcast.251), channel_id=3, replica_groups=mesh['y'=4,'zh'=2,'x'=4,'c'=2,'zl'=8] {'c'}, dimensions={0}, use_global_device_ids=true | all-gather | bytes 147648 | tf_op jit(solution)/shard_map/all_gather | solution.py:175
  47.2 13.4 %all-gather.2 = bf16[8,2,8,1026]{3,2,1,0:T(8,128)(2,1)} all-gather(bf16[2,2,8,1026]{3,2,1,0:T(8,128)(2,1)S(1)} %pad_maximum_fusion.2), channel_id=4, replica_groups=mesh['y'=4,'zh'=2,'x'=4,'c'=2,'zl'=8] {'x'}, dimensions={0}, use_global_device_ids=true | all-gather | bytes 328320 | tf_op jit(solution)/shard_map/all_gather | solution.py:114
  61.3 28.3 %all-gather.6.cloned.1.call-done = bf16[16,2,2,8,1026]{4,3,2,1,0:T(8,128)(2,1)} async-done(((bf16[4,2,2,8,1026]{4,3,2,1,0:T(8,128)(2,1)}), bf16[16,2,2,8,1026]{4,3,2,1,0:T(8,128)(2,1)}) %all-gather.6.cloned.1.call-update) | async-done | bytes 1050640 | tf_op jit(solution)/shard_map/all_gather | solution.py:114
  89.6 1.4 copy.65
  94.7 1.4 copy.77
  96.1 3.6 %all-to-all-start.1 = ((f32[4,1,34816]{2,1,0:T(1,128)}), f32[4,1,34816]{2,1,0:T(1,128)S(1)}, u32[]{:S(2)}, u32[]{:S(2)}) async-start(f32[4,1,34816]{2,1,0:T(1,128)} %copy.77), calls=%async_computation.1 | async-start | bytes 1114112 | tf_op jit(solution)/shard_map/all_to_all | solution.py:131
  101.2 0.8 copy-done.2
  102.3 6.4 %all-to-all-done.1 = f32[4,1,34816]{2,1,0:T(1,128)S(1)} async-done(((f32[4,1,34816]{2,1,0:T(1,128)}), f32[4,1,34816]{2,1,0:T(1,128)S(1)}, u32[]{:S(2)}, u32[]{:S(2)}) %all-to-all-start.1) | async-done | bytes 557088 | tf_op jit(solution)/shard_map/all_to_all | solution.py:131
  110.9 0.8 all_to_all.39
  111.7 11.3 %all-to-all-start.2 = ((f32[2,1,18432]{2,1,0:T(1,128)}), f32[2,1,18432]{2,1,0:T(1,128)S(1)}, u32[]{:S(2)}, u32[]{:S(2)}) async-start(f32[2,1,18432]{2,1,0:T(1,128)} %all_to_all.39), calls=%async_computation.2 | async-start | bytes 294912 | tf_op jit(solution)/shard_map/all_to_all | solution.py:131
  122.9 1.0 fusion.8
  124.0 1.8 %all_gather.35 = bf16[2,3,16,128]{3,2,1,0:T(8,128)(2,1)S(1)} all-gather(bf16[1,3,16,128]{3,2,1,0:T(8,128)(2,1)S(1)} %pad_maximum_fusion.4), channel_id=1, replica_groups=mesh['y'=4,'zh'=2,'x'=4,'c'=2,'zl'=8] {'c'}, dimensions={0}, use_global_device_ids=true | all-gather | bytes 36864 | tf_op jit(solution)/shard_map/all_gather | solution.py:252
  125.8 12.4 %all-to-all-done.2 = f32[2,1,18432]{2,1,0:T(1,128)S(1)} async-done(((f32[2,1,18432]{2,1,0:T(1,128)}), f32[2,1,18432]{2,1,0:T(1,128)S(1)}, u32[]{:S(2)}, u32[]{:S(2)}) %all-to-all-start.2) | async-done | bytes 147488 | tf_op jit(solution)/shard_map/all_to_all | solution.py:131
  140.0 4.2 %all-to-all-start.3 = ((f32[4,1,6144]{2,1,0:T(1,128)}), f32[4,1,6144]{2,1,0:T(1,128)S(1)}, u32[]{:S(2)}, u32[]{:S(2)}) async-start(f32[4,1,6144]{2,1,0:T(1,128)} %all_to_all.42), calls=%async_computation.3 | async-start | bytes 196608 | tf_op jit(solution)/shard_map/all_to_all | solution.py:131
  144.8 5.2 %all-to-all-done.3 = f32[4,1,6144]{2,1,0:T(1,128)S(1)} async-done(((f32[4,1,6144]{2,1,0:T(1,128)}), f32[4,1,6144]{2,1,0:T(1,128)S(1)}, u32[]{:S(2)}, u32[]{:S(2)}) %all-to-all-start.3) | async-done | bytes 98336 | tf_op jit(solution)/shard_map/all_to_all | solution.py:131
  150.7 3.7 %all_to_all.53 = f32[2,1,4096]{2,1,0:T(1,128)S(1)} all-to-all(f32[2,1,4096]{2,1,0:T(1,128)S(1)} %all_to_all.45), channel_id=1, replica_groups=mesh['y'=4,'zh'=2,'x'=4,'c'=2,'zl'=8] {'c'}, dimensions={0} | all-to-all | bytes 65536 | tf_op jit(solution)/shard_map/all_to_all | solution.py:131
  155.3 0.7 copy.91
  156.0 0.7 copy.90
  (108 shorter events, 12.4 us)
Async XLA Ops:
  7.2 84.8 %copy-start = (bf16[128,256]{1,0:T(8,128)(2,1)S(1)}, bf16[128,256]{1,0:T(8,128)(2,1)}, u32[]{:S(2)}) copy-start(bf16[128,256]{1,0:T(8,128)(2,1)} %param.13) | copy-start | bytes 196612
  8.6 21.6 %all-to-all-start = ((bf16[8,4,256]{2,1,0:T(4,128)(2,1)}), bf16[8,4,256]{2,1,0:T(4,128)(2,1)S(1)}, u32[]{:S(2)}, u32[]{:S(2)}) async-start(bf16[8,4,256]{2,1,0:T(4,128)(2,1)} %maximum_bitcast_fusion.1), calls=%async_computation | async-start | bytes 32768 | tf_op jit(solution)/shard_map/all_to_all | solution.py:166
  21.2 68.4 %all-gather.6.cloned.1.call-start = ((), (), s32[]{:S(2)}) async-start(), calls=%async_computation.5 | async-start | bytes 1474560 | tf_op jit(solution)/shard_map/all_gather | solution.py:114
  91.8 9.4 %copy-start.1 = (bf16[512,512]{0,1:T(8,128)(2,1)}, bf16[512,512]{0,1:T(8,128)(2,1)S(1)}, u32[]{:S(2)}) copy-start(bf16[512,512]{0,1:T(8,128)(2,1)S(1)} %copy.88) | copy-start | bytes 1572868
  91.8 0.9 copy-start.3
  96.1 12.6 %all-to-all-start.1 = ((f32[4,1,34816]{2,1,0:T(1,128)}), f32[4,1,34816]{2,1,0:T(1,128)S(1)}, u32[]{:S(2)}, u32[]{:S(2)}) async-start(f32[4,1,34816]{2,1,0:T(1,128)} %copy.77), calls=%async_computation.1 | async-start | bytes 1114112 | tf_op jit(solution)/shard_map/all_to_all | solution.py:131
  101.2 0.8 copy-start.2
  111.7 26.6 %all-to-all-start.2 = ((f32[2,1,18432]{2,1,0:T(1,128)}), f32[2,1,18432]{2,1,0:T(1,128)S(1)}, u32[]{:S(2)}, u32[]{:S(2)}) async-start(f32[2,1,18432]{2,1,0:T(1,128)} %all_to_all.39), calls=%async_computation.2 | async-start | bytes 294912 | tf_op jit(solution)/shard_map/all_to_all | solution.py:131
  140.0 10.0 %all-to-all-start.3 = ((f32[4,1,6144]{2,1,0:T(1,128)}), f32[4,1,6144]{2,1,0:T(1,128)S(1)}, u32[]{:S(2)}, u32[]{:S(2)}) async-start(f32[4,1,6144]{2,1,0:T(1,128)} %all_to_all.42), calls=%async_computation.3 | async-start | bytes 196608 | tf_op jit(solution)/shard_map/all_to_all | solution.py:131
Sparse Core Ops, SparseCore 0:
  60.7 28.8 all-gather.5

commit v6 on v5

--- a/solution.py
+++ b/solution.py
@@ -111,7 +111,7 @@
 
 def gather_seq(x, axes):
     for axis in axes:
-        x = lax.all_gather(x, axis, axis=0, tiled=False)
+        x = from_everyone(x, axis)
     order = [GATHER_ORDER[::-1].index(axis) for axis in SEQ_AXES]
     x = jnp.transpose(x, (*order, *range(4, x.ndim)))
     return x.reshape(-1, *x.shape[5:])
@@ -172,7 +172,7 @@
     cross_width = cross_cols.shape[1]
     first = jnp.concatenate((cross_cols, self_cols), axis=1)
     for axis in GATHER_ORDER[:2]:
-        first = lax.all_gather(first, axis, axis=0)
+        first = from_everyone(first, axis)
     core = lax.axis_index("c")
     self_heads = first[..., cross_width:].reshape(*first.shape[:-1], 4, local_heads, HEAD_DIM)
     self_mine = lax.dynamic_index_in_dim(self_heads, core, axis=4, keepdims=False)

time: 166 us -> 141 us (0.85)
  blocking collectives: 34.9 us -> 20.8 us
  between operations: 15.3 us -> 1.91 us
  starting transfers between devices: 31.7 us -> 34.9 us
    all_gather x3 -> x0, blocking collectives: 29.4 us -> none  [the longest x2 15.9 us: shards(): first = lax.all_gather(first, axis, axis=0)]
    all_to_all x0 -> x2, waiting for transfers between devices: none -> 28.6 us  [from_everyone(): return lax.all_to_all(copies, axis, split_axis=0, concat_axis=0, tiled=True)]
    all_gather x1 -> x0, waiting for transfers between devices: 28.3 us -> none  [gather_seq(): x = lax.all_gather(x, axis, axis=0, tiled=False)]
    all_to_all x0 -> x2, blocking collectives: none -> 15.2 us  [from_everyone(): return lax.all_to_all(copies, axis, split_axis=0, concat_axis=0, tiled=True)]
    all_to_all x0 -> x2, starting transfers between devices: none -> 12 us  [from_everyone(): return lax.all_to_all(copies, axis, split_axis=0, concat_axis=0, tiled=True)]
    all_to_all x3, starting transfers between devices: 19.1 us -> 10.2 us  [merged_with_dq(): got = lax.all_to_all(send, axis, 0, 0, tiled=True)]
    broadcast_in_dim x0 -> x4, local copies, waits for them, and re-layouts: none -> 1.75 us  [from_everyone(): copies = jnp.broadcast_to(x, (lax.axis_size(axis), *x.shape))]
  transfers between devices with their start and end apart: 5 -> 6, of which waited for: 5 -> 6; matrix products, arithmetic and copies ran while one was open for 3% -> 3% of each run, Pallas kernels for 0% -> 0%
where the time goes in v6:
time: 141 us; the launch traced here: 140 us
  waiting for transfers between devices  59.6 us (42%)
  starting transfers between devices  34.9 us (25%)
  blocking collectives  20.8 us (15%)
  local copies, waits for them, and re-layouts  14 us (10%)
  other arithmetic  4.67 us (3%)
  matrix products  4.01 us (3%)
  between operations  1.91 us (1%)
    all_to_all x2, waiting for transfers between devices, from_everyone(): return lax.all_to_all(copies, axis, split_axis=0, concat_axis=0, tiled=True)  28.6 us
    all_to_all x3, waiting for transfers between devices, merged_with_dq(): got = lax.all_to_all(send, axis, 0, 0, tiled=True)  22.9 us
    all_to_all x2, blocking collectives, from_everyone(): return lax.all_to_all(copies, axis, split_axis=0, concat_axis=0, tiled=True)  15.2 us
    all_to_all x1, starting transfers between devices, shards(): lax.all_to_all(jnp.transpose(stacked, (1, 0, 2)), 'zl', split_axis=0, con...  12.6 us
    all_to_all x2, starting transfers between devices, from_everyone(): return lax.all_to_all(copies, axis, split_axis=0, concat_axis=0, tiled=True)  12 us
    all_to_all x3, starting transfers between devices, merged_with_dq(): got = lax.all_to_all(send, axis, 0, 0, tiled=True)  10.2 us
    all_to_all x1, waiting for transfers between devices, shards(): lax.all_to_all(jnp.transpose(stacked, (1, 0, 2)), 'zl', split_axis=0, con...  8.11 us
    all_to_all x1, blocking collectives, merged_with_dq(): got = lax.all_to_all(send, axis, 0, 0, tiled=True)  3.75 us
  transfers between devices with their start and end apart: 6, of which 6 were waited for; matrix products, arithmetic and copies ran while one was open for 3% of the time, Pallas kernels for 0%

profile of v6, /device:TPU:32, one launch (start us, length us, event | category | flops | bytes accessed | tf_op | source)
XLA Modules:
  0.0 139.9 jit_solution(8247081155582598899)
XLA Ops:
  0.6 1.4 %maximum_bitcast_fusion.1 = bf16[8,4,256]{2,1,0:T(4,128)(2,1)} fusion(bf16[1,8,256]{2,0,1:T(2,128)(2,1)} %bitcast.258, bf16[1,8,256]{2,0,1:T(2,128)(2,1)} %bitcast.259, bf16[1,8,256]{2,0,1:T(2,128)(2,1)} %bitcast.260, bf16[1,8,256]{2,0,1:T(2,128)(2,1)} %bitcast.261), kind=kLoop, calls=%fused_computation.76 | loop fusion | flops 65536 | bytes 32768 | tf_op jit(solution)/shard_map/transpose | solution.py:167
  2.1 12.6 %all-to-all-start = ((bf16[8,4,256]{2,1,0:T(4,128)(2,1)}), bf16[8,4,256]{2,1,0:T(4,128)(2,1)S(1)}, u32[]{:S(2)}, u32[]{:S(2)}) async-start(bf16[8,4,256]{2,1,0:T(4,128)(2,1)} %maximum_bitcast_fusion.1), calls=%async_computation | async-start | bytes 32768 | tf_op jit(solution)/shard_map/all_to_all | solution.py:166
  14.7 0.8 bitcast_reduce_fusion.4
  15.6 8.1 %all-to-all-done = bf16[8,4,256]{2,1,0:T(4,128)(2,1)S(1)} async-done(((bf16[8,4,256]{2,1,0:T(4,128)(2,1)}), bf16[8,4,256]{2,1,0:T(4,128)(2,1)S(1)}, u32[]{:S(2)}, u32[]{:S(2)}) %all-to-all-start) | async-done | bytes 16416 | tf_op jit(solution)/shard_map/all_to_all | solution.py:166
  23.7 0.8 concatenate.29
  25.1 7.6 %all-to-all-start.1 = ((bf16[2,8,1538]{2,1,0:T(8,128)(2,1)}), bf16[2,8,1538]{2,1,0:T(8,128)(2,1)S(1)}, u32[]{:S(2)}, u32[]{:S(2)}) async-start(bf16[2,8,1538]{2,1,0:T(8,128)(2,1)} %broadcast_in_dim.85), calls=%async_computation.1 | async-start | bytes 106496 | tf_op jit(solution)/shard_map/all_to_all | solution.py:20
  32.7 13.6 %all-to-all-done.1 = bf16[2,8,1538]{2,1,0:T(8,128)(2,1)S(1)} async-done(((bf16[2,8,1538]{2,1,0:T(8,128)(2,1)}), bf16[2,8,1538]{2,1,0:T(8,128)(2,1)S(1)}, u32[]{:S(2)}, u32[]{:S(2)}) %all-to-all-start.1) | async-done | bytes 49248 | tf_op jit(solution)/shard_map/all_to_all | solution.py:20
  46.3 3.8 %all_to_all.73 = bf16[2,2,8,1538]{3,2,1,0:T(8,128)(2,1)S(1)} all-to-all(bf16[2,2,8,1538]{3,2,1,0:T(8,128)(2,1)S(1)} %broadcast_in_dim.86), channel_id=1, replica_groups=mesh['y'=4,'zh'=2,'x'=4,'c'=2,'zl'=8] {'c'}, dimensions={0} | all-to-all | bytes 196864 | tf_op jit(solution)/shard_map/all_to_all | solution.py:20
  50.4 11.4 %all_to_all.74 = bf16[4,2,2,8,1026]{4,3,1,2,0:T(8,128)(2,1)S(1)} all-to-all(bf16[4,2,2,8,1026]{4,3,1,2,0:T(8,128)(2,1)S(1)} %broadcast_in_dim.87), channel_id=1, replica_groups=mesh['y'=4,'zh'=2,'x'=4,'c'=2,'zl'=8] {'x'}, dimensions={0} | all-to-all | bytes 525312 | tf_op jit(solution)/shard_map/all_to_all | solution.py:20
  61.9 1.1 broadcast_in_dim.88
  63.0 4.5 %all-to-all-start.4 = ((bf16[4,4,2,2,8,1026]{5,4,2,1,3,0:T(8,128)(2,1)}), bf16[4,4,2,2,8,1026]{5,4,2,1,3,0:T(8,128)(2,1)S(1)}, u32[]{:S(2)}, u32[]{:S(2)}) async-start(bf16[4,4,2,2,8,1026]{5,4,2,1,3,0:T(8,128)(2,1)} %broadcast_in_dim.88), calls=%async_computation.4 | async-start | bytes 2359296 | tf_op jit(solution)/shard_map/all_to_all | solution.py:20
  68.1 15.0 %all-to-all-done.4 = bf16[4,4,2,2,8,1026]{5,4,2,1,3,0:T(8,128)(2,1)S(1)} async-done(((bf16[4,4,2,2,8,1026]{5,4,2,1,3,0:T(8,128)(2,1)}), bf16[4,4,2,2,8,1026]{5,4,2,1,3,0:T(8,128)(2,1)S(1)}, u32[]{:S(2)}, u32[]{:S(2)}) %all-to-all-start.4) | async-done | bytes 1050656 | tf_op jit(solution)/shard_map/all_to_all | solution.py:20
  86.8 1.4 copy.87
  88.2 3.5 %all-to-all-start.5 = ((f32[4,1,34816]{2,1,0:T(1,128)}), f32[4,1,34816]{2,1,0:T(1,128)S(1)}, u32[]{:S(2)}, u32[]{:S(2)}) async-start(f32[4,1,34816]{2,1,0:T(1,128)} %copy.87), calls=%async_computation.5 | async-start | bytes 1114112 | tf_op jit(solution)/shard_map/all_to_all | solution.py:131
  93.2 0.8 copy-done.2
  94.3 5.6 %all-to-all-done.5 = f32[4,1,34816]{2,1,0:T(1,128)S(1)} async-done(((f32[4,1,34816]{2,1,0:T(1,128)}), f32[4,1,34816]{2,1,0:T(1,128)S(1)}, u32[]{:S(2)}, u32[]{:S(2)}) %all-to-all-start.5) | async-done | bytes 557088 | tf_op jit(solution)/shard_map/all_to_all | solution.py:131
  102.1 0.8 all_to_all.55
  102.9 3.4 %all-to-all-start.6 = ((f32[2,1,18432]{2,1,0:T(1,128)}), f32[2,1,18432]{2,1,0:T(1,128)S(1)}, u32[]{:S(2)}, u32[]{:S(2)}) async-start(f32[2,1,18432]{2,1,0:T(1,128)} %all_to_all.55), calls=%async_computation.6 | async-start | bytes 294912 | tf_op jit(solution)/shard_map/all_to_all | solution.py:131
  106.3 1.0 fusion.8
  107.4 1.8 %all_gather.3 = bf16[2,3,16,128]{3,2,1,0:T(8,128)(2,1)S(1)} all-gather(bf16[1,3,16,128]{3,2,1,0:T(8,128)(2,1)S(1)} %pad_maximum_fusion.4), channel_id=1, replica_groups=mesh['y'=4,'zh'=2,'x'=4,'c'=2,'zl'=8] {'c'}, dimensions={0}, use_global_device_ids=true | all-gather | bytes 36864 | tf_op jit(solution)/shard_map/all_gather | solution.py:252
  109.2 12.1 %all-to-all-done.6 = f32[2,1,18432]{2,1,0:T(1,128)S(1)} async-done(((f32[2,1,18432]{2,1,0:T(1,128)}), f32[2,1,18432]{2,1,0:T(1,128)S(1)}, u32[]{:S(2)}, u32[]{:S(2)}) %all-to-all-start.6) | async-done | bytes 147488 | tf_op jit(solution)/shard_map/all_to_all | solution.py:131
  123.1 3.3 %all-to-all-start.7 = ((f32[4,1,6144]{2,1,0:T(1,128)}), f32[4,1,6144]{2,1,0:T(1,128)S(1)}, u32[]{:S(2)}, u32[]{:S(2)}) async-start(f32[4,1,6144]{2,1,0:T(1,128)} %all_to_all.58), calls=%async_computation.7 | async-start | bytes 196608 | tf_op jit(solution)/shard_map/all_to_all | solution.py:131
  127.0 5.2 %all-to-all-done.7 = f32[4,1,6144]{2,1,0:T(1,128)S(1)} async-done(((f32[4,1,6144]{2,1,0:T(1,128)}), f32[4,1,6144]{2,1,0:T(1,128)S(1)}, u32[]{:S(2)}, u32[]{:S(2)}) %all-to-all-start.7) | async-done | bytes 98336 | tf_op jit(solution)/shard_map/all_to_all | solution.py:131
  132.9 3.7 %all_to_all.75 = f32[2,1,4096]{2,1,0:T(1,128)S(1)} all-to-all(f32[2,1,4096]{2,1,0:T(1,128)S(1)} %all_to_all.61), channel_id=1, replica_groups=mesh['y'=4,'zh'=2,'x'=4,'c'=2,'zl'=8] {'c'}, dimensions={0} | all-to-all | bytes 65536 | tf_op jit(solution)/shard_map/all_to_all | solution.py:131
  (113 shorter events, 14.6 us)
Async XLA Ops:
  0.6 83.5 %copy-start = (bf16[128,256]{1,0:T(8,128)(2,1)S(1)}, bf16[128,256]{1,0:T(8,128)(2,1)}, u32[]{:S(2)}) copy-start(bf16[128,256]{1,0:T(8,128)(2,1)} %param.13) | copy-start | bytes 196612
  2.1 21.6 %all-to-all-start = ((bf16[8,4,256]{2,1,0:T(4,128)(2,1)}), bf16[8,4,256]{2,1,0:T(4,128)(2,1)S(1)}, u32[]{:S(2)}, u32[]{:S(2)}) async-start(bf16[8,4,256]{2,1,0:T(4,128)(2,1)} %maximum_bitcast_fusion.1), calls=%async_computation | async-start | bytes 32768 | tf_op jit(solution)/shard_map/all_to_all | solution.py:166
  25.1 21.2 %all-to-all-start.1 = ((bf16[2,8,1538]{2,1,0:T(8,128)(2,1)}), bf16[2,8,1538]{2,1,0:T(8,128)(2,1)S(1)}, u32[]{:S(2)}, u32[]{:S(2)}) async-start(bf16[2,8,1538]{2,1,0:T(8,128)(2,1)} %broadcast_in_dim.85), calls=%async_computation.1 | async-start | bytes 106496 | tf_op jit(solution)/shard_map/all_to_all | solution.py:20
  63.0 20.1 %all-to-all-start.4 = ((bf16[4,4,2,2,8,1026]{5,4,2,1,3,0:T(8,128)(2,1)}), bf16[4,4,2,2,8,1026]{5,4,2,1,3,0:T(8,128)(2,1)S(1)}, u32[]{:S(2)}, u32[]{:S(2)}) async-start(bf16[4,4,2,2,8,1026]{5,4,2,1,3,0:T(8,128)(2,1)} %broadcast_in_dim.88), calls=%async_computation.4 | async-start | bytes 2359296 | tf_op jit(solution)/shard_map/all_to_all | solution.py:20
  83.9 9.3 %copy-start.1 = (bf16[512,512]{0,1:T(8,128)(2,1)}, bf16[512,512]{0,1:T(8,128)(2,1)S(1)}, u32[]{:S(2)}) copy-start(bf16[512,512]{0,1:T(8,128)(2,1)S(1)} %copy.98) | copy-start | bytes 1572868
  83.9 0.9 copy-start.3
  88.2 11.7 %all-to-all-start.5 = ((f32[4,1,34816]{2,1,0:T(1,128)}), f32[4,1,34816]{2,1,0:T(1,128)S(1)}, u32[]{:S(2)}, u32[]{:S(2)}) async-start(f32[4,1,34816]{2,1,0:T(1,128)} %copy.87), calls=%async_computation.5 | async-start | bytes 1114112 | tf_op jit(solution)/shard_map/all_to_all | solution.py:131
  93.2 0.8 copy-start.2
  102.9 18.5 %all-to-all-start.6 = ((f32[2,1,18432]{2,1,0:T(1,128)}), f32[2,1,18432]{2,1,0:T(1,128)S(1)}, u32[]{:S(2)}, u32[]{:S(2)}) async-start(f32[2,1,18432]{2,1,0:T(1,128)} %all_to_all.55), calls=%async_computation.6 | async-start | bytes 294912 | tf_op jit(solution)/shard_map/all_to_all | solution.py:131
  123.1 9.1 %all-to-all-start.7 = ((f32[4,1,6144]{2,1,0:T(1,128)}), f32[4,1,6144]{2,1,0:T(1,128)S(1)}, u32[]{:S(2)}, u32[]{:S(2)}) async-start(f32[4,1,6144]{2,1,0:T(1,128)} %all_to_all.58), calls=%async_computation.7 | async-start | bytes 196608 | tf_op jit(solution)/shard_map/all_to_all | solution.py:131

commit v7 on v6

--- a/solution.py
+++ b/solution.py
@@ -162,17 +162,29 @@
     out_own = cross_out.reshape(own_rows, local_heads, HEAD_DIM).astype(jnp.float32)
     row_dot = jnp.sum(grad_own * out_own, axis=2).astype(jnp.bfloat16)
     head_groups = lax.axis_size("zl")
+    far_pairs = lax.axis_size("zh")
     stacked = jnp.stack([self_q, self_k, self_v, self_grad]).reshape(4, head_groups, feature_width)
-    regrouped = lax.all_to_all(
-        jnp.transpose(stacked, (1, 0, 2)), "zl", split_axis=0, concat_axis=0, tiled=True
-    )
-    block_rows = regrouped.shape[0]
-    self_cols = regrouped.reshape(block_rows, -1)
+    self_chunks = jnp.transpose(stacked, (1, 0, 2)).reshape(head_groups, -1)
     cross_cols = jnp.concatenate((cross_q, cross_grad, row_dot), axis=1)
     cross_width = cross_cols.shape[1]
-    first = jnp.concatenate((cross_cols, self_cols), axis=1)
-    for axis in GATHER_ORDER[:2]:
-        first = from_everyone(first, axis)
+    self_width = self_chunks.shape[1]
+    outgoing = jnp.concatenate(
+        (
+            self_chunks,
+            jnp.broadcast_to(cross_cols.reshape(1, -1), (head_groups, cross_cols.size)),
+        ),
+        axis=1,
+    )
+    outgoing = jnp.broadcast_to(outgoing[None], (far_pairs, *outgoing.shape))
+    incoming = lax.all_to_all(
+        outgoing.reshape(far_pairs * head_groups, -1), ("zh", "zl"), 0, 0, tiled=True
+    ).reshape(far_pairs, head_groups, -1)
+    block_rows = head_groups
+    self_cols = incoming[:, :, :self_width]
+    far_cross = lax.dynamic_index_in_dim(incoming, lax.axis_index("zl"), 1, keepdims=False)
+    far_cross = far_cross[:, self_width:].reshape(far_pairs, own_rows, cross_width)
+    first = jnp.concatenate((far_cross, self_cols), axis=2)
+    first = from_everyone(first, "c")
     core = lax.axis_index("c")
     self_heads = first[..., cross_width:].reshape(*first.shape[:-1], 4, local_heads, HEAD_DIM)
     self_mine = lax.dynamic_index_in_dim(self_heads, core, axis=4, keepdims=False)

time: 141 us -> 133 us (0.943)
  the two profiles are of different devices: /device:TPU:32 before, /device:TPU:1 now
where the time goes in v7:
time: 133 us; the launch traced here: 132 us
  waiting for transfers between devices  41.5 us (31%)
  blocking collectives  33.7 us (25%)
  starting transfers between devices  30.8 us (23%)
  local copies, waits for them, and re-layouts  14.5 us (11%)
  other arithmetic  5.6 us (4%)
  matrix products  4 us (3%)
  between operations  1.99 us (1%)
    all_to_all x2, blocking collectives, from_everyone(): return lax.all_to_all(copies, axis, split_axis=0, concat_axis=0, tiled=True)  18.2 us
    all_to_all x1, starting transfers between devices, shards(): lax.all_to_all(outgoing.reshape(far_pairs * head_groups, -1), ('zh', 'zl'...  15.7 us
    all_to_all x3, waiting for transfers between devices, merged_with_dq(): got = lax.all_to_all(send, axis, 0, 0, tiled=True)  15.1 us
    all_to_all x1, waiting for transfers between devices, from_everyone(): return lax.all_to_all(copies, axis, split_axis=0, concat_axis=0, tiled=True)  14.1 us
    all_to_all x1, waiting for transfers between devices, shards(): lax.all_to_all(outgoing.reshape(far_pairs * head_groups, -1), ('zh', 'zl'...  12.2 us
    all_to_all x3, starting transfers between devices, merged_with_dq(): got = lax.all_to_all(send, axis, 0, 0, tiled=True)  10.9 us
    all_to_all x1, blocking collectives, merged_with_dq(): got = lax.all_to_all(send, axis, 0, 0, tiled=True)  9.82 us
    all_gather x1, blocking collectives, shards(): lax.all_gather(head_results.reshape(3, chip_rows, HEAD_DIM), 'c', axis=0)  5.61 us
  transfers between devices with their start and end apart: 5, of which 5 were waited for; matrix products, arithmetic and copies ran while one was open for 3% of the time, Pallas kernels for 0%

profile of v7, /device:TPU:1, one launch (start us, length us, event | category | flops | bytes accessed | tf_op | source)
XLA Modules:
  0.0 132.0 jit_solution(4371953051957074478)
XLA Ops:
  0.6 0.8 bitcast_reduce_fusion.4
  2.4 0.8 maximum_bitcast_fusion.1
  4.5 0.9 reshape.353
  5.4 15.7 %all-to-all-start = ((bf16[16,2,2568]{2,1,0:T(2,128)(2,1)}), bf16[16,2,2568]{2,1,0:T(2,128)(2,1)S(1)}, u32[]{:S(2)}, u32[]{:S(2)}) async-start(bf16[16,2,2568]{2,1,0:T(2,128)(2,1)} %reshape.353), calls=%async_computation | async-start | bytes 344064 | tf_op jit(solution)/shard_map/all_to_all | solution.py:179
  21.1 12.2 %all-to-all-done = bf16[16,2,2568]{2,1,0:T(2,128)(2,1)S(1)} async-done(((bf16[16,2,2568]{2,1,0:T(2,128)(2,1)}), bf16[16,2,2568]{2,1,0:T(2,128)(2,1)S(1)}, u32[]{:S(2)}, u32[]{:S(2)}) %all-to-all-start) | async-done | bytes 164384 | tf_op jit(solution)/shard_map/all_to_all | solution.py:179
  34.0 7.9 %all_to_all.72 = bf16[2,2,8,1538]{3,2,1,0:T(8,128)(2,1)S(1)} all-to-all(bf16[2,2,8,1538]{3,2,1,0:T(8,128)(2,1)S(1)} %broadcast_in_dim.98), channel_id=1, replica_groups=mesh['y'=4,'zh'=2,'x'=4,'c'=2,'zl'=8] {'c'}, dimensions={0} | all-to-all | bytes 196864 | tf_op jit(solution)/shard_map/all_to_all | solution.py:20
  42.2 10.3 %all_to_all.73 = bf16[4,2,2,8,1026]{4,3,1,2,0:T(8,128)(2,1)S(1)} all-to-all(bf16[4,2,2,8,1026]{4,3,1,2,0:T(8,128)(2,1)S(1)} %broadcast_in_dim.99), channel_id=1, replica_groups=mesh['y'=4,'zh'=2,'x'=4,'c'=2,'zl'=8] {'x'}, dimensions={0} | all-to-all | bytes 525312 | tf_op jit(solution)/shard_map/all_to_all | solution.py:20
  52.5 1.1 broadcast_in_dim.100
  53.6 4.2 %all-to-all-start.3 = ((bf16[4,4,2,2,8,1026]{5,4,2,1,3,0:T(8,128)(2,1)}), bf16[4,4,2,2,8,1026]{5,4,2,1,3,0:T(8,128)(2,1)S(1)}, u32[]{:S(2)}, u32[]{:S(2)}) async-start(bf16[4,4,2,2,8,1026]{5,4,2,1,3,0:T(8,128)(2,1)} %broadcast_in_dim.100), calls=%async_computation.3 | async-start | bytes 2359296 | tf_op jit(solution)/shard_map/all_to_all | solution.py:20
  58.4 14.1 %all-to-all-done.3 = bf16[4,4,2,2,8,1026]{5,4,2,1,3,0:T(8,128)(2,1)S(1)} async-done(((bf16[4,4,2,2,8,1026]{5,4,2,1,3,0:T(8,128)(2,1)}), bf16[4,4,2,2,8,1026]{5,4,2,1,3,0:T(8,128)(2,1)S(1)}, u32[]{:S(2)}, u32[]{:S(2)}) %all-to-all-start.3) | async-done | bytes 1050656 | tf_op jit(solution)/shard_map/all_to_all | solution.py:20
  76.2 1.4 %copy.86 = f32[4,1,34816]{2,1,0:T(1,128)} copy(f32[4,1,34816]{2,0,1:T(4,128)S(1)} %maximum_bitcast_fusion) | data formatting | bytes 1114112 | tf_op jit(solution)/shard_map/all_to_all | solution.py:131
  77.6 3.5 %all-to-all-start.4 = ((f32[4,1,34816]{2,1,0:T(1,128)}), f32[4,1,34816]{2,1,0:T(1,128)S(1)}, u32[]{:S(2)}, u32[]{:S(2)}) async-start(f32[4,1,34816]{2,1,0:T(1,128)} %copy.86), calls=%async_computation.4 | async-start | bytes 1114112 | tf_op jit(solution)/shard_map/all_to_all | solution.py:131
  82.7 0.8 copy-done.2
  83.7 4.5 %all-to-all-done.4 = f32[4,1,34816]{2,1,0:T(1,128)S(1)} async-done(((f32[4,1,34816]{2,1,0:T(1,128)}), f32[4,1,34816]{2,1,0:T(1,128)S(1)}, u32[]{:S(2)}, u32[]{:S(2)}) %all-to-all-start.4) | async-done | bytes 557088 | tf_op jit(solution)/shard_map/all_to_all | solution.py:131
  90.4 0.8 all_to_all.55
  91.2 4.1 %all-to-all-start.5 = ((f32[2,1,18432]{2,1,0:T(1,128)}), f32[2,1,18432]{2,1,0:T(1,128)S(1)}, u32[]{:S(2)}, u32[]{:S(2)}) async-start(f32[2,1,18432]{2,1,0:T(1,128)} %all_to_all.55), calls=%async_computation.5 | async-start | bytes 294912 | tf_op jit(solution)/shard_map/all_to_all | solution.py:131
  95.3 1.0 fusion.8
  96.3 5.6 %all_gather.3 = bf16[2,3,16,128]{3,2,1,0:T(8,128)(2,1)S(1)} all-gather(bf16[1,3,16,128]{3,2,1,0:T(8,128)(2,1)S(1)} %pad_maximum_fusion.6), channel_id=1, replica_groups=mesh['y'=4,'zh'=2,'x'=4,'c'=2,'zl'=8] {'c'}, dimensions={0}, use_global_device_ids=true | all-gather | bytes 36864 | tf_op jit(solution)/shard_map/all_gather | solution.py:264
  102.0 6.7 %all-to-all-done.5 = f32[2,1,18432]{2,1,0:T(1,128)S(1)} async-done(((f32[2,1,18432]{2,1,0:T(1,128)}), f32[2,1,18432]{2,1,0:T(1,128)S(1)}, u32[]{:S(2)}, u32[]{:S(2)}) %all-to-all-start.5) | async-done | bytes 147488 | tf_op jit(solution)/shard_map/all_to_all | solution.py:131
  110.3 3.3 %all-to-all-start.6 = ((f32[4,1,6144]{2,1,0:T(1,128)}), f32[4,1,6144]{2,1,0:T(1,128)S(1)}, u32[]{:S(2)}, u32[]{:S(2)}) async-start(f32[4,1,6144]{2,1,0:T(1,128)} %all_to_all.58), calls=%async_computation.6 | async-start | bytes 196608 | tf_op jit(solution)/shard_map/all_to_all | solution.py:131
  114.3 4.0 %all-to-all-done.6 = f32[4,1,6144]{2,1,0:T(1,128)S(1)} async-done(((f32[4,1,6144]{2,1,0:T(1,128)}), f32[4,1,6144]{2,1,0:T(1,128)S(1)}, u32[]{:S(2)}, u32[]{:S(2)}) %all-to-all-start.6) | async-done | bytes 98336 | tf_op jit(solution)/shard_map/all_to_all | solution.py:131
  119.0 9.8 %all_to_all.74 = f32[2,1,4096]{2,1,0:T(1,128)S(1)} all-to-all(f32[2,1,4096]{2,1,0:T(1,128)S(1)} %all_to_all.61), channel_id=1, replica_groups=mesh['y'=4,'zh'=2,'x'=4,'c'=2,'zl'=8] {'c'}, dimensions={0} | all-to-all | bytes 65536 | tf_op jit(solution)/shard_map/all_to_all | solution.py:131
  129.6 0.7 copy.100
  130.4 0.7 copy.99
  (125 shorter events, 15.1 us)
Async XLA Ops:
  0.6 72.9 %copy-start = (bf16[128,256]{1,0:T(8,128)(2,1)S(1)}, bf16[128,256]{1,0:T(8,128)(2,1)}, u32[]{:S(2)}) copy-start(bf16[128,256]{1,0:T(8,128)(2,1)} %param.13) | copy-start | bytes 196612
  5.4 28.0 %all-to-all-start = ((bf16[16,2,2568]{2,1,0:T(2,128)(2,1)}), bf16[16,2,2568]{2,1,0:T(2,128)(2,1)S(1)}, u32[]{:S(2)}, u32[]{:S(2)}) async-start(bf16[16,2,2568]{2,1,0:T(2,128)(2,1)} %reshape.353), calls=%async_computation | async-start | bytes 344064 | tf_op jit(solution)/shard_map/all_to_all | solution.py:179
  53.6 18.9 %all-to-all-start.3 = ((bf16[4,4,2,2,8,1026]{5,4,2,1,3,0:T(8,128)(2,1)}), bf16[4,4,2,2,8,1026]{5,4,2,1,3,0:T(8,128)(2,1)S(1)}, u32[]{:S(2)}, u32[]{:S(2)}) async-start(bf16[4,4,2,2,8,1026]{5,4,2,1,3,0:T(8,128)(2,1)} %broadcast_in_dim.100), calls=%async_computation.3 | async-start | bytes 2359296 | tf_op jit(solution)/shard_map/all_to_all | solution.py:20
  73.3 9.3 %copy-start.1 = (bf16[512,512]{0,1:T(8,128)(2,1)}, bf16[512,512]{0,1:T(8,128)(2,1)S(1)}, u32[]{:S(2)}) copy-start(bf16[512,512]{0,1:T(8,128)(2,1)S(1)} %copy.97) | copy-start | bytes 1572868
  73.4 0.9 copy-start.3
  77.6 10.6 %all-to-all-start.4 = ((f32[4,1,34816]{2,1,0:T(1,128)}), f32[4,1,34816]{2,1,0:T(1,128)S(1)}, u32[]{:S(2)}, u32[]{:S(2)}) async-start(f32[4,1,34816]{2,1,0:T(1,128)} %copy.86), calls=%async_computation.4 | async-start | bytes 1114112 | tf_op jit(solution)/shard_map/all_to_all | solution.py:131
  82.6 0.8 copy-start.2
  91.2 17.4 %all-to-all-start.5 = ((f32[2,1,18432]{2,1,0:T(1,128)}), f32[2,1,18432]{2,1,0:T(1,128)S(1)}, u32[]{:S(2)}, u32[]{:S(2)}) async-start(f32[2,1,18432]{2,1,0:T(1,128)} %all_to_all.55), calls=%async_computation.5 | async-start | bytes 294912 | tf_op jit(solution)/shard_map/all_to_all | solution.py:131
  110.3 7.9 %all-to-all-start.6 = ((f32[4,1,6144]{2,1,0:T(1,128)}), f32[4,1,6144]{2,1,0:T(1,128)S(1)}, u32[]{:S(2)}, u32[]{:S(2)}) async-start(f32[4,1,6144]{2,1,0:T(1,128)} %all_to_all.58), calls=%async_computation.6 | async-start | bytes 196608 | tf_op jit(solution)/shard_map/all_to_all | solution.py:131

commit v8 on v7

--- a/solution.py
+++ b/solution.py
@@ -117,28 +117,45 @@
     return x.reshape(-1, *x.shape[5:])
 
 
+MERGE_ORDER = ("c", "y", "x", "zh")
+
+
+def pick_own(values, digits, at):
+    for axis in digits:
+        values = lax.dynamic_index_in_dim(
+            values, lax.axis_index(axis), at + SEQ_AXES.index(axis) - digits.index(axis), False
+        )
+    return values
+
+
 def merged_with_dq(row_max, row_sum, partial_dq):
-    rows = partial_dq.shape[0]
-    width = partial_dq[0].size
-    start = 0
-    for axis in SEQ_AXES:
+    sizes = [lax.axis_size(axis) for axis in SEQ_AXES]
+    heads = row_max.shape[0]
+    by_digit = (heads, *sizes, -1)
+    partial_dq = partial_dq.reshape(*sizes, -1, *partial_dq.shape[1:])
+    left = list(SEQ_AXES)
+    done = []
+    for axis in MERGE_ORDER:
         size = lax.axis_size(axis)
-        rows //= size
+        moved = jnp.moveaxis(partial_dq, left.index(axis), 0)
+        left.remove(axis)
+        done.append(axis)
         stats = jnp.stack([row_max, row_sum]).reshape(1, -1)
         send = jnp.concatenate(
-            [partial_dq.reshape(size, -1), jnp.broadcast_to(stats, (size, stats.shape[1]))], axis=1
+            [moved.reshape(size, -1), jnp.broadcast_to(stats, (size, stats.shape[1]))], axis=1
         )
         got = lax.all_to_all(send, axis, 0, 0, tiled=True)
-        got_dq = got[:, : rows * width].reshape(size, rows, *partial_dq.shape[1:])
-        got_stats = got[:, rows * width :].reshape(size, 2, *row_max.shape)
+        got_dq = got[:, : moved[0].size].reshape(moved.shape)
+        got_stats = got[:, moved[0].size :].reshape(size, 2, *row_max.shape)
         top = jnp.max(got_stats[:, 0], axis=0)
         rescale = jnp.exp(got_stats[:, 0] - top)
         row_sum = jnp.sum(got_stats[:, 1] * rescale, axis=0)
         row_max = top
-        start = start + lax.axis_index(axis) * rows
-        dq_rescale = jnp.transpose(lax.dynamic_slice_in_dim(rescale, start, rows, 2), (0, 2, 1))
+        own_done = [d for d in SEQ_AXES if d in done]
+        dq_rescale = pick_own(rescale.reshape(size, *by_digit), own_done, 2)
+        dq_rescale = jnp.moveaxis(dq_rescale, 1, -1)
         partial_dq = jnp.sum(dq_rescale[..., None] * got_dq, axis=0)
-    own_sum = jnp.transpose(lax.dynamic_slice_in_dim(row_sum, start, rows, 1))
+    own_sum = jnp.transpose(pick_own(row_sum.reshape(by_digit), list(SEQ_AXES), 1))
     return row_max, row_sum, partial_dq / own_sum[..., None]
 
 

time: 133 us -> 134 us (level)
  the two profiles are of different devices: /device:TPU:1 before, /device:TPU:32 now
where the time goes in v8:
time: 134 us; the launch traced here: 133 us
  waiting for transfers between devices  51.3 us (38%)
  starting transfers between devices  31 us (23%)
  blocking collectives  21.4 us (16%)
  local copies, waits for them, and re-layouts  17.2 us (13%)
  other arithmetic  6.58 us (5%)
  matrix products  3.1 us (2%)
  between operations  2.09 us (2%)
    all_to_all x3, waiting for transfers between devices, merged_with_dq(): got = lax.all_to_all(send, axis, 0, 0, tiled=True)  21.4 us
    all_to_all x2, blocking collectives, from_everyone(): return lax.all_to_all(copies, axis, split_axis=0, concat_axis=0, tiled=True)  15.2 us
    all_to_all x1, starting transfers between devices, shards(): lax.all_to_all(outgoing.reshape(far_pairs * head_groups, -1), ('zh', 'zl'...  15.2 us
    all_to_all x1, waiting for transfers between devices, from_everyone(): return lax.all_to_all(copies, axis, split_axis=0, concat_axis=0, tiled=True)  15 us
    all_to_all x1, waiting for transfers between devices, shards(): lax.all_to_all(outgoing.reshape(far_pairs * head_groups, -1), ('zh', 'zl'...  14.9 us
    all_to_all x3, starting transfers between devices, merged_with_dq(): got = lax.all_to_all(send, axis, 0, 0, tiled=True)  11.3 us
    all_to_all x1, starting transfers between devices, from_everyone(): return lax.all_to_all(copies, axis, split_axis=0, concat_axis=0, tiled=True)  4.46 us
    all_to_all x1, blocking collectives, merged_with_dq(): got = lax.all_to_all(send, axis, 0, 0, tiled=True)  4.14 us
  transfers between devices with their start and end apart: 5, of which 5 were waited for; matrix products, arithmetic and copies ran while one was open for 2% of the time, Pallas kernels for 0%

profile of v8, /device:TPU:32, one launch (start us, length us, event | category | flops | bytes accessed | tf_op | source)
XLA Modules:
  0.0 132.7 jit_solution(5238137841714654993)
XLA Ops:
  0.6 0.8 bitcast_reduce_fusion
  2.4 0.8 maximum_bitcast_fusion.2
  4.5 0.9 reshape.394
  5.4 15.2 %all-to-all-start = ((bf16[16,2,2568]{2,1,0:T(2,128)(2,1)}), bf16[16,2,2568]{2,1,0:T(2,128)(2,1)S(1)}, u32[]{:S(2)}, u32[]{:S(2)}) async-start(bf16[16,2,2568]{2,1,0:T(2,128)(2,1)} %reshape.394), calls=%async_computation | async-start | bytes 344064 | tf_op jit(solution)/shard_map/all_to_all | solution.py:196
  20.6 14.9 %all-to-all-done = bf16[16,2,2568]{2,1,0:T(2,128)(2,1)S(1)} async-done(((bf16[16,2,2568]{2,1,0:T(2,128)(2,1)}), bf16[16,2,2568]{2,1,0:T(2,128)(2,1)S(1)}, u32[]{:S(2)}, u32[]{:S(2)}) %all-to-all-start) | async-done | bytes 164384 | tf_op jit(solution)/shard_map/all_to_all | solution.py:196
  36.1 3.8 %all_to_all.72 = bf16[2,2,8,1538]{3,2,1,0:T(8,128)(2,1)S(1)} all-to-all(bf16[2,2,8,1538]{3,2,1,0:T(8,128)(2,1)S(1)} %broadcast_in_dim.98), channel_id=1, replica_groups=mesh['y'=4,'zh'=2,'x'=4,'c'=2,'zl'=8] {'c'}, dimensions={0} | all-to-all | bytes 196864 | tf_op jit(solution)/shard_map/all_to_all | solution.py:20
  40.2 11.4 %all_to_all.73 = bf16[4,2,2,8,1026]{4,3,1,2,0:T(8,128)(2,1)S(1)} all-to-all(bf16[4,2,2,8,1026]{4,3,1,2,0:T(8,128)(2,1)S(1)} %broadcast_in_dim.99), channel_id=1, replica_groups=mesh['y'=4,'zh'=2,'x'=4,'c'=2,'zl'=8] {'x'}, dimensions={0} | all-to-all | bytes 525312 | tf_op jit(solution)/shard_map/all_to_all | solution.py:20
  51.6 1.1 broadcast_in_dim.100
  52.7 4.5 %all-to-all-start.3 = ((bf16[4,4,2,2,8,1026]{5,4,2,1,3,0:T(8,128)(2,1)}), bf16[4,4,2,2,8,1026]{5,4,2,1,3,0:T(8,128)(2,1)S(1)}, u32[]{:S(2)}, u32[]{:S(2)}) async-start(bf16[4,4,2,2,8,1026]{5,4,2,1,3,0:T(8,128)(2,1)} %broadcast_in_dim.100), calls=%async_computation.3 | async-start | bytes 2359296 | tf_op jit(solution)/shard_map/all_to_all | solution.py:20
  57.9 15.0 %all-to-all-done.3 = bf16[4,4,2,2,8,1026]{5,4,2,1,3,0:T(8,128)(2,1)S(1)} async-done(((bf16[4,4,2,2,8,1026]{5,4,2,1,3,0:T(8,128)(2,1)}), bf16[4,4,2,2,8,1026]{5,4,2,1,3,0:T(8,128)(2,1)S(1)}, u32[]{:S(2)}, u32[]{:S(2)}) %all-to-all-start.3) | async-done | bytes 1050656 | tf_op jit(solution)/shard_map/all_to_all | solution.py:20
  77.0 4.1 %all_to_all.74 = f32[2,1,67584]{2,1,0:T(1,128)S(1)} all-to-all(f32[2,1,67584]{2,1,0:T(1,128)S(1)} %copy.119), channel_id=1, replica_groups=mesh['y'=4,'zh'=2,'x'=4,'c'=2,'zl'=8] {'c'}, dimensions={0} | all-to-all | bytes 1081344 | tf_op jit(solution)/shard_map/all_to_all | solution.py:147
  81.7 1.0 copy.133
  84.8 1.0 fusion.11
  86.0 0.9 all_to_all.55
  86.9 3.5 %all-to-all-start.5 = ((f32[4,1,18432]{2,1,0:T(1,128)}), f32[4,1,18432]{2,1,0:T(1,128)S(1)}, u32[]{:S(2)}, u32[]{:S(2)}) async-start(f32[4,1,18432]{2,1,0:T(1,128)} %all_to_all.55), calls=%async_computation.5 | async-start | bytes 589824 | tf_op jit(solution)/shard_map/all_to_all | solution.py:147
  92.3 2.0 %all_gather.3 = bf16[2,3,16,128]{3,2,1,0:T(8,128)(2,1)S(1)} all-gather(bf16[1,3,16,128]{3,2,1,0:T(8,128)(2,1)S(1)} %pad_maximum_fusion.5), channel_id=1, replica_groups=mesh['y'=4,'zh'=2,'x'=4,'c'=2,'zl'=8] {'c'}, dimensions={0}, use_global_device_ids=true | all-gather | bytes 36864 | tf_op jit(solution)/shard_map/all_gather | solution.py:281
  94.3 3.6 %all-to-all-done.5 = f32[4,1,18432]{2,1,0:T(1,128)S(1)} async-done(((f32[4,1,18432]{2,1,0:T(1,128)}), f32[4,1,18432]{2,1,0:T(1,128)S(1)}, u32[]{:S(2)}, u32[]{:S(2)}) %all-to-all-start.5) | async-done | bytes 294944 | tf_op jit(solution)/shard_map/all_to_all | solution.py:147
  100.1 0.7 copy.125
  100.8 3.3 %all-to-all-start.6 = ((f32[4,1,6144]{2,1,0:T(1,128)}), f32[4,1,6144]{2,1,0:T(1,128)S(1)}, u32[]{:S(2)}, u32[]{:S(2)}) async-start(f32[4,1,6144]{2,1,0:T(1,128)} %copy.125), calls=%async_computation.6 | async-start | bytes 196608 | tf_op jit(solution)/shard_map/all_to_all | solution.py:147
  104.1 5.7 %all-to-all-done.6 = f32[4,1,6144]{2,1,0:T(1,128)S(1)} async-done(((f32[4,1,6144]{2,1,0:T(1,128)}), f32[4,1,6144]{2,1,0:T(1,128)S(1)}, u32[]{:S(2)}, u32[]{:S(2)}) %all-to-all-start.6) | async-done | bytes 98336 | tf_op jit(solution)/shard_map/all_to_all | solution.py:147
  111.8 4.6 %all-to-all-start.7 = ((f32[2,1,4096]{2,1,0:T(1,128)}), f32[2,1,4096]{2,1,0:T(1,128)S(1)}, u32[]{:S(2)}, u32[]{:S(2)}) async-start(f32[2,1,4096]{2,1,0:T(1,128)} %all_to_all.61), calls=%async_computation.7 | async-start | bytes 65536 | tf_op jit(solution)/shard_map/all_to_all | solution.py:147
  117.0 12.1 %all-to-all-done.7 = f32[2,1,4096]{2,1,0:T(1,128)S(1)} async-done(((f32[2,1,4096]{2,1,0:T(1,128)}), f32[2,1,4096]{2,1,0:T(1,128)S(1)}, u32[]{:S(2)}, u32[]{:S(2)}) %all-to-all-start.7) | async-done | bytes 32800 | tf_op jit(solution)/shard_map/all_to_all | solution.py:147
  130.0 0.7 copy.136
  130.8 0.7 copy.135
  (140 shorter events, 18.2 us)
Async XLA Ops:
  0.6 73.0 %copy-start = (bf16[128,256]{1,0:T(8,128)(2,1)S(1)}, bf16[128,256]{1,0:T(8,128)(2,1)}, u32[]{:S(2)}) copy-start(bf16[128,256]{1,0:T(8,128)(2,1)} %param.13) | copy-start | bytes 196612
  5.4 30.2 %all-to-all-start = ((bf16[16,2,2568]{2,1,0:T(2,128)(2,1)}), bf16[16,2,2568]{2,1,0:T(2,128)(2,1)S(1)}, u32[]{:S(2)}, u32[]{:S(2)}) async-start(bf16[16,2,2568]{2,1,0:T(2,128)(2,1)} %reshape.394), calls=%async_computation | async-start | bytes 344064 | tf_op jit(solution)/shard_map/all_to_all | solution.py:196
  52.7 20.1 %all-to-all-start.3 = ((bf16[4,4,2,2,8,1026]{5,4,2,1,3,0:T(8,128)(2,1)}), bf16[4,4,2,2,8,1026]{5,4,2,1,3,0:T(8,128)(2,1)S(1)}, u32[]{:S(2)}, u32[]{:S(2)}) async-start(bf16[4,4,2,2,8,1026]{5,4,2,1,3,0:T(8,128)(2,1)} %broadcast_in_dim.100), calls=%async_computation.3 | async-start | bytes 2359296 | tf_op jit(solution)/shard_map/all_to_all | solution.py:20
  73.3 0.9 copy-start.2
  85.8 4.6 %copy-start.1 = (bf16[512,512]{0,1:T(8,128)(2,1)S(1)}, bf16[512,512]{0,1:T(8,128)(2,1)}, u32[]{:S(2)}) copy-start(bf16[512,512]{0,1:T(8,128)(2,1)} %copy.133) | copy-start | bytes 1572868
  86.9 11.0 %all-to-all-start.5 = ((f32[4,1,18432]{2,1,0:T(1,128)}), f32[4,1,18432]{2,1,0:T(1,128)S(1)}, u32[]{:S(2)}, u32[]{:S(2)}) async-start(f32[4,1,18432]{2,1,0:T(1,128)} %all_to_all.55), calls=%async_computation.5 | async-start | bytes 589824 | tf_op jit(solution)/shard_map/all_to_all | solution.py:147
  100.8 9.1 %all-to-all-start.6 = ((f32[4,1,6144]{2,1,0:T(1,128)}), f32[4,1,6144]{2,1,0:T(1,128)S(1)}, u32[]{:S(2)}, u32[]{:S(2)}) async-start(f32[4,1,6144]{2,1,0:T(1,128)} %copy.125), calls=%async_computation.6 | async-start | bytes 196608 | tf_op jit(solution)/shard_map/all_to_all | solution.py:147
  111.8 17.2 %all-to-all-start.7 = ((f32[2,1,4096]{2,1,0:T(1,128)}), f32[2,1,4096]{2,1,0:T(1,128)S(1)}, u32[]{:S(2)}, u32[]{:S(2)}) async-start(f32[2,1,4096]{2,1,0:T(1,128)} %all_to_all.61), calls=%async_computation.7 | async-start | bytes 65536 | tf_op jit(solution)/shard_map/all_to_all | solution.py:147

commit v9 on v7

--- a/solution.py
+++ b/solution.py
@@ -110,18 +110,22 @@
 
 
 def gather_seq(x, axes):
-    for axis in axes:
-        x = from_everyone(x, axis)
-    order = [GATHER_ORDER[::-1].index(axis) for axis in SEQ_AXES]
+    x = from_everyone(x, axes)
+    x = x.reshape(*[lax.axis_size(axis) for axis in axes], *x.shape[1:])
+    stacked = (*axes, *GATHER_ORDER[: 4 - len(axes)][::-1])
+    order = [stacked.index(axis) for axis in SEQ_AXES]
     x = jnp.transpose(x, (*order, *range(4, x.ndim)))
     return x.reshape(-1, *x.shape[5:])
+
+
+MERGE_GROUPS = ("y", ("zh", "x"), "c")
 
 
 def merged_with_dq(row_max, row_sum, partial_dq):
     rows = partial_dq.shape[0]
     width = partial_dq[0].size
     start = 0
-    for axis in SEQ_AXES:
+    for axis in MERGE_GROUPS:
         size = lax.axis_size(axis)
         rows //= size
         stats = jnp.stack([row_max, row_sum]).reshape(1, -1)
@@ -191,7 +195,7 @@
     rest = jnp.concatenate(
         (first[..., :cross_width], self_mine.reshape(*first.shape[:-1], -1)), axis=-1
     )
-    gathered = gather_seq(rest, GATHER_ORDER[2:])
+    gathered = gather_seq(rest, GATHER_ORDER[2:][::-1])
     query_all = gathered[:, : cross_q.shape[1]]
     grad_all = gathered[:, cross_q.shape[1] : 2 * cross_q.shape[1]]
     dots_all = gathered[:, 2 * cross_q.shape[1] : cross_width]

time: 133 us -> 124 us (0.932)
  blocking collectives: 33.7 us -> 19.3 us
  starting transfers between devices: 30.8 us -> 33.3 us
  local copies, waits for them, and re-layouts: 14.5 us -> 12.3 us
  other arithmetic: 5.6 us -> 7.39 us
  waiting for transfers between devices: 41.5 us -> 43.1 us
  matrix products: 4 us -> 5.6 us
    all_to_all x2 -> x1, blocking collectives: 18.2 us -> 7.95 us  [from_everyone(): return lax.all_to_all(copies, axis, split_axis=0, concat_axis=0, tiled=True)]
    all_to_all x1, waiting for transfers between devices: 14.1 us -> 17.3 us  [from_everyone(): return lax.all_to_all(copies, axis, split_axis=0, concat_axis=0, tiled=True)]
    all_to_all x1, starting transfers between devices: 4.18 us -> 6.75 us  [from_everyone(): return lax.all_to_all(copies, axis, split_axis=0, concat_axis=0, tiled=True)]
    all_gather x1, blocking collectives: 5.61 us -> 3.37 us  [shards(): lax.all_gather(head_results.reshape(3, chip_rows, HEAD_DIM), 'c', axis=0)]
    unnamed x5 -> x7, other arithmetic: 0.82 us -> 2.94 us
    all_to_all x1, blocking collectives: 9.82 us -> 7.98 us  [merged_with_dq(): got = lax.all_to_all(send, axis, 0, 0, tiled=True)]
    all_to_all x3 -> x2, waiting for transfers between devices: 15.1 us -> 13.5 us  [merged_with_dq(): got = lax.all_to_all(send, axis, 0, 0, tiled=True)]
    unnamed x23 -> x20, local copies, waits for them, and re-layouts: 4.22 us -> 3.36 us
  transfers between devices with their start and end apart: 5 -> 4, of which waited for: 5 -> 4; matrix products, arithmetic and copies ran while one was open for 3% -> 4% of each run, Pallas kernels for 0% -> 0%
where the time goes in v9:
time: 124 us; the launch traced here: 123 us
  waiting for transfers between devices  43.1 us (35%)
  starting transfers between devices  33.3 us (27%)
  blocking collectives  19.3 us (16%)
  local copies, waits for them, and re-layouts  12.3 us (10%)
  other arithmetic  7.39 us (6%)
  matrix products  5.6 us (5%)
  between operations  1.9 us (2%)
    all_to_all x1, waiting for transfers between devices, from_everyone(): return lax.all_to_all(copies, axis, split_axis=0, concat_axis=0, tiled=True)  17.3 us
    all_to_all x1, starting transfers between devices, shards(): lax.all_to_all(outgoing.reshape(far_pairs * head_groups, -1), ('zh', 'zl'...  15.7 us
    all_to_all x2, waiting for transfers between devices, merged_with_dq(): got = lax.all_to_all(send, axis, 0, 0, tiled=True)  13.5 us
    all_to_all x1, waiting for transfers between devices, shards(): lax.all_to_all(outgoing.reshape(far_pairs * head_groups, -1), ('zh', 'zl'...  12.2 us
    all_to_all x2, starting transfers between devices, merged_with_dq(): got = lax.all_to_all(send, axis, 0, 0, tiled=True)  10.8 us
    all_to_all x1, blocking collectives, merged_with_dq(): got = lax.all_to_all(send, axis, 0, 0, tiled=True)  7.98 us
    all_to_all x1, blocking collectives, from_everyone(): return lax.all_to_all(copies, axis, split_axis=0, concat_axis=0, tiled=True)  7.95 us
    all_to_all x1, starting transfers between devices, from_everyone(): return lax.all_to_all(copies, axis, split_axis=0, concat_axis=0, tiled=True)  6.75 us
  transfers between devices with their start and end apart: 4, of which 4 were waited for; matrix products, arithmetic and copies ran while one was open for 4% of the time, Pallas kernels for 0%

profile of v9, /device:TPU:1, one launch (start us, length us, event | category | flops | bytes accessed | tf_op | source)
XLA Modules:
  0.0 122.9 jit_solution(15213188646513472181)
XLA Ops:
  0.6 0.8 bitcast_reduce_fusion.2
  2.3 0.7 reduce.12
  3.1 0.7 reduce.13
  3.8 0.7 reduce.14
  6.7 0.9 reshape.342
  7.5 15.7 %all-to-all-start = ((bf16[16,2,2568]{2,1,0:T(2,128)(2,1)}), bf16[16,2,2568]{2,1,0:T(2,128)(2,1)S(1)}, u32[]{:S(2)}, u32[]{:S(2)}) async-start(bf16[16,2,2568]{2,1,0:T(2,128)(2,1)} %reshape.342), calls=%async_computation | async-start | bytes 344064 | tf_op jit(solution)/shard_map/all_to_all | solution.py:183
  23.3 12.2 %all-to-all-done = bf16[16,2,2568]{2,1,0:T(2,128)(2,1)S(1)} async-done(((bf16[16,2,2568]{2,1,0:T(2,128)(2,1)}), bf16[16,2,2568]{2,1,0:T(2,128)(2,1)S(1)}, u32[]{:S(2)}, u32[]{:S(2)}) %all-to-all-start) | async-done | bytes 164384 | tf_op jit(solution)/shard_map/all_to_all | solution.py:183
  36.1 7.9 %all_to_all.55 = bf16[2,2,8,1538]{3,2,1,0:T(8,128)(2,1)S(1)} all-to-all(bf16[2,2,8,1538]{3,2,1,0:T(8,128)(2,1)S(1)} %broadcast_in_dim.84), channel_id=1, replica_groups=mesh['y'=4,'zh'=2,'x'=4,'c'=2,'zl'=8] {'c'}, dimensions={0} | all-to-all | bytes 196864 | tf_op jit(solution)/shard_map/all_to_all | solution.py:20
  44.3 1.1 broadcast_in_dim.85
  45.4 6.8 %all-to-all-start.2 = ((bf16[16,2,2,8,1026]{4,3,2,1,0:T(8,128)(2,1)}), bf16[16,2,2,8,1026]{4,3,2,1,0:T(8,128)(2,1)S(1)}, u32[]{:S(2)}, u32[]{:S(2)}) async-start(bf16[16,2,2,8,1026]{4,3,2,1,0:T(8,128)(2,1)} %broadcast_in_dim.85), calls=%async_computation.2 | async-start | bytes 2359296 | tf_op jit(solution)/shard_map/all_to_all | solution.py:20
  52.8 17.3 %all-to-all-done.2 = bf16[16,2,2,8,1026]{4,3,2,1,0:T(8,128)(2,1)S(1)} async-done(((bf16[16,2,2,8,1026]{4,3,2,1,0:T(8,128)(2,1)}), bf16[16,2,2,8,1026]{4,3,2,1,0:T(8,128)(2,1)S(1)}, u32[]{:S(2)}, u32[]{:S(2)}) %all-to-all-start.2) | async-done | bytes 1050656 | tf_op jit(solution)/shard_map/all_to_all | solution.py:20
  74.0 1.4 %copy.124 = f32[4,1,34816]{2,1,0:T(1,128)} copy(f32[4,1,34816]{2,0,1:T(4,128)S(1)} %maximum_bitcast_fusion) | data formatting | bytes 1114112 | tf_op jit(solution)/shard_map/all_to_all | solution.py:135
  75.4 3.5 %all-to-all-start.3 = ((f32[4,1,34816]{2,1,0:T(1,128)}), f32[4,1,34816]{2,1,0:T(1,128)S(1)}, u32[]{:S(2)}, u32[]{:S(2)}) async-start(f32[4,1,34816]{2,1,0:T(1,128)} %copy.124), calls=%async_computation.3 | async-start | bytes 1114112 | tf_op jit(solution)/shard_map/all_to_all | solution.py:135
  80.0 1.2 fusion.3
  81.2 4.8 %all-to-all-done.3 = f32[4,1,34816]{2,1,0:T(1,128)S(1)} async-done(((f32[4,1,34816]{2,1,0:T(1,128)}), f32[4,1,34816]{2,1,0:T(1,128)S(1)}, u32[]{:S(2)}, u32[]{:S(2)}) %all-to-all-start.3) | async-done | bytes 557088 | tf_op jit(solution)/shard_map/all_to_all | solution.py:135
  88.2 0.8 all_to_all.43
  89.0 7.3 %all-to-all-start.4 = ((f32[8,1,6144]{2,1,0:T(1,128)}), f32[8,1,6144]{2,1,0:T(1,128)S(1)}, u32[]{:S(2)}, u32[]{:S(2)}) async-start(f32[8,1,6144]{2,1,0:T(1,128)} %all_to_all.43), calls=%async_computation.4 | async-start | bytes 393216 | tf_op jit(solution)/shard_map/all_to_all | solution.py:135
  96.3 0.9 fusion.8
  97.2 1.2 fusion.7
  98.4 3.4 %all_gather.3 = bf16[2,3,16,128]{3,2,1,0:T(8,128)(2,1)S(1)} all-gather(bf16[1,3,16,128]{3,2,1,0:T(8,128)(2,1)S(1)} %pad_maximum_fusion.6), channel_id=1, replica_groups=mesh['y'=4,'zh'=2,'x'=4,'c'=2,'zl'=8] {'c'}, dimensions={0}, use_global_device_ids=true | all-gather | bytes 36864 | tf_op jit(solution)/shard_map/all_gather | solution.py:268
  102.4 8.7 %all-to-all-done.4 = f32[8,1,6144]{2,1,0:T(1,128)S(1)} async-done(((f32[8,1,6144]{2,1,0:T(1,128)}), f32[8,1,6144]{2,1,0:T(1,128)S(1)}, u32[]{:S(2)}, u32[]{:S(2)}) %all-to-all-start.4) | async-done | bytes 196640 | tf_op jit(solution)/shard_map/all_to_all | solution.py:135
  111.7 8.0 %all_to_all.56 = f32[2,1,4096]{2,1,0:T(1,128)S(1)} all-to-all(f32[2,1,4096]{2,1,0:T(1,128)S(1)} %all_to_all.46), channel_id=1, replica_groups=mesh['y'=4,'zh'=2,'x'=4,'c'=2,'zl'=8] {'c'}, dimensions={0} | all-to-all | bytes 65536 | tf_op jit(solution)/shard_map/all_to_all | solution.py:135
  120.5 0.7 copy.135
  121.2 0.7 copy.134
  (109 shorter events, 13.4 us)
Async XLA Ops:
  0.6 70.6 %copy-start = (bf16[128,256]{1,0:T(8,128)(2,1)S(1)}, bf16[128,256]{1,0:T(8,128)(2,1)}, u32[]{:S(2)}) copy-start(bf16[128,256]{1,0:T(8,128)(2,1)} %param.13) | copy-start | bytes 196612
  7.5 28.0 %all-to-all-start = ((bf16[16,2,2568]{2,1,0:T(2,128)(2,1)}), bf16[16,2,2568]{2,1,0:T(2,128)(2,1)S(1)}, u32[]{:S(2)}, u32[]{:S(2)}) async-start(bf16[16,2,2568]{2,1,0:T(2,128)(2,1)} %reshape.342), calls=%async_computation | async-start | bytes 344064 | tf_op jit(solution)/shard_map/all_to_all | solution.py:183
  45.4 24.8 %all-to-all-start.2 = ((bf16[16,2,2,8,1026]{4,3,2,1,0:T(8,128)(2,1)}), bf16[16,2,2,8,1026]{4,3,2,1,0:T(8,128)(2,1)S(1)}, u32[]{:S(2)}, u32[]{:S(2)}) async-start(bf16[16,2,2,8,1026]{4,3,2,1,0:T(8,128)(2,1)} %broadcast_in_dim.85), calls=%async_computation.2 | async-start | bytes 2359296 | tf_op jit(solution)/shard_map/all_to_all | solution.py:20
  71.1 8.9 %copy-start.1 = (bf16[512,512]{0,1:T(8,128)(2,1)}, bf16[512,512]{0,1:T(8,128)(2,1)S(1)}, u32[]{:S(2)}) copy-start(bf16[512,512]{0,1:T(8,128)(2,1)S(1)} %copy.132) | copy-start | bytes 1572868
  71.1 0.9 copy-start.3
  75.4 10.7 %all-to-all-start.3 = ((f32[4,1,34816]{2,1,0:T(1,128)}), f32[4,1,34816]{2,1,0:T(1,128)S(1)}, u32[]{:S(2)}, u32[]{:S(2)}) async-start(f32[4,1,34816]{2,1,0:T(1,128)} %copy.124), calls=%async_computation.3 | async-start | bytes 1114112 | tf_op jit(solution)/shard_map/all_to_all | solution.py:135
  87.7 8.6 %copy-start.2 = (bf16[512,512]{0,1:T(8,128)(2,1)S(1)}, bf16[512,512]{0,1:T(8,128)(2,1)}, u32[]{:S(2)}) copy-start(bf16[512,512]{0,1:T(8,128)(2,1)} %copy-done.1) | copy-start | bytes 1572868
  89.0 22.1 %all-to-all-start.4 = ((f32[8,1,6144]{2,1,0:T(1,128)}), f32[8,1,6144]{2,1,0:T(1,128)S(1)}, u32[]{:S(2)}, u32[]{:S(2)}) async-start(f32[8,1,6144]{2,1,0:T(1,128)} %all_to_all.43), calls=%async_computation.4 | async-start | bytes 393216 | tf_op jit(solution)/shard_map/all_to_all | solution.py:135

commit v10 on v9

--- a/solution.py
+++ b/solution.py
@@ -118,7 +118,7 @@
     return x.reshape(-1, *x.shape[5:])
 
 
-MERGE_GROUPS = ("y", ("zh", "x"), "c")
+MERGE_GROUPS = ("y", ("zh", "x", "c"))
 
 
 def merged_with_dq(row_max, row_sum, partial_dq):

time: 124 us -> 134 us (1.081)
  the two profiles are of different devices: /device:TPU:1 before, /device:TPU:32 now
where the time goes in v10:
time: 134 us; the launch traced here: 133 us
  waiting for transfers between devices  60.8 us (45%)
  starting transfers between devices  32.3 us (24%)
  local copies, waits for them, and re-layouts  18.7 us (14%)
  other arithmetic  9.95 us (7%)
  blocking collectives  5.7 us (4%)
  matrix products  3.83 us (3%)
  between operations  1.78 us (1%)
    all_to_all x2, waiting for transfers between devices, merged_with_dq(): got = lax.all_to_all(send, axis, 0, 0, tiled=True)  26.9 us
    all_to_all x1, waiting for transfers between devices, from_everyone(): return lax.all_to_all(copies, axis, split_axis=0, concat_axis=0, tiled=True)  19 us
    all_to_all x1, starting transfers between devices, shards(): lax.all_to_all(outgoing.reshape(far_pairs * head_groups, -1), ('zh', 'zl'...  15.2 us
    all_to_all x1, waiting for transfers between devices, shards(): lax.all_to_all(outgoing.reshape(far_pairs * head_groups, -1), ('zh', 'zl'...  14.9 us
    all_to_all x2, starting transfers between devices, merged_with_dq(): got = lax.all_to_all(send, axis, 0, 0, tiled=True)  10.1 us
    all_to_all x1, starting transfers between devices, from_everyone(): return lax.all_to_all(copies, axis, split_axis=0, concat_axis=0, tiled=True)  7.03 us
    unnamed x20, local copies, waits for them, and re-layouts  5.27 us
    mul x4, local copies, waits for them, and re-layouts, merged_with_dq(): partial_dq = jnp.sum(dq_rescale[..., None] * got_dq, axis=0)  4.07 us
  transfers between devices with their start and end apart: 4, of which 4 were waited for; matrix products, arithmetic and copies ran while one was open for 2% of the time, Pallas kernels for 0%

profile of v10, /device:TPU:32, one launch (start us, length us, event | category | flops | bytes accessed | tf_op | source)
XLA Modules:
  0.0 133.1 jit_solution(8530301601984091196)
XLA Ops:
  0.6 0.8 bitcast_reduce_fusion.2
  6.7 0.9 reshape.323
  7.5 15.2 %all-to-all-start = ((bf16[16,2,2568]{2,1,0:T(2,128)(2,1)}), bf16[16,2,2568]{2,1,0:T(2,128)(2,1)S(1)}, u32[]{:S(2)}, u32[]{:S(2)}) async-start(bf16[16,2,2568]{2,1,0:T(2,128)(2,1)} %reshape.323), calls=%async_computation | async-start | bytes 344064 | tf_op jit(solution)/shard_map/all_to_all | solution.py:183
  22.7 14.9 %all-to-all-done = bf16[16,2,2568]{2,1,0:T(2,128)(2,1)S(1)} async-done(((bf16[16,2,2568]{2,1,0:T(2,128)(2,1)}), bf16[16,2,2568]{2,1,0:T(2,128)(2,1)S(1)}, u32[]{:S(2)}, u32[]{:S(2)}) %all-to-all-start) | async-done | bytes 164384 | tf_op jit(solution)/shard_map/all_to_all | solution.py:183
  38.3 3.8 %all_to_all.43 = bf16[2,2,8,1538]{3,2,1,0:T(8,128)(2,1)S(1)} all-to-all(bf16[2,2,8,1538]{3,2,1,0:T(8,128)(2,1)S(1)} %broadcast_in_dim.73), channel_id=1, replica_groups=mesh['y'=4,'zh'=2,'x'=4,'c'=2,'zl'=8] {'c'}, dimensions={0} | all-to-all | bytes 196864 | tf_op jit(solution)/shard_map/all_to_all | solution.py:20
  42.3 1.1 broadcast_in_dim.74
  43.4 7.0 %all-to-all-start.2 = ((bf16[16,2,2,8,1026]{4,3,2,1,0:T(8,128)(2,1)}), bf16[16,2,2,8,1026]{4,3,2,1,0:T(8,128)(2,1)S(1)}, u32[]{:S(2)}, u32[]{:S(2)}) async-start(bf16[16,2,2,8,1026]{4,3,2,1,0:T(8,128)(2,1)} %broadcast_in_dim.74), calls=%async_computation.2 | async-start | bytes 2359296 | tf_op jit(solution)/shard_map/all_to_all | solution.py:20
  51.1 19.0 %all-to-all-done.2 = bf16[16,2,2,8,1026]{4,3,2,1,0:T(8,128)(2,1)S(1)} async-done(((bf16[16,2,2,8,1026]{4,3,2,1,0:T(8,128)(2,1)}), bf16[16,2,2,8,1026]{4,3,2,1,0:T(8,128)(2,1)S(1)}, u32[]{:S(2)}, u32[]{:S(2)}) %all-to-all-start.2) | async-done | bytes 1050656 | tf_op jit(solution)/shard_map/all_to_all | solution.py:20
  74.0 1.4 %copy.120 = f32[4,1,34816]{2,1,0:T(1,128)} copy(f32[4,1,34816]{2,0,1:T(4,128)S(1)} %maximum_bitcast_fusion) | data formatting | bytes 1114112 | tf_op jit(solution)/shard_map/all_to_all | solution.py:135
  75.4 4.1 %all-to-all-start.3 = ((f32[4,1,34816]{2,1,0:T(1,128)}), f32[4,1,34816]{2,1,0:T(1,128)}, u32[]{:S(2)}, u32[]{:S(2)}) async-start(f32[4,1,34816]{2,1,0:T(1,128)} %copy.120), calls=%async_computation.3 | async-start | bytes 1114112 | tf_op jit(solution)/shard_map/all_to_all | solution.py:135
  80.3 0.8 copy-done.3
  81.3 6.7 %all-to-all-done.3 = f32[4,1,34816]{2,1,0:T(1,128)} async-done(((f32[4,1,34816]{2,1,0:T(1,128)}), f32[4,1,34816]{2,1,0:T(1,128)}, u32[]{:S(2)}, u32[]{:S(2)}) %all-to-all-start.3) | async-done | bytes 557088 | tf_op jit(solution)/shard_map/all_to_all | solution.py:135
  88.0 1.3 copy.167
  89.6 1.4 %mul.93 = f32[4,128,2,128]{3,2,1,0:T(2,128)} broadcast(f32[4,128,2]{2,1,0:T(8,128)S(1)} %copy.122), dimensions={0,1,2} | broadcast | bytes 528384 | tf_op jit(solution)/shard_map/mul | solution.py:144
  91.0 2.3 %mul.94 = f32[4,32768]{1,0:T(4,128)} reshape(f32[4,128,2,128]{3,2,1,0:T(2,128)} %mul.93) | data formatting | bytes 1048576 | tf_op jit(solution)/shard_map/mul | solution.py:144
  93.4 2.1 %fusion.11 = f32[32768]{0:T(1024)} fusion(f32[4,32768]{1,0:T(4,128)} %mul.94, f32[4,34816]{1,0:T(4,128)S(1)} %bitcast.187), kind=kLoop, calls=%fused_computation.28 | loop fusion | flops 229376 | bytes 1179648 | tf_op jit(solution)/shard_map/reduce_sum | solution.py:144
  95.4 1.6 %reshape.308 = f32[16,2048]{1,0:T(8,128)} reshape(f32[32768]{0:T(1024)} %fusion.11) | data formatting | bytes 262144 | tf_op jit(solution)/shard_map/reshape | solution.py:133
  97.1 0.9 pad_maximum_fusion
  98.0 1.0 all_to_all.35
  99.0 6.0 %all-to-all-start.4 = ((f32[16,1,4096]{2,1,0:T(1,128)}), f32[16,1,4096]{2,1,0:T(1,128)S(1)}, u32[]{:S(2)}, u32[]{:S(2)}) async-start(f32[16,1,4096]{2,1,0:T(1,128)} %all_to_all.35), calls=%async_computation.4 | async-start | bytes 524288 | tf_op jit(solution)/shard_map/all_to_all | solution.py:135
  104.9 0.9 fusion.9
  106.6 1.9 %all_gather.3 = bf16[2,3,16,128]{3,2,1,0:T(8,128)(2,1)S(1)} all-gather(bf16[1,3,16,128]{3,2,1,0:T(8,128)(2,1)S(1)} %pad_maximum_fusion.5), channel_id=1, replica_groups=mesh['y'=4,'zh'=2,'x'=4,'c'=2,'zl'=8] {'c'}, dimensions={0}, use_global_device_ids=true | all-gather | bytes 36864 | tf_op jit(solution)/shard_map/all_gather | solution.py:268
  109.1 20.2 %all-to-all-done.4 = f32[16,1,4096]{2,1,0:T(1,128)S(1)} async-done(((f32[16,1,4096]{2,1,0:T(1,128)}), f32[16,1,4096]{2,1,0:T(1,128)S(1)}, u32[]{:S(2)}, u32[]{:S(2)}) %all-to-all-start.4) | async-done | bytes 262176 | tf_op jit(solution)/shard_map/all_to_all | solution.py:135
  130.4 0.8 copy.130
  (96 shorter events, 15.3 us)
Async XLA Ops:
  0.6 70.6 %copy-start = (bf16[128,256]{1,0:T(8,128)(2,1)S(1)}, bf16[128,256]{1,0:T(8,128)(2,1)}, u32[]{:S(2)}) copy-start(bf16[128,256]{1,0:T(8,128)(2,1)} %param.13) | copy-start | bytes 196612
  7.5 30.2 %all-to-all-start = ((bf16[16,2,2568]{2,1,0:T(2,128)(2,1)}), bf16[16,2,2568]{2,1,0:T(2,128)(2,1)S(1)}, u32[]{:S(2)}, u32[]{:S(2)}) async-start(bf16[16,2,2568]{2,1,0:T(2,128)(2,1)} %reshape.323), calls=%async_computation | async-start | bytes 344064 | tf_op jit(solution)/shard_map/all_to_all | solution.py:183
  43.4 26.7 %all-to-all-start.2 = ((bf16[16,2,2,8,1026]{4,3,2,1,0:T(8,128)(2,1)}), bf16[16,2,2,8,1026]{4,3,2,1,0:T(8,128)(2,1)S(1)}, u32[]{:S(2)}, u32[]{:S(2)}) async-start(bf16[16,2,2,8,1026]{4,3,2,1,0:T(8,128)(2,1)} %broadcast_in_dim.74), calls=%async_computation.2 | async-start | bytes 2359296 | tf_op jit(solution)/shard_map/all_to_all | solution.py:20
  71.1 9.2 %copy-start.1 = (bf16[512,512]{0,1:T(8,128)(2,1)}, bf16[512,512]{0,1:T(8,128)(2,1)S(1)}, u32[]{:S(2)}) copy-start(bf16[512,512]{0,1:T(8,128)(2,1)S(1)} %copy.127) | copy-start | bytes 1572868
  71.1 0.9 copy-start.4
  75.4 12.6 %all-to-all-start.3 = ((f32[4,1,34816]{2,1,0:T(1,128)}), f32[4,1,34816]{2,1,0:T(1,128)}, u32[]{:S(2)}, u32[]{:S(2)}) async-start(f32[4,1,34816]{2,1,0:T(1,128)} %copy.120), calls=%async_computation.3 | async-start | bytes 1114112 | tf_op jit(solution)/shard_map/all_to_all | solution.py:135
  80.3 0.8 copy-start.3
  95.4 9.5 %copy-start.2 = (bf16[512,512]{0,1:T(8,128)(2,1)S(1)}, bf16[512,512]{0,1:T(8,128)(2,1)}, u32[]{:S(2)}) copy-start(bf16[512,512]{0,1:T(8,128)(2,1)} %copy-done.1) | copy-start | bytes 1572868
  99.0 30.3 %all-to-all-start.4 = ((f32[16,1,4096]{2,1,0:T(1,128)}), f32[16,1,4096]{2,1,0:T(1,128)S(1)}, u32[]{:S(2)}, u32[]{:S(2)}) async-start(f32[16,1,4096]{2,1,0:T(1,128)} %all_to_all.35), calls=%async_computation.4 | async-start | bytes 524288 | tf_op jit(solution)/shard_map/all_to_all | solution.py:135

commit v11 on v9

--- a/solution.py
+++ b/solution.py
@@ -121,7 +121,7 @@
 MERGE_GROUPS = ("y", ("zh", "x"), "c")
 
 
-def merged_with_dq(row_max, row_sum, partial_dq):
+def merged_with_dq(row_max, row_sum, partial_dq, extra):
     rows = partial_dq.shape[0]
     width = partial_dq[0].size
     start = 0
@@ -129,10 +129,15 @@
         size = lax.axis_size(axis)
         rows //= size
         stats = jnp.stack([row_max, row_sum]).reshape(1, -1)
+        if axis == MERGE_GROUPS[-1]:
+            stats = jnp.concatenate([stats, extra.reshape(1, -1)], axis=1)
         send = jnp.concatenate(
             [partial_dq.reshape(size, -1), jnp.broadcast_to(stats, (size, stats.shape[1]))], axis=1
         )
         got = lax.all_to_all(send, axis, 0, 0, tiled=True)
+        if axis == MERGE_GROUPS[-1]:
+            got_extra = got[:, send.shape[1] - extra.size :]
+            got = got[:, : send.shape[1] - extra.size]
         got_dq = got[:, : rows * width].reshape(size, rows, *partial_dq.shape[1:])
         got_stats = got[:, rows * width :].reshape(size, 2, *row_max.shape)
         top = jnp.max(got_stats[:, 0], axis=0)
@@ -143,7 +148,7 @@
         dq_rescale = jnp.transpose(lax.dynamic_slice_in_dim(rescale, start, rows, 2), (0, 2, 1))
         partial_dq = jnp.sum(dq_rescale[..., None] * got_dq, axis=0)
     own_sum = jnp.transpose(lax.dynamic_slice_in_dim(row_sum, start, rows, 1))
-    return row_max, row_sum, partial_dq / own_sum[..., None]
+    return row_max, row_sum, partial_dq / own_sum[..., None], got_extra
 
 
 def shards(
@@ -223,19 +228,6 @@
         precision=lax.Precision.HIGHEST,
         preferred_element_type=jnp.float32,
     )
-    row_maxes, row_sums, own_dq = merged_with_dq(row_max, row_sum, local_dq)
-    log_total = row_maxes + jnp.log(row_sums)
-    weights = jnp.exp(scores - log_total[:, :, None])
-    prefix_dv = (
-        contract_rows(weights.astype(jnp.bfloat16), grad_heads)
-        .reshape(tokens, feature_width)
-        .astype(jnp.bfloat16)
-    )
-    grad_scores = scores_grad(weights, grad_heads, value_heads, row_dots, score_scale)
-    prefix_dk = (
-        contract_rows(grad_scores, query_heads).reshape(tokens, feature_width).astype(jnp.bfloat16)
-    )
-    cross_dq = own_dq.reshape(own_rows, feature_width).astype(jnp.bfloat16)
     everything = jnp.transpose(self_all.reshape(latents, 4, HEAD_DIM), (1, 0, 2))
     all_rows = everything.shape[1]
     query_every = everything[0].reshape(all_rows, 1, HEAD_DIM)
@@ -265,10 +257,24 @@
             contract_rows(half_part, grad_every),
         ]
     ).astype(jnp.bfloat16)
-    both = lax.all_gather(head_results.reshape(3, chip_rows, HEAD_DIM), "c", axis=0)
+    self_extra = head_results.astype(jnp.float32).reshape(-1)
+    row_maxes, row_sums, own_dq, got_extra = merged_with_dq(row_max, row_sum, local_dq, self_extra)
+    both = got_extra.astype(jnp.bfloat16).reshape(cores, 3, chip_rows, HEAD_DIM)
     mine = lax.dynamic_slice_in_dim(both, core * block_rows, block_rows, 2)
     mine = jnp.transpose(mine, (1, 2, 0, 3)).reshape(3, block_rows, feature_width)
     self_dq, self_dk, self_dv = mine[0], mine[1], mine[2]
+    log_total = row_maxes + jnp.log(row_sums)
+    weights = jnp.exp(scores - log_total[:, :, None])
+    prefix_dv = (
+        contract_rows(weights.astype(jnp.bfloat16), grad_heads)
+        .reshape(tokens, feature_width)
+        .astype(jnp.bfloat16)
+    )
+    grad_scores = scores_grad(weights, grad_heads, value_heads, row_dots, score_scale)
+    prefix_dk = (
+        contract_rows(grad_scores, query_heads).reshape(tokens, feature_width).astype(jnp.bfloat16)
+    )
+    cross_dq = own_dq.reshape(own_rows, feature_width).astype(jnp.bfloat16)
     return (cross_dq, prefix_dk, prefix_dv, self_dq, self_dk, self_dv)
 
 

time: 124 us -> 130 us (1.048)
  waiting for transfers between devices: 43.1 us -> 48.1 us
  local copies, waits for them, and re-layouts: 12.3 us -> 16.9 us
  blocking collectives: 19.3 us -> 15.9 us
  matrix products: 5.6 us -> 3.83 us
    all_to_all x2, waiting for transfers between devices: 13.5 us -> 18.6 us  [merged_with_dq(): got = lax.all_to_all(send, axis, 0, 0, tiled=True)]
    all_gather x1 -> x0, blocking collectives: 3.37 us -> none  [shards(): lax.all_gather(head_results.reshape(3, chip_rows, HEAD_DIM), 'c', axis=0)]
    mul x5, local copies, waits for them, and re-layouts: 1.32 us -> 3.96 us  [merged_with_dq(): partial_dq = jnp.sum(dq_rescale[..., None] * got_dq, axis=0)]
    unnamed x20 -> x23, local copies, waits for them, and re-layouts: 3.36 us -> 5.24 us
    unnamed x7 -> x6, other arithmetic: 2.94 us -> 2.93 us
  transfers between devices with their start and end apart: 4 -> 4, of which waited for: 4 -> 4; matrix products, arithmetic and copies ran while one was open for 4% -> 2% of each run, Pallas kernels for 0% -> 0%
where the time goes in v11:
time: 130 us; the launch traced here: 129 us
  waiting for transfers between devices  48.1 us (37%)
  starting transfers between devices  34.2 us (26%)
  local copies, waits for them, and re-layouts  16.9 us (13%)
  blocking collectives  15.9 us (12%)
  other arithmetic  8.48 us (7%)
  matrix products  3.83 us (3%)
  between operations  1.93 us (1%)
    all_to_all x2, waiting for transfers between devices, merged_with_dq(): got = lax.all_to_all(send, axis, 0, 0, tiled=True)  18.6 us
    all_to_all x1, waiting for transfers between devices, from_everyone(): return lax.all_to_all(copies, axis, split_axis=0, concat_axis=0, tiled=True)  17.3 us
    all_to_all x1, starting transfers between devices, shards(): lax.all_to_all(outgoing.reshape(far_pairs * head_groups, -1), ('zh', 'zl'...  15.7 us
    all_to_all x1, waiting for transfers between devices, shards(): lax.all_to_all(outgoing.reshape(far_pairs * head_groups, -1), ('zh', 'zl'...  12.2 us
    all_to_all x2, starting transfers between devices, merged_with_dq(): got = lax.all_to_all(send, axis, 0, 0, tiled=True)  11.7 us
    all_to_all x1, blocking collectives, merged_with_dq(): got = lax.all_to_all(send, axis, 0, 0, tiled=True)  7.97 us
    all_to_all x1, blocking collectives, from_everyone(): return lax.all_to_all(copies, axis, split_axis=0, concat_axis=0, tiled=True)  7.95 us
    all_to_all x1, starting transfers between devices, from_everyone(): return lax.all_to_all(copies, axis, split_axis=0, concat_axis=0, tiled=True)  6.75 us
  transfers between devices with their start and end apart: 4, of which 4 were waited for; matrix products, arithmetic and copies ran while one was open for 2% of the time, Pallas kernels for 0%

profile of v11, /device:TPU:1, one launch (start us, length us, event | category | flops | bytes accessed | tf_op | source)
XLA Modules:
  0.0 129.4 jit_solution(6800022027786033684)
XLA Ops:
  0.6 0.8 bitcast_reduce_fusion.2
  3.1 0.7 reduce.13
  6.7 0.9 reshape.321
  7.5 15.7 %all-to-all-start = ((bf16[16,2,2568]{2,1,0:T(2,128)(2,1)}), bf16[16,2,2568]{2,1,0:T(2,128)(2,1)S(1)}, u32[]{:S(2)}, u32[]{:S(2)}) async-start(bf16[16,2,2568]{2,1,0:T(2,128)(2,1)} %reshape.321), calls=%async_computation | async-start | bytes 344064 | tf_op jit(solution)/shard_map/all_to_all | solution.py:188
  23.3 12.2 %all-to-all-done = bf16[16,2,2568]{2,1,0:T(2,128)(2,1)S(1)} async-done(((bf16[16,2,2568]{2,1,0:T(2,128)(2,1)}), bf16[16,2,2568]{2,1,0:T(2,128)(2,1)S(1)}, u32[]{:S(2)}, u32[]{:S(2)}) %all-to-all-start) | async-done | bytes 164384 | tf_op jit(solution)/shard_map/all_to_all | solution.py:188
  36.1 7.9 %all_to_all.55 = bf16[2,2,8,1538]{3,2,1,0:T(8,128)(2,1)S(1)} all-to-all(bf16[2,2,8,1538]{3,2,1,0:T(8,128)(2,1)S(1)} %broadcast_in_dim.84), channel_id=1, replica_groups=mesh['y'=4,'zh'=2,'x'=4,'c'=2,'zl'=8] {'c'}, dimensions={0} | all-to-all | bytes 196864 | tf_op jit(solution)/shard_map/all_to_all | solution.py:20
  44.3 1.1 broadcast_in_dim.85
  45.4 6.8 %all-to-all-start.2 = ((bf16[16,2,2,8,1026]{4,3,2,1,0:T(8,128)(2,1)}), bf16[16,2,2,8,1026]{4,3,2,1,0:T(8,128)(2,1)S(1)}, u32[]{:S(2)}, u32[]{:S(2)}) async-start(bf16[16,2,2,8,1026]{4,3,2,1,0:T(8,128)(2,1)} %broadcast_in_dim.85), calls=%async_computation.2 | async-start | bytes 2359296 | tf_op jit(solution)/shard_map/all_to_all | solution.py:20
  52.8 17.3 %all-to-all-done.2 = bf16[16,2,2,8,1026]{4,3,2,1,0:T(8,128)(2,1)S(1)} async-done(((bf16[16,2,2,8,1026]{4,3,2,1,0:T(8,128)(2,1)}), bf16[16,2,2,8,1026]{4,3,2,1,0:T(8,128)(2,1)S(1)}, u32[]{:S(2)}, u32[]{:S(2)}) %all-to-all-start.2) | async-done | bytes 1050656 | tf_op jit(solution)/shard_map/all_to_all | solution.py:20
  74.0 1.4 %copy.124 = f32[4,1,34816]{2,1,0:T(1,128)} copy(f32[4,1,34816]{2,0,1:T(4,128)S(1)} %maximum_bitcast_fusion) | data formatting | bytes 1114112 | tf_op jit(solution)/shard_map/all_to_all | solution.py:137
  75.4 4.1 %all-to-all-start.3 = ((f32[4,1,34816]{2,1,0:T(1,128)}), f32[4,1,34816]{2,1,0:T(1,128)}, u32[]{:S(2)}, u32[]{:S(2)}) async-start(f32[4,1,34816]{2,1,0:T(1,128)} %copy.124), calls=%async_computation.3 | async-start | bytes 1114112 | tf_op jit(solution)/shard_map/all_to_all | solution.py:137
  80.3 0.8 copy-done.3
  81.3 5.5 %all-to-all-done.3 = f32[4,1,34816]{2,1,0:T(1,128)} async-done(((f32[4,1,34816]{2,1,0:T(1,128)}), f32[4,1,34816]{2,1,0:T(1,128)}, u32[]{:S(2)}, u32[]{:S(2)}) %all-to-all-start.3) | async-done | bytes 557088 | tf_op jit(solution)/shard_map/all_to_all | solution.py:137
  86.8 1.3 copy.175
  88.4 1.4 %mul.109 = f32[4,128,2,128]{3,2,1,0:T(2,128)} broadcast(f32[4,128,2]{2,1,0:T(8,128)S(1)} %copy.126), dimensions={0,1,2} | broadcast | bytes 528384 | tf_op jit(solution)/shard_map/mul | solution.py:149
  89.8 2.4 %mul.110 = f32[4,32768]{1,0:T(4,128)} reshape(f32[4,128,2,128]{3,2,1,0:T(2,128)} %mul.109) | data formatting | bytes 1048576 | tf_op jit(solution)/shard_map/mul | solution.py:149
  92.1 1.4 %fusion.11 = f32[32768]{0:T(1024)S(1)} fusion(f32[4,32768]{1,0:T(4,128)} %mul.110, f32[4,34816]{1,0:T(4,128)S(1)} %bitcast.213), kind=kLoop, calls=%fused_computation.28 | loop fusion | flops 229376 | bytes 1179648 | tf_op jit(solution)/shard_map/reduce_sum | solution.py:149
  93.6 0.8 all_to_all.43
  94.4 7.6 %all-to-all-start.4 = ((f32[8,1,6144]{2,1,0:T(1,128)}), f32[8,1,6144]{2,1,0:T(1,128)S(1)}, u32[]{:S(2)}, u32[]{:S(2)}) async-start(f32[8,1,6144]{2,1,0:T(1,128)} %all_to_all.43), calls=%async_computation.4 | async-start | bytes 393216 | tf_op jit(solution)/shard_map/all_to_all | solution.py:137
  102.1 0.9 fusion.9
  103.8 13.1 %all-to-all-done.4 = f32[8,1,6144]{2,1,0:T(1,128)S(1)} async-done(((f32[8,1,6144]{2,1,0:T(1,128)}), f32[8,1,6144]{2,1,0:T(1,128)S(1)}, u32[]{:S(2)}, u32[]{:S(2)}) %all-to-all-start.4) | async-done | bytes 196640 | tf_op jit(solution)/shard_map/all_to_all | solution.py:137
  117.5 8.0 %all_to_all.56 = f32[2,1,10240]{2,1,0:T(1,128)S(1)} all-to-all(f32[2,1,10240]{2,1,0:T(1,128)S(1)} %all_to_all.46), channel_id=1, replica_groups=mesh['y'=4,'zh'=2,'x'=4,'c'=2,'zl'=8] {'c'}, dimensions={0} | all-to-all | bytes 163840 | tf_op jit(solution)/shard_map/all_to_all | solution.py:137
  126.4 0.7 copy.135
  127.1 0.7 copy.134
  (113 shorter events, 13.9 us)
Async XLA Ops:
  0.6 70.6 %copy-start = (bf16[128,256]{1,0:T(8,128)(2,1)S(1)}, bf16[128,256]{1,0:T(8,128)(2,1)}, u32[]{:S(2)}) copy-start(bf16[128,256]{1,0:T(8,128)(2,1)} %param.13) | copy-start | bytes 196612
  7.5 28.0 %all-to-all-start = ((bf16[16,2,2568]{2,1,0:T(2,128)(2,1)}), bf16[16,2,2568]{2,1,0:T(2,128)(2,1)S(1)}, u32[]{:S(2)}, u32[]{:S(2)}) async-start(bf16[16,2,2568]{2,1,0:T(2,128)(2,1)} %reshape.321), calls=%async_computation | async-start | bytes 344064 | tf_op jit(solution)/shard_map/all_to_all | solution.py:188
  45.4 24.8 %all-to-all-start.2 = ((bf16[16,2,2,8,1026]{4,3,2,1,0:T(8,128)(2,1)}), bf16[16,2,2,8,1026]{4,3,2,1,0:T(8,128)(2,1)S(1)}, u32[]{:S(2)}, u32[]{:S(2)}) async-start(bf16[16,2,2,8,1026]{4,3,2,1,0:T(8,128)(2,1)} %broadcast_in_dim.85), calls=%async_computation.2 | async-start | bytes 2359296 | tf_op jit(solution)/shard_map/all_to_all | solution.py:20
  71.1 9.2 %copy-start.1 = (bf16[512,512]{0,1:T(8,128)(2,1)}, bf16[512,512]{0,1:T(8,128)(2,1)S(1)}, u32[]{:S(2)}) copy-start(bf16[512,512]{0,1:T(8,128)(2,1)S(1)} %copy.128) | copy-start | bytes 1572868
  71.1 0.9 copy-start.4
  75.4 11.4 %all-to-all-start.3 = ((f32[4,1,34816]{2,1,0:T(1,128)}), f32[4,1,34816]{2,1,0:T(1,128)}, u32[]{:S(2)}, u32[]{:S(2)}) async-start(f32[4,1,34816]{2,1,0:T(1,128)} %copy.124), calls=%async_computation.3 | async-start | bytes 1114112 | tf_op jit(solution)/shard_map/all_to_all | solution.py:137
  80.3 0.8 copy-start.3
  93.6 8.5 %copy-start.2 = (bf16[512,512]{0,1:T(8,128)(2,1)S(1)}, bf16[512,512]{0,1:T(8,128)(2,1)}, u32[]{:S(2)}) copy-start(bf16[512,512]{0,1:T(8,128)(2,1)} %copy-done.1) | copy-start | bytes 1572868
  94.4 22.4 %all-to-all-start.4 = ((f32[8,1,6144]{2,1,0:T(1,128)}), f32[8,1,6144]{2,1,0:T(1,128)S(1)}, u32[]{:S(2)}, u32[]{:S(2)}) async-start(f32[8,1,6144]{2,1,0:T(1,128)} %all_to_all.43), calls=%async_computation.4 | async-start | bytes 393216 | tf_op jit(solution)/shard_map/all_to_all | solution.py:137

commit v12 on v10

--- a/solution.py
+++ b/solution.py
@@ -118,7 +118,7 @@
     return x.reshape(-1, *x.shape[5:])
 
 
-MERGE_GROUPS = ("y", ("zh", "x", "c"))
+MERGE_GROUPS = (("y", "zh"), "x", "c")
 
 
 def merged_with_dq(row_max, row_sum, partial_dq):

time: 134 us -> 136 us (1.015)
  waiting for transfers between devices: 60.8 us -> 69.7 us
  local copies, waits for them, and re-layouts: 18.7 us -> 11.2 us
  blocking collectives: 5.7 us -> 9.37 us
  other arithmetic: 9.95 us -> 7.07 us
    all_to_all x2, waiting for transfers between devices: 26.9 us -> 35.7 us  [merged_with_dq(): got = lax.all_to_all(send, axis, 0, 0, tiled=True)]
    all_to_all x0 -> x1, blocking collectives: none -> 3.75 us  [merged_with_dq(): got = lax.all_to_all(send, axis, 0, 0, tiled=True)]
    mul x4 -> x5, local copies, waits for them, and re-layouts: 4.07 us -> 0.5 us  [merged_with_dq(): partial_dq = jnp.sum(dq_rescale[..., None] * got_dq, axis=0)]
    unnamed x20 -> x16, local copies, waits for them, and re-layouts: 5.27 us -> 3.24 us
    reduce_sum x2 -> x3, other arithmetic: 2.11 us -> 0.25 us  [merged_with_dq(): partial_dq = jnp.sum(dq_rescale[..., None] * got_dq, axis=0)]
    reshape x2 -> x3, local copies, waits for them, and re-layouts: 2.14 us -> 0.46 us  [merged_with_dq(): partial_dq.reshape(size, -1)]
    unnamed x6 -> x7, other arithmetic: 2.93 us -> 2.94 us
where the time goes in v12:
time: 136 us; the launch traced here: 134 us
  waiting for transfers between devices  69.7 us (51%)
  starting transfers between devices  32.1 us (24%)
  local copies, waits for them, and re-layouts  11.2 us (8%)
  blocking collectives  9.37 us (7%)
  other arithmetic  7.07 us (5%)
  matrix products  3.12 us (2%)
  between operations  1.84 us (1%)
    all_to_all x2, waiting for transfers between devices, merged_with_dq(): got = lax.all_to_all(send, axis, 0, 0, tiled=True)  35.7 us
    all_to_all x1, waiting for transfers between devices, from_everyone(): return lax.all_to_all(copies, axis, split_axis=0, concat_axis=0, tiled=True)  19 us
    all_to_all x1, starting transfers between devices, shards(): lax.all_to_all(outgoing.reshape(far_pairs * head_groups, -1), ('zh', 'zl'...  15.2 us
    all_to_all x1, waiting for transfers between devices, shards(): lax.all_to_all(outgoing.reshape(far_pairs * head_groups, -1), ('zh', 'zl'...  14.9 us
    all_to_all x2, starting transfers between devices, merged_with_dq(): got = lax.all_to_all(send, axis, 0, 0, tiled=True)  9.82 us
    all_to_all x1, starting transfers between devices, from_everyone(): return lax.all_to_all(copies, axis, split_axis=0, concat_axis=0, tiled=True)  7.03 us
    all_to_all x1, blocking collectives, from_everyone(): return lax.all_to_all(copies, axis, split_axis=0, concat_axis=0, tiled=True)  3.81 us
    all_to_all x1, blocking collectives, merged_with_dq(): got = lax.all_to_all(send, axis, 0, 0, tiled=True)  3.75 us
  transfers between devices with their start and end apart: 4, of which 4 were waited for; matrix products, arithmetic and copies ran while one was open for 2% of the time, Pallas kernels for 0%

profile of v12, /device:TPU:32, one launch (start us, length us, event | category | flops | bytes accessed | tf_op | source)
XLA Modules:
  0.0 134.4 jit_solution(16578770041087466482)
XLA Ops:
  0.6 0.8 bitcast_reduce_fusion.2
  1.6 0.7 reduce.11
  2.3 0.7 reduce.12
  3.1 0.7 reduce.13
  3.8 0.7 reduce.14
  4.5 0.7 pad_maximum_fusion.7
  5.9 0.7 reduce.15
  6.7 0.9 reshape.342
  7.5 15.2 %all-to-all-start = ((bf16[16,2,2568]{2,1,0:T(2,128)(2,1)}), bf16[16,2,2568]{2,1,0:T(2,128)(2,1)S(1)}, u32[]{:S(2)}, u32[]{:S(2)}) async-start(bf16[16,2,2568]{2,1,0:T(2,128)(2,1)} %reshape.342), calls=%async_computation | async-start | bytes 344064 | tf_op jit(solution)/shard_map/all_to_all | solution.py:183
  22.7 14.9 %all-to-all-done = bf16[16,2,2568]{2,1,0:T(2,128)(2,1)S(1)} async-done(((bf16[16,2,2568]{2,1,0:T(2,128)(2,1)}), bf16[16,2,2568]{2,1,0:T(2,128)(2,1)S(1)}, u32[]{:S(2)}, u32[]{:S(2)}) %all-to-all-start) | async-done | bytes 164384 | tf_op jit(solution)/shard_map/all_to_all | solution.py:183
  38.3 3.8 %all_to_all.55 = bf16[2,2,8,1538]{3,2,1,0:T(8,128)(2,1)S(1)} all-to-all(bf16[2,2,8,1538]{3,2,1,0:T(8,128)(2,1)S(1)} %broadcast_in_dim.84), channel_id=1, replica_groups=mesh['y'=4,'zh'=2,'x'=4,'c'=2,'zl'=8] {'c'}, dimensions={0} | all-to-all | bytes 196864 | tf_op jit(solution)/shard_map/all_to_all | solution.py:20
  42.3 1.1 broadcast_in_dim.85
  43.4 7.0 %all-to-all-start.2 = ((bf16[16,2,2,8,1026]{4,3,2,1,0:T(8,128)(2,1)}), bf16[16,2,2,8,1026]{4,3,2,1,0:T(8,128)(2,1)S(1)}, u32[]{:S(2)}, u32[]{:S(2)}) async-start(bf16[16,2,2,8,1026]{4,3,2,1,0:T(8,128)(2,1)} %broadcast_in_dim.85), calls=%async_computation.2 | async-start | bytes 2359296 | tf_op jit(solution)/shard_map/all_to_all | solution.py:20
  51.1 19.0 %all-to-all-done.2 = bf16[16,2,2,8,1026]{4,3,2,1,0:T(8,128)(2,1)S(1)} async-done(((bf16[16,2,2,8,1026]{4,3,2,1,0:T(8,128)(2,1)}), bf16[16,2,2,8,1026]{4,3,2,1,0:T(8,128)(2,1)S(1)}, u32[]{:S(2)}, u32[]{:S(2)}) %all-to-all-start.2) | async-done | bytes 1050656 | tf_op jit(solution)/shard_map/all_to_all | solution.py:20
  73.7 1.4 %copy.124 = f32[8,1,18432]{2,1,0:T(1,128)} copy(f32[8,1,18432]{2,0,1:T(8,128)S(1)} %maximum_bitcast_fusion) | data formatting | bytes 1179648 | tf_op jit(solution)/shard_map/all_to_all | solution.py:135
  75.1 5.1 %all-to-all-start.3 = ((f32[8,1,18432]{2,1,0:T(1,128)}), f32[8,1,18432]{2,1,0:T(1,128)S(1)}, u32[]{:S(2)}, u32[]{:S(2)}) async-start(f32[8,1,18432]{2,1,0:T(1,128)} %copy.124), calls=%async_computation.3 | async-start | bytes 1179648 | tf_op jit(solution)/shard_map/all_to_all | solution.py:135
  82.2 1.8 %all_gather.3 = bf16[2,3,16,128]{3,2,1,0:T(8,128)(2,1)S(1)} all-gather(bf16[1,3,16,128]{3,2,1,0:T(8,128)(2,1)S(1)} %pad_maximum_fusion.6), channel_id=1, replica_groups=mesh['y'=4,'zh'=2,'x'=4,'c'=2,'zl'=8] {'c'}, dimensions={0}, use_global_device_ids=true | all-gather | bytes 36864 | tf_op jit(solution)/shard_map/all_gather | solution.py:268
  84.0 30.5 %all-to-all-done.3 = f32[8,1,18432]{2,1,0:T(1,128)S(1)} async-done(((f32[8,1,18432]{2,1,0:T(1,128)}), f32[8,1,18432]{2,1,0:T(1,128)S(1)}, u32[]{:S(2)}, u32[]{:S(2)}) %all-to-all-start.3) | async-done | bytes 589856 | tf_op jit(solution)/shard_map/all_to_all | solution.py:135
  115.5 0.7 all_to_all.43
  116.1 4.7 %all-to-all-start.4 = ((f32[4,1,6144]{2,1,0:T(1,128)}), f32[4,1,6144]{2,1,0:T(1,128)S(1)}, u32[]{:S(2)}, u32[]{:S(2)}) async-start(f32[4,1,6144]{2,1,0:T(1,128)} %all_to_all.43), calls=%async_computation.4 | async-start | bytes 196608 | tf_op jit(solution)/shard_map/all_to_all | solution.py:135
  121.5 5.2 %all-to-all-done.4 = f32[4,1,6144]{2,1,0:T(1,128)S(1)} async-done(((f32[4,1,6144]{2,1,0:T(1,128)}), f32[4,1,6144]{2,1,0:T(1,128)S(1)}, u32[]{:S(2)}, u32[]{:S(2)}) %all-to-all-start.4) | async-done | bytes 98336 | tf_op jit(solution)/shard_map/all_to_all | solution.py:135
  127.4 3.7 %all_to_all.56 = f32[2,1,4096]{2,1,0:T(1,128)S(1)} all-to-all(f32[2,1,4096]{2,1,0:T(1,128)S(1)} %all_to_all.46), channel_id=1, replica_groups=mesh['y'=4,'zh'=2,'x'=4,'c'=2,'zl'=8] {'c'}, dimensions={0} | all-to-all | bytes 65536 | tf_op jit(solution)/shard_map/all_to_all | solution.py:135
  131.9 0.7 copy.135
  132.7 0.7 copy.134
  (105 shorter events, 10.7 us)
Async XLA Ops:
  0.6 70.6 %copy-start = (bf16[128,256]{1,0:T(8,128)(2,1)S(1)}, bf16[128,256]{1,0:T(8,128)(2,1)}, u32[]{:S(2)}) copy-start(bf16[128,256]{1,0:T(8,128)(2,1)} %param.13) | copy-start | bytes 196612
  7.5 30.2 %all-to-all-start = ((bf16[16,2,2568]{2,1,0:T(2,128)(2,1)}), bf16[16,2,2568]{2,1,0:T(2,128)(2,1)S(1)}, u32[]{:S(2)}, u32[]{:S(2)}) async-start(bf16[16,2,2568]{2,1,0:T(2,128)(2,1)} %reshape.342), calls=%async_computation | async-start | bytes 344064 | tf_op jit(solution)/shard_map/all_to_all | solution.py:183
  43.4 26.7 %all-to-all-start.2 = ((bf16[16,2,2,8,1026]{4,3,2,1,0:T(8,128)(2,1)}), bf16[16,2,2,8,1026]{4,3,2,1,0:T(8,128)(2,1)S(1)}, u32[]{:S(2)}, u32[]{:S(2)}) async-start(bf16[16,2,2,8,1026]{4,3,2,1,0:T(8,128)(2,1)} %broadcast_in_dim.85), calls=%async_computation.2 | async-start | bytes 2359296 | tf_op jit(solution)/shard_map/all_to_all | solution.py:20
  71.1 0.8 copy-start.1
  75.1 39.4 %all-to-all-start.3 = ((f32[8,1,18432]{2,1,0:T(1,128)}), f32[8,1,18432]{2,1,0:T(1,128)S(1)}, u32[]{:S(2)}, u32[]{:S(2)}) async-start(f32[8,1,18432]{2,1,0:T(1,128)} %copy.124), calls=%async_computation.3 | async-start | bytes 1179648 | tf_op jit(solution)/shard_map/all_to_all | solution.py:135
  116.1 10.5 %all-to-all-start.4 = ((f32[4,1,6144]{2,1,0:T(1,128)}), f32[4,1,6144]{2,1,0:T(1,128)S(1)}, u32[]{:S(2)}, u32[]{:S(2)}) async-start(f32[4,1,6144]{2,1,0:T(1,128)} %all_to_all.43), calls=%async_computation.4 | async-start | bytes 196608 | tf_op jit(solution)/shard_map/all_to_all | solution.py:135

commit v13 on v9

--- a/solution.py
+++ b/solution.py
@@ -187,15 +187,18 @@
     self_cols = incoming[:, :, :self_width]
     far_cross = lax.dynamic_index_in_dim(incoming, lax.axis_index("zl"), 1, keepdims=False)
     far_cross = far_cross[:, self_width:].reshape(far_pairs, own_rows, cross_width)
-    first = jnp.concatenate((far_cross, self_cols), axis=2)
-    first = from_everyone(first, "c")
     core = lax.axis_index("c")
-    self_heads = first[..., cross_width:].reshape(*first.shape[:-1], 4, local_heads, HEAD_DIM)
-    self_mine = lax.dynamic_index_in_dim(self_heads, core, axis=4, keepdims=False)
-    rest = jnp.concatenate(
-        (first[..., :cross_width], self_mine.reshape(*first.shape[:-1], -1)), axis=-1
-    )
-    gathered = gather_seq(rest, GATHER_ORDER[2:][::-1])
+    cores = lax.axis_size("c")
+    self_heads = self_cols.reshape(far_pairs, head_groups, 4, local_heads, HEAD_DIM)
+    per_core = jnp.moveaxis(self_heads, 3, 0).reshape(cores, far_pairs, head_groups, -1)
+    chunks = jnp.concatenate(
+        (jnp.broadcast_to(far_cross[None], (cores, *far_cross.shape)), per_core), axis=-1
+    )
+    plane = lax.axis_size("y") * lax.axis_size("x")
+    sent = jnp.broadcast_to(chunks[None], (plane, *chunks.shape)).reshape(plane * cores, *chunks.shape[1:])
+    got = lax.all_to_all(sent, ("y", "x", "c"), 0, 0, tiled=True)
+    got = got.reshape(lax.axis_size("y"), lax.axis_size("x"), cores, *chunks.shape[1:])
+    gathered = jnp.transpose(got, (0, 3, 1, 2, 4, 5)).reshape(-1, got.shape[-1])
     query_all = gathered[:, : cross_q.shape[1]]
     grad_all = gathered[:, cross_q.shape[1] : 2 * cross_q.shape[1]]
     dots_all = gathered[:, 2 * cross_q.shape[1] : cross_width]

time: 124 us -> 121 us (0.976)
  blocking collectives: 19.3 us -> 10.6 us
  starting transfers between devices: 33.3 us -> 38.4 us
  waiting for transfers between devices: 43.1 us -> 44.4 us
    all_to_all x1 -> x0, blocking collectives: 7.95 us -> none  [from_everyone(): return lax.all_to_all(copies, axis, split_axis=0, concat_axis=0, tiled=True)]
    all_to_all x1, starting transfers between devices: 6.75 us -> 11.6 us  [shards(): got = lax.all_to_all(sent, ('y', 'x', 'c'), 0, 0, tiled=True)]
    all_to_all x2, waiting for transfers between devices: 13.5 us -> 15.2 us  [merged_with_dq(): got = lax.all_to_all(send, axis, 0, 0, tiled=True)]
where the time goes in v13:
time: 121 us; the launch traced here: 120 us
  waiting for transfers between devices  44.4 us (37%)
  starting transfers between devices  38.4 us (32%)
  local copies, waits for them, and re-layouts  12.2 us (10%)
  blocking collectives  10.6 us (9%)
  other arithmetic  7.31 us (6%)
  matrix products  5.59 us (5%)
  between operations  1.88 us (2%)
    all_to_all x1, waiting for transfers between devices, shards(): got = lax.all_to_all(sent, ('y', 'x', 'c'), 0, 0, tiled=True)  17 us
    all_to_all x1, starting transfers between devices, shards(): lax.all_to_all(outgoing.reshape(far_pairs * head_groups, -1), ('zh', 'zl'...  15.7 us
    all_to_all x2, waiting for transfers between devices, merged_with_dq(): got = lax.all_to_all(send, axis, 0, 0, tiled=True)  15.2 us
    all_to_all x1, waiting for transfers between devices, shards(): lax.all_to_all(outgoing.reshape(far_pairs * head_groups, -1), ('zh', 'zl'...  12.2 us
    all_to_all x1, starting transfers between devices, shards(): got = lax.all_to_all(sent, ('y', 'x', 'c'), 0, 0, tiled=True)  11.6 us
    all_to_all x2, starting transfers between devices, merged_with_dq(): got = lax.all_to_all(send, axis, 0, 0, tiled=True)  11.1 us
    all_to_all x1, blocking collectives, merged_with_dq(): got = lax.all_to_all(send, axis, 0, 0, tiled=True)  7.95 us
    unnamed x20, local copies, waits for them, and re-layouts  3.37 us
  transfers between devices with their start and end apart: 4, of which 4 were waited for; matrix products, arithmetic and copies ran while one was open for 4% of the time, Pallas kernels for 0%

profile of v13, /device:TPU:1, one launch (start us, length us, event | category | flops | bytes accessed | tf_op | source)
XLA Modules:
  0.0 120.3 jit_solution(11199683067377052094)
XLA Ops:
  0.6 0.8 bitcast_reduce_fusion.2
  1.6 0.7 reduce.11
  2.3 0.7 reduce.12
  3.1 0.7 reduce.13
  3.8 0.7 reduce.14
  6.7 0.9 reshape.343
  7.5 15.7 %all-to-all-start = ((bf16[16,2,2568]{2,1,0:T(2,128)(2,1)}), bf16[16,2,2568]{2,1,0:T(2,128)(2,1)S(1)}, u32[]{:S(2)}, u32[]{:S(2)}) async-start(bf16[16,2,2568]{2,1,0:T(2,128)(2,1)} %reshape.343), calls=%async_computation | async-start | bytes 344064 | tf_op jit(solution)/shard_map/all_to_all | solution.py:183
  23.3 12.2 %all-to-all-done = bf16[16,2,2568]{2,1,0:T(2,128)(2,1)S(1)} async-done(((bf16[16,2,2568]{2,1,0:T(2,128)(2,1)}), bf16[16,2,2568]{2,1,0:T(2,128)(2,1)S(1)}, u32[]{:S(2)}, u32[]{:S(2)}) %all-to-all-start) | async-done | bytes 164384 | tf_op jit(solution)/shard_map/all_to_all | solution.py:183
  36.2 1.1 broadcast_in_dim.93
  37.3 11.6 %all-to-all-start.1 = ((bf16[32,2,8,1026]{3,2,1,0:T(8,128)(2,1)}), bf16[32,2,8,1026]{3,2,1,0:T(8,128)(2,1)S(1)}, u32[]{:S(2)}, u32[]{:S(2)}) async-start(bf16[32,2,8,1026]{3,2,1,0:T(8,128)(2,1)} %bitcast.8), calls=%async_computation.1 | async-start | bytes 2359296 | tf_op jit(solution)/shard_map/all_to_all | solution.py:199
  49.5 17.0 %all-to-all-done.1 = bf16[32,2,8,1026]{3,2,1,0:T(8,128)(2,1)S(1)} async-done(((bf16[32,2,8,1026]{3,2,1,0:T(8,128)(2,1)}), bf16[32,2,8,1026]{3,2,1,0:T(8,128)(2,1)S(1)}, u32[]{:S(2)}, u32[]{:S(2)}) %all-to-all-start.1) | async-done | bytes 1050656 | tf_op jit(solution)/shard_map/all_to_all | solution.py:199
  70.4 1.4 %copy.121 = f32[4,1,34816]{2,1,0:T(1,128)} copy(f32[4,1,34816]{2,0,1:T(4,128)S(1)} %maximum_bitcast_fusion) | data formatting | bytes 1114112 | tf_op jit(solution)/shard_map/all_to_all | solution.py:135
  71.7 3.5 %all-to-all-start.2 = ((f32[4,1,34816]{2,1,0:T(1,128)}), f32[4,1,34816]{2,1,0:T(1,128)S(1)}, u32[]{:S(2)}, u32[]{:S(2)}) async-start(f32[4,1,34816]{2,1,0:T(1,128)} %copy.121), calls=%async_computation.2 | async-start | bytes 1114112 | tf_op jit(solution)/shard_map/all_to_all | solution.py:135
  76.4 1.2 fusion.3
  77.6 5.6 %all-to-all-done.2 = f32[4,1,34816]{2,1,0:T(1,128)S(1)} async-done(((f32[4,1,34816]{2,1,0:T(1,128)}), f32[4,1,34816]{2,1,0:T(1,128)S(1)}, u32[]{:S(2)}, u32[]{:S(2)}) %all-to-all-start.2) | async-done | bytes 557088 | tf_op jit(solution)/shard_map/all_to_all | solution.py:135
  85.3 0.8 all_to_all.39
  86.1 7.6 %all-to-all-start.3 = ((f32[8,1,6144]{2,1,0:T(1,128)}), f32[8,1,6144]{2,1,0:T(1,128)S(1)}, u32[]{:S(2)}, u32[]{:S(2)}) async-start(f32[8,1,6144]{2,1,0:T(1,128)} %all_to_all.39), calls=%async_computation.3 | async-start | bytes 393216 | tf_op jit(solution)/shard_map/all_to_all | solution.py:135
  93.7 0.9 fusion.8
  94.6 1.2 %fusion.7 = bf16[1,1,16,128]{3,2,1,0:T(8,128)(2,1)S(1)} fusion(bf16[512,512]{0,1:T(8,128)(2,1)} %fusion.3, s32[]{:T(128)S(6)} %select_n.51, bf16[4,512,128]{1,2,0:T(8,128)(2,1)S(1)} %bitcast.218), kind=kOutput, calls=%fused_computation.18 | convolution fusion | flops 2099200 | bytes 266244 | tf_op jit(solution)/shard_map/hqk,khd->qhd/dot_general | solution.py:103
  95.8 2.6 %all_gather.3 = bf16[2,3,16,128]{3,2,1,0:T(8,128)(2,1)S(1)} all-gather(bf16[1,3,16,128]{3,2,1,0:T(8,128)(2,1)S(1)} %pad_maximum_fusion.5), channel_id=1, replica_groups=mesh['y'=4,'zh'=2,'x'=4,'c'=2,'zl'=8] {'c'}, dimensions={0}, use_global_device_ids=true | all-gather | bytes 36864 | tf_op jit(solution)/shard_map/all_gather | solution.py:271
  99.0 9.6 %all-to-all-done.3 = f32[8,1,6144]{2,1,0:T(1,128)S(1)} async-done(((f32[8,1,6144]{2,1,0:T(1,128)}), f32[8,1,6144]{2,1,0:T(1,128)S(1)}, u32[]{:S(2)}, u32[]{:S(2)}) %all-to-all-start.3) | async-done | bytes 196640 | tf_op jit(solution)/shard_map/all_to_all | solution.py:135
  109.2 7.9 %all_to_all.50 = f32[2,1,4096]{2,1,0:T(1,128)S(1)} all-to-all(f32[2,1,4096]{2,1,0:T(1,128)S(1)} %all_to_all.42), channel_id=1, replica_groups=mesh['y'=4,'zh'=2,'x'=4,'c'=2,'zl'=8] {'c'}, dimensions={0} | all-to-all | bytes 65536 | tf_op jit(solution)/shard_map/all_to_all | solution.py:135
  117.9 0.7 copy.132
  118.7 0.7 copy.131
  (105 shorter events, 12.5 us)
Async XLA Ops:
  0.6 67.0 %copy-start = (bf16[128,256]{1,0:T(8,128)(2,1)S(1)}, bf16[128,256]{1,0:T(8,128)(2,1)}, u32[]{:S(2)}) copy-start(bf16[128,256]{1,0:T(8,128)(2,1)} %param.13) | copy-start | bytes 196612
  7.5 28.0 %all-to-all-start = ((bf16[16,2,2568]{2,1,0:T(2,128)(2,1)}), bf16[16,2,2568]{2,1,0:T(2,128)(2,1)S(1)}, u32[]{:S(2)}, u32[]{:S(2)}) async-start(bf16[16,2,2568]{2,1,0:T(2,128)(2,1)} %reshape.343), calls=%async_computation | async-start | bytes 344064 | tf_op jit(solution)/shard_map/all_to_all | solution.py:183
  37.3 29.3 %all-to-all-start.1 = ((bf16[32,2,8,1026]{3,2,1,0:T(8,128)(2,1)}), bf16[32,2,8,1026]{3,2,1,0:T(8,128)(2,1)S(1)}, u32[]{:S(2)}, u32[]{:S(2)}) async-start(bf16[32,2,8,1026]{3,2,1,0:T(8,128)(2,1)} %bitcast.8), calls=%async_computation.1 | async-start | bytes 2359296 | tf_op jit(solution)/shard_map/all_to_all | solution.py:199
  67.5 8.9 %copy-start.1 = (bf16[512,512]{0,1:T(8,128)(2,1)}, bf16[512,512]{0,1:T(8,128)(2,1)S(1)}, u32[]{:S(2)}) copy-start(bf16[512,512]{0,1:T(8,128)(2,1)S(1)} %copy.129) | copy-start | bytes 1572868
  67.5 0.9 copy-start.3
  71.7 11.4 %all-to-all-start.2 = ((f32[4,1,34816]{2,1,0:T(1,128)}), f32[4,1,34816]{2,1,0:T(1,128)S(1)}, u32[]{:S(2)}, u32[]{:S(2)}) async-start(f32[4,1,34816]{2,1,0:T(1,128)} %copy.121), calls=%async_computation.2 | async-start | bytes 1114112 | tf_op jit(solution)/shard_map/all_to_all | solution.py:135
  84.8 8.9 %copy-start.2 = (bf16[512,512]{0,1:T(8,128)(2,1)S(1)}, bf16[512,512]{0,1:T(8,128)(2,1)}, u32[]{:S(2)}) copy-start(bf16[512,512]{0,1:T(8,128)(2,1)} %copy-done.1) | copy-start | bytes 1572868
  86.1 22.5 %all-to-all-start.3 = ((f32[8,1,6144]{2,1,0:T(1,128)}), f32[8,1,6144]{2,1,0:T(1,128)S(1)}, u32[]{:S(2)}, u32[]{:S(2)}) async-start(f32[8,1,6144]{2,1,0:T(1,128)} %all_to_all.39), calls=%async_computation.3 | async-start | bytes 393216 | tf_op jit(solution)/shard_map/all_to_all | solution.py:135

commit v14 on v13

--- a/solution.py
+++ b/solution.py
@@ -118,7 +118,7 @@
     return x.reshape(-1, *x.shape[5:])
 
 
-MERGE_GROUPS = ("y", ("zh", "x"), "c")
+MERGE_GROUPS = (("y", "zh"), ("x", "c"))
 
 
 def merged_with_dq(row_max, row_sum, partial_dq):

time: 121 us -> 128 us (1.058)
  the two profiles are of different devices: /device:TPU:1 before, /device:TPU:32 now
where the time goes in v14:
time: 128 us; the launch traced here: 127 us
  waiting for transfers between devices  71.9 us (56%)
  starting transfers between devices  30.7 us (24%)
  local copies, waits for them, and re-layouts  10.7 us (8%)
  other arithmetic  6.87 us (5%)
  matrix products  3.11 us (2%)
  blocking collectives  1.82 us (1%)
  between operations  1.73 us (1%)
    all_to_all x2, waiting for transfers between devices, merged_with_dq(): got = lax.all_to_all(send, axis, 0, 0, tiled=True)  38.6 us
    all_to_all x1, waiting for transfers between devices, shards(): got = lax.all_to_all(sent, ('y', 'x', 'c'), 0, 0, tiled=True)  18.3 us
    all_to_all x1, starting transfers between devices, shards(): lax.all_to_all(outgoing.reshape(far_pairs * head_groups, -1), ('zh', 'zl'...  15.2 us
    all_to_all x1, waiting for transfers between devices, shards(): lax.all_to_all(outgoing.reshape(far_pairs * head_groups, -1), ('zh', 'zl'...  14.9 us
    all_to_all x2, starting transfers between devices, merged_with_dq(): got = lax.all_to_all(send, axis, 0, 0, tiled=True)  8.2 us
    all_to_all x1, starting transfers between devices, shards(): got = lax.all_to_all(sent, ('y', 'x', 'c'), 0, 0, tiled=True)  7.32 us
    unnamed x14, local copies, waits for them, and re-layouts  3.25 us
    unnamed x6, other arithmetic  2.93 us
  transfers between devices with their start and end apart: 4, of which 4 were waited for; matrix products, arithmetic and copies ran while one was open for 2% of the time, Pallas kernels for 0%

profile of v14, /device:TPU:32, one launch (start us, length us, event | category | flops | bytes accessed | tf_op | source)
XLA Modules:
  0.0 126.8 jit_solution(4974016126530690562)
XLA Ops:
  0.6 0.8 bitcast_reduce_fusion
  1.6 0.7 reduce.9
  2.3 0.7 reduce.10
  3.1 0.7 reduce.11
  3.8 0.7 reduce.12
  4.5 0.7 pad_maximum_fusion.5
  5.9 0.7 reduce.13
  6.7 0.9 reshape.324
  7.5 15.2 %all-to-all-start = ((bf16[16,2,2568]{2,1,0:T(2,128)(2,1)}), bf16[16,2,2568]{2,1,0:T(2,128)(2,1)S(1)}, u32[]{:S(2)}, u32[]{:S(2)}) async-start(bf16[16,2,2568]{2,1,0:T(2,128)(2,1)} %reshape.324), calls=%async_computation | async-start | bytes 344064 | tf_op jit(solution)/shard_map/all_to_all | solution.py:183
  22.7 14.9 %all-to-all-done = bf16[16,2,2568]{2,1,0:T(2,128)(2,1)S(1)} async-done(((bf16[16,2,2568]{2,1,0:T(2,128)(2,1)}), bf16[16,2,2568]{2,1,0:T(2,128)(2,1)S(1)}, u32[]{:S(2)}, u32[]{:S(2)}) %all-to-all-start) | async-done | bytes 164384 | tf_op jit(solution)/shard_map/all_to_all | solution.py:183
  38.3 1.1 broadcast_in_dim.82
  39.4 7.3 %all-to-all-start.1 = ((bf16[32,2,8,1026]{3,2,1,0:T(8,128)(2,1)}), bf16[32,2,8,1026]{3,2,1,0:T(8,128)(2,1)S(1)}, u32[]{:S(2)}, u32[]{:S(2)}) async-start(bf16[32,2,8,1026]{3,2,1,0:T(8,128)(2,1)} %bitcast.8), calls=%async_computation.1 | async-start | bytes 2359296 | tf_op jit(solution)/shard_map/all_to_all | solution.py:199
  47.4 18.3 %all-to-all-done.1 = bf16[32,2,8,1026]{3,2,1,0:T(8,128)(2,1)S(1)} async-done(((bf16[32,2,8,1026]{3,2,1,0:T(8,128)(2,1)}), bf16[32,2,8,1026]{3,2,1,0:T(8,128)(2,1)S(1)}, u32[]{:S(2)}, u32[]{:S(2)}) %all-to-all-start.1) | async-done | bytes 1050656 | tf_op jit(solution)/shard_map/all_to_all | solution.py:199
  69.3 1.4 %copy.109 = f32[8,1,18432]{2,1,0:T(1,128)} copy(f32[8,1,18432]{2,0,1:T(8,128)S(1)} %maximum_bitcast_fusion) | data formatting | bytes 1179648 | tf_op jit(solution)/shard_map/all_to_all | solution.py:135
  70.7 4.8 %all-to-all-start.2 = ((f32[8,1,18432]{2,1,0:T(1,128)}), f32[8,1,18432]{2,1,0:T(1,128)S(1)}, u32[]{:S(2)}, u32[]{:S(2)}) async-start(f32[8,1,18432]{2,1,0:T(1,128)} %copy.109), calls=%async_computation.2 | async-start | bytes 1179648 | tf_op jit(solution)/shard_map/all_to_all | solution.py:135
  77.5 1.8 %all_gather.3 = bf16[2,3,16,128]{3,2,1,0:T(8,128)(2,1)S(1)} all-gather(bf16[1,3,16,128]{3,2,1,0:T(8,128)(2,1)S(1)} %pad_maximum_fusion.4), channel_id=1, replica_groups=mesh['y'=4,'zh'=2,'x'=4,'c'=2,'zl'=8] {'c'}, dimensions={0}, use_global_device_ids=true | all-gather | bytes 36864 | tf_op jit(solution)/shard_map/all_gather | solution.py:271
  79.3 33.2 %all-to-all-done.2 = f32[8,1,18432]{2,1,0:T(1,128)S(1)} async-done(((f32[8,1,18432]{2,1,0:T(1,128)}), f32[8,1,18432]{2,1,0:T(1,128)S(1)}, u32[]{:S(2)}, u32[]{:S(2)}) %all-to-all-start.2) | async-done | bytes 589856 | tf_op jit(solution)/shard_map/all_to_all | solution.py:135
  113.4 0.7 all_to_all.31
  114.2 3.4 %all-to-all-start.3 = ((f32[8,1,4096]{2,1,0:T(1,128)}), f32[8,1,4096]{2,1,0:T(1,128)S(1)}, u32[]{:S(2)}, u32[]{:S(2)}) async-start(f32[8,1,4096]{2,1,0:T(1,128)} %all_to_all.31), calls=%async_computation.3 | async-start | bytes 262144 | tf_op jit(solution)/shard_map/all_to_all | solution.py:135
  117.6 0.6 slice_bitcast_fusion.11
  118.2 5.4 %all-to-all-done.3 = f32[8,1,4096]{2,1,0:T(1,128)S(1)} async-done(((f32[8,1,4096]{2,1,0:T(1,128)}), f32[8,1,4096]{2,1,0:T(1,128)S(1)}, u32[]{:S(2)}, u32[]{:S(2)}) %all-to-all-start.3) | async-done | bytes 131104 | tf_op jit(solution)/shard_map/all_to_all | solution.py:135
  124.5 0.7 copy.117
  125.2 0.7 copy.116
  126.2 0.7 fusion.42
  (82 shorter events, 8.6 us)
Async XLA Ops:
  0.6 66.2 %copy-start = (bf16[128,256]{1,0:T(8,128)(2,1)S(1)}, bf16[128,256]{1,0:T(8,128)(2,1)}, u32[]{:S(2)}) copy-start(bf16[128,256]{1,0:T(8,128)(2,1)} %param.13) | copy-start | bytes 196612
  7.5 30.2 %all-to-all-start = ((bf16[16,2,2568]{2,1,0:T(2,128)(2,1)}), bf16[16,2,2568]{2,1,0:T(2,128)(2,1)S(1)}, u32[]{:S(2)}, u32[]{:S(2)}) async-start(bf16[16,2,2568]{2,1,0:T(2,128)(2,1)} %reshape.324), calls=%async_computation | async-start | bytes 344064 | tf_op jit(solution)/shard_map/all_to_all | solution.py:183
  39.4 26.3 %all-to-all-start.1 = ((bf16[32,2,8,1026]{3,2,1,0:T(8,128)(2,1)}), bf16[32,2,8,1026]{3,2,1,0:T(8,128)(2,1)S(1)}, u32[]{:S(2)}, u32[]{:S(2)}) async-start(bf16[32,2,8,1026]{3,2,1,0:T(8,128)(2,1)} %bitcast.8), calls=%async_computation.1 | async-start | bytes 2359296 | tf_op jit(solution)/shard_map/all_to_all | solution.py:199
  66.7 0.8 copy-start.1
  70.7 41.8 %all-to-all-start.2 = ((f32[8,1,18432]{2,1,0:T(1,128)}), f32[8,1,18432]{2,1,0:T(1,128)S(1)}, u32[]{:S(2)}, u32[]{:S(2)}) async-start(f32[8,1,18432]{2,1,0:T(1,128)} %copy.109), calls=%async_computation.2 | async-start | bytes 1179648 | tf_op jit(solution)/shard_map/all_to_all | solution.py:135
  114.2 9.4 %all-to-all-start.3 = ((f32[8,1,4096]{2,1,0:T(1,128)}), f32[8,1,4096]{2,1,0:T(1,128)S(1)}, u32[]{:S(2)}, u32[]{:S(2)}) async-start(f32[8,1,4096]{2,1,0:T(1,128)} %all_to_all.31), calls=%async_computation.3 | async-start | bytes 262144 | tf_op jit(solution)/shard_map/all_to_all | solution.py:135

commit v15 on v14

--- a/solution.py
+++ b/solution.py
@@ -118,7 +118,7 @@
     return x.reshape(-1, *x.shape[5:])
 
 
-MERGE_GROUPS = (("y", "zh"), ("x", "c"))
+MERGE_GROUPS = ("y", "zh", ("x", "c"))
 
 
 def merged_with_dq(row_max, row_sum, partial_dq):

time: 128 us -> 124 us (0.969)
  the two profiles are of different devices: /device:TPU:32 before, /device:TPU:1 now
where the time goes in v15:
time: 124 us; the launch traced here: 123 us
  waiting for transfers between devices  48.4 us (39%)
  starting transfers between devices  42.7 us (34%)
  local copies, waits for them, and re-layouts  14 us (11%)
  other arithmetic  7.53 us (6%)
  blocking collectives  4.56 us (4%)
  matrix products  4 us (3%)
  between operations  1.89 us (2%)
    all_to_all x3, waiting for transfers between devices, merged_with_dq(): got = lax.all_to_all(send, axis, 0, 0, tiled=True)  19.1 us
    all_to_all x1, waiting for transfers between devices, shards(): got = lax.all_to_all(sent, ('y', 'x', 'c'), 0, 0, tiled=True)  17 us
    all_to_all x1, starting transfers between devices, shards(): lax.all_to_all(outgoing.reshape(far_pairs * head_groups, -1), ('zh', 'zl'...  15.7 us
    all_to_all x3, starting transfers between devices, merged_with_dq(): got = lax.all_to_all(send, axis, 0, 0, tiled=True)  15.4 us
    all_to_all x1, waiting for transfers between devices, shards(): lax.all_to_all(outgoing.reshape(far_pairs * head_groups, -1), ('zh', 'zl'...  12.2 us
    all_to_all x1, starting transfers between devices, shards(): got = lax.all_to_all(sent, ('y', 'x', 'c'), 0, 0, tiled=True)  11.6 us
    all_gather x1, blocking collectives, shards(): lax.all_gather(head_results.reshape(3, chip_rows, HEAD_DIM), 'c', axis=0)  4.56 us
    unnamed x20, local copies, waits for them, and re-layouts  4.23 us
  transfers between devices with their start and end apart: 5, of which 5 were waited for; matrix products, arithmetic and copies ran while one was open for 3% of the time, Pallas kernels for 0%

profile of v15, /device:TPU:1, one launch (start us, length us, event | category | flops | bytes accessed | tf_op | source)
XLA Modules:
  0.0 123.1 jit_solution(10627056143538289332)
XLA Ops:
  0.6 0.8 bitcast_reduce_fusion.2
  2.3 0.7 reduce.12
  3.1 0.7 reduce.13
  3.8 0.7 reduce.14
  6.7 0.9 reshape.343
  7.5 15.7 %all-to-all-start = ((bf16[16,2,2568]{2,1,0:T(2,128)(2,1)}), bf16[16,2,2568]{2,1,0:T(2,128)(2,1)S(1)}, u32[]{:S(2)}, u32[]{:S(2)}) async-start(bf16[16,2,2568]{2,1,0:T(2,128)(2,1)} %reshape.343), calls=%async_computation | async-start | bytes 344064 | tf_op jit(solution)/shard_map/all_to_all | solution.py:183
  23.3 12.2 %all-to-all-done = bf16[16,2,2568]{2,1,0:T(2,128)(2,1)S(1)} async-done(((bf16[16,2,2568]{2,1,0:T(2,128)(2,1)}), bf16[16,2,2568]{2,1,0:T(2,128)(2,1)S(1)}, u32[]{:S(2)}, u32[]{:S(2)}) %all-to-all-start) | async-done | bytes 164384 | tf_op jit(solution)/shard_map/all_to_all | solution.py:183
  36.2 1.1 broadcast_in_dim.93
  37.3 11.6 %all-to-all-start.1 = ((bf16[32,2,8,1026]{3,2,1,0:T(8,128)(2,1)}), bf16[32,2,8,1026]{3,2,1,0:T(8,128)(2,1)S(1)}, u32[]{:S(2)}, u32[]{:S(2)}) async-start(bf16[32,2,8,1026]{3,2,1,0:T(8,128)(2,1)} %bitcast.8), calls=%async_computation.1 | async-start | bytes 2359296 | tf_op jit(solution)/shard_map/all_to_all | solution.py:199
  49.5 17.0 %all-to-all-done.1 = bf16[32,2,8,1026]{3,2,1,0:T(8,128)(2,1)S(1)} async-done(((bf16[32,2,8,1026]{3,2,1,0:T(8,128)(2,1)}), bf16[32,2,8,1026]{3,2,1,0:T(8,128)(2,1)S(1)}, u32[]{:S(2)}, u32[]{:S(2)}) %all-to-all-start.1) | async-done | bytes 1050656 | tf_op jit(solution)/shard_map/all_to_all | solution.py:199
  70.4 1.4 %copy.121 = f32[4,1,34816]{2,1,0:T(1,128)} copy(f32[4,1,34816]{2,0,1:T(4,128)S(1)} %maximum_bitcast_fusion) | data formatting | bytes 1114112 | tf_op jit(solution)/shard_map/all_to_all | solution.py:135
  71.7 3.5 %all-to-all-start.2 = ((f32[4,1,34816]{2,1,0:T(1,128)}), f32[4,1,34816]{2,1,0:T(1,128)S(1)}, u32[]{:S(2)}, u32[]{:S(2)}) async-start(f32[4,1,34816]{2,1,0:T(1,128)} %copy.121), calls=%async_computation.2 | async-start | bytes 1114112 | tf_op jit(solution)/shard_map/all_to_all | solution.py:135
  76.8 0.8 copy-done.2
  77.8 5.3 %all-to-all-done.2 = f32[4,1,34816]{2,1,0:T(1,128)S(1)} async-done(((f32[4,1,34816]{2,1,0:T(1,128)}), f32[4,1,34816]{2,1,0:T(1,128)S(1)}, u32[]{:S(2)}, u32[]{:S(2)}) %all-to-all-start.2) | async-done | bytes 557088 | tf_op jit(solution)/shard_map/all_to_all | solution.py:135
  85.4 0.8 all_to_all.39
  86.2 4.1 %all-to-all-start.3 = ((f32[2,1,18432]{2,1,0:T(1,128)}), f32[2,1,18432]{2,1,0:T(1,128)S(1)}, u32[]{:S(2)}, u32[]{:S(2)}) async-start(f32[2,1,18432]{2,1,0:T(1,128)} %all_to_all.39), calls=%async_computation.3 | async-start | bytes 294912 | tf_op jit(solution)/shard_map/all_to_all | solution.py:135
  90.3 1.0 fusion.8
  91.3 4.6 %all_gather.3 = bf16[2,3,16,128]{3,2,1,0:T(8,128)(2,1)S(1)} all-gather(bf16[1,3,16,128]{3,2,1,0:T(8,128)(2,1)S(1)} %pad_maximum_fusion.5), channel_id=1, replica_groups=mesh['y'=4,'zh'=2,'x'=4,'c'=2,'zl'=8] {'c'}, dimensions={0}, use_global_device_ids=true | all-gather | bytes 36864 | tf_op jit(solution)/shard_map/all_gather | solution.py:271
  95.9 9.1 %all-to-all-done.3 = f32[2,1,18432]{2,1,0:T(1,128)S(1)} async-done(((f32[2,1,18432]{2,1,0:T(1,128)}), f32[2,1,18432]{2,1,0:T(1,128)S(1)}, u32[]{:S(2)}, u32[]{:S(2)}) %all-to-all-start.3) | async-done | bytes 147488 | tf_op jit(solution)/shard_map/all_to_all | solution.py:135
  106.0 0.7 all_to_all.42
  106.8 7.8 %all-to-all-start.4 = ((f32[8,1,4096]{2,1,0:T(1,128)}), f32[8,1,4096]{2,1,0:T(1,128)S(1)}, u32[]{:S(2)}, u32[]{:S(2)}) async-start(f32[8,1,4096]{2,1,0:T(1,128)} %all_to_all.42), calls=%async_computation.4 | async-start | bytes 262144 | tf_op jit(solution)/shard_map/all_to_all | solution.py:135
  115.2 4.7 %all-to-all-done.4 = f32[8,1,4096]{2,1,0:T(1,128)S(1)} async-done(((f32[8,1,4096]{2,1,0:T(1,128)}), f32[8,1,4096]{2,1,0:T(1,128)S(1)}, u32[]{:S(2)}, u32[]{:S(2)}) %all-to-all-start.4) | async-done | bytes 131104 | tf_op jit(solution)/shard_map/all_to_all | solution.py:135
  120.7 0.7 copy.132
  121.5 0.7 copy.131
  (106 shorter events, 14.4 us)
Async XLA Ops:
  0.6 67.0 %copy-start = (bf16[128,256]{1,0:T(8,128)(2,1)S(1)}, bf16[128,256]{1,0:T(8,128)(2,1)}, u32[]{:S(2)}) copy-start(bf16[128,256]{1,0:T(8,128)(2,1)} %param.13) | copy-start | bytes 196612
  7.5 28.0 %all-to-all-start = ((bf16[16,2,2568]{2,1,0:T(2,128)(2,1)}), bf16[16,2,2568]{2,1,0:T(2,128)(2,1)S(1)}, u32[]{:S(2)}, u32[]{:S(2)}) async-start(bf16[16,2,2568]{2,1,0:T(2,128)(2,1)} %reshape.343), calls=%async_computation | async-start | bytes 344064 | tf_op jit(solution)/shard_map/all_to_all | solution.py:183
  37.3 29.3 %all-to-all-start.1 = ((bf16[32,2,8,1026]{3,2,1,0:T(8,128)(2,1)}), bf16[32,2,8,1026]{3,2,1,0:T(8,128)(2,1)S(1)}, u32[]{:S(2)}, u32[]{:S(2)}) async-start(bf16[32,2,8,1026]{3,2,1,0:T(8,128)(2,1)} %bitcast.8), calls=%async_computation.1 | async-start | bytes 2359296 | tf_op jit(solution)/shard_map/all_to_all | solution.py:199
  67.5 9.3 %copy-start.1 = (bf16[512,512]{0,1:T(8,128)(2,1)}, bf16[512,512]{0,1:T(8,128)(2,1)S(1)}, u32[]{:S(2)}) copy-start(bf16[512,512]{0,1:T(8,128)(2,1)S(1)} %copy.129) | copy-start | bytes 1572868
  67.5 0.9 copy-start.3
  71.7 11.4 %all-to-all-start.2 = ((f32[4,1,34816]{2,1,0:T(1,128)}), f32[4,1,34816]{2,1,0:T(1,128)S(1)}, u32[]{:S(2)}, u32[]{:S(2)}) async-start(f32[4,1,34816]{2,1,0:T(1,128)} %copy.121), calls=%async_computation.2 | async-start | bytes 1114112 | tf_op jit(solution)/shard_map/all_to_all | solution.py:135
  76.8 0.8 copy-start.2
  86.2 18.8 %all-to-all-start.3 = ((f32[2,1,18432]{2,1,0:T(1,128)}), f32[2,1,18432]{2,1,0:T(1,128)S(1)}, u32[]{:S(2)}, u32[]{:S(2)}) async-start(f32[2,1,18432]{2,1,0:T(1,128)} %all_to_all.39), calls=%async_computation.3 | async-start | bytes 294912 | tf_op jit(solution)/shard_map/all_to_all | solution.py:135
  106.8 13.1 %all-to-all-start.4 = ((f32[8,1,4096]{2,1,0:T(1,128)}), f32[8,1,4096]{2,1,0:T(1,128)S(1)}, u32[]{:S(2)}, u32[]{:S(2)}) async-start(f32[8,1,4096]{2,1,0:T(1,128)} %all_to_all.42), calls=%async_computation.4 | async-start | bytes 262144 | tf_op jit(solution)/shard_map/all_to_all | solution.py:135
